TPU v7x, 32 devices: a whole 2x2x4 slice. The times are simulated.
32 devices in a mesh: groups: 2 (over x), state: 16 (over z, y, core).
Axes of the slice: x: 2, y: 2, z: 4, core: 2. Of those that a mesh axis runs over, the one named last changes fastest.
Arguments:
- forward_probs: float32 [256, 8, 8192], P('groups', None, 'state'), parts along dimension 0, may hold values from 0.1 to 10
- token_ids: int32 [256, 8], P('groups'), parts along dimension 0, may hold values from 0 to 16383
- transition: bfloat16 [8192, 8192], P('state'), may hold values from 0.1 to 10
- emission: bfloat16 [8192, 16384], P('state'), may hold values from 0.05 to 20
Outputs:
- backward_probs: float32 [256, 8, 8192], P('groups', None, 'state'), parts along dimension 0
- trans_counts: float32 [16384, 8192], P(('groups', 'state')), parts along dimension 0
There are 2 independent parts, one for each index of `groups`. A program takes and returns all parts, laid end to end along the dimension named above; an argument that names none is the same for every part. Nothing has to cross between parts.
All inputs are finite; a program needn't handle non-finite values.
Results may differ from a plain program's by a relative error of at most 0.00031.
Values may be sent and summed in bfloat16 or wider, within the bound.
No kernel may reach another device: no remote copies, remote signals or barrier semaphores. Data moves between devices by JAX's collectives and lax.ppermute only.
A program may use at most 192 MiB of HBM per device.

v0:
```python
import jax
import jax.numpy as jnp
from jax import lax
from jax.sharding import PartitionSpec as P


def on_device(forward_probs, token_ids, transition, emission):
    state_rows = transition.shape[0]
    states = transition.shape[1]
    seq_count = token_ids.shape[0]
    step_count = token_ids.shape[1]
    emitted = jnp.take(emission, token_ids.reshape(-1), axis=1).astype(jnp.float32)
    emitted = emitted.reshape(state_rows, seq_count, step_count)
    backward = jnp.ones((seq_count, state_rows), jnp.float32)
    weighted = (emitted[:, :, step_count - 1].T * backward).astype(jnp.bfloat16)
    backs = [backward]
    stored = []
    scales = []
    for t in range(step_count - 2, -1, -1):
        whole = lax.all_gather(weighted, "state", axis=1, tiled=True)
        scale_sum = lax.psum(jnp.sum(weighted.astype(jnp.float32), axis=1), "state")
        product = lax.dot_general(
            whole, transition, (((1,), (1,)), ((), ())), preferred_element_type=jnp.float32
        )
        backward = product / scale_sum[:, None]
        stored.append(whole)
        scales.append(scale_sum)
        backs.append(backward)
        if t > 0:
            weighted = (emitted[:, :, t].T * backward).astype(jnp.bfloat16)
    backs = backs[::-1]
    stored = stored[::-1]
    scales = scales[::-1]
    backward_probs = jnp.stack(backs, axis=1)
    partial_norms = jnp.sum(
        forward_probs[:, : step_count - 1, :] * backward_probs[:, : step_count - 1, :], axis=2
    )
    norm_sums = lax.psum(partial_norms, "state")
    shares = []
    for t in range(step_count - 1):
        shares.append(
            (forward_probs[:, t, :] / (scales[t] * norm_sums[:, t])[:, None]).astype(jnp.bfloat16)
        )
    share_mat = jnp.concatenate(shares, axis=0)
    vector_mat = jnp.concatenate(stored, axis=0)
    moments = lax.dot_general(
        share_mat, vector_mat, (((0,), (0,)), ((), ())), preferred_element_type=jnp.float32
    )
    factor = float(states) * float(states) / float(seq_count * (step_count - 1))
    trans_counts = transition.astype(jnp.float32) * moments * factor
    return (backward_probs, trans_counts)


def solution(mesh):
    placed = (P("groups", None, "state"), P("groups", None), P("state", None), P("state", None))
    return jax.shard_map(
        on_device,
        mesh=mesh,
        in_specs=placed,
        out_specs=(P("groups", None, "state"), P(("groups", "state"), None)),
        check_vma=False,
    )
```

profile of v0, /device:TPU:0, one launch (start us, length us, event | category | flops | bytes accessed | tf_op | source)
XLA Modules:
  0.0 467.3 jit_solution(17282354931980316428)
XLA Ops:
  7.2 0.7 compare_and_fusion
  7.9 0.8 copy.15
  8.7 0.1 reshape.62
  8.8 22.4 %copy.16 = bf16[512,16384]{0,1:T(8,128)(2,1)} copy(bf16[512,16384]{1,0:T(8,128)(2,1)} %param.7) | data formatting | bytes 33554432 | tf_op args[3]
  31.2 11.9 %gather_fusion = bf16[1024,512]{1,0:T(8,128)(2,1)S(1)} fusion(bf16[512,16384]{0,1:T(8,128)(2,1)} %copy.16, s32[1024]{0:T(1024)S(1)} %broadcast_clamp_fusion), kind=kCustom, calls=%fused_computation | custom fusion | bytes 2101248 | tf_op jit(solution)/shard_map/jit(_take)/gather | solution.py:12
  43.2 0.8 fusion.41
  44.0 0.9 copy-done.9
  44.9 0.7 slice_bitcast_fusion.6
  45.7 1.0 convert_reduce_fusion.6
  46.7 35.4 %psum.56 = f32[128]{0:T(128)S(1)} all-reduce(f32[128]{0:T(128)S(1)} %convert_reduce_fusion.6), channel_id=1, replica_groups=mesh['groups'=2,'state'=16] {'state'}, use_global_device_ids=true, to_apply=%region_1.2 | all-reduce | flops 128 | bytes 1024 | tf_op jit(solution)/shard_map/psum | solution.py:21
  82.1 7.6 %all-gather.8.cloned.1.call-done = bf16[128,8192]{1,0:T(8,128)(2,1)} async-done(((bf16[128,512]{1,0:T(8,128)(2,1)}), bf16[128,8192]{1,0:T(8,128)(2,1)}) %all-gather.8.cloned.1.call-update) | async-done | bytes 2097168 | tf_op jit(solution)/shard_map/all_gather | solution.py:20
  89.7 7.7 %convert_reduce_fusion.5 = (f32[128]{0:T(128)S(1)}, bf16[128,512]{1,0:T(8,128)(2,1)}, f32[128,512]{1,0:T(8,128)}) fusion(f32[512,128,8]{0,1,2:T(8,128)S(1)} %get-tuple-element.18, f32[128]{0:T(128)S(1)} %psum.56, bf16[128,8192]{1,0:T(8,128)(2,1)} %all-gather.8.cloned.1.call-done, bf16[512,8192]{1,0:T(8,128)(2,1)} %param.6), kind=kOutput, calls=%fused_computation.69 | convolution fusion | flops 1074069376 | bytes 11142144 | tf_op jit(solution)/shard_map/dot_general | solution.py:22
  97.4 0.0 all-gather.12.cloned.1.call-start
  97.4 32.3 %psum.57 = f32[128]{0:T(128)S(1)} all-reduce(f32[128]{0:T(128)S(1)} %get-tuple-element.16), channel_id=1, replica_groups=mesh['groups'=2,'state'=16] {'state'}, use_global_device_ids=true, to_apply=%region_3.4 | all-reduce | flops 128 | bytes 1024 | tf_op jit(solution)/shard_map/psum | solution.py:21
  129.7 8.1 %all-gather.10.cloned.1.call-done = bf16[128,8192]{1,0:T(8,128)(2,1)} async-done(((bf16[128,512]{1,0:T(8,128)(2,1)}), bf16[128,8192]{1,0:T(8,128)(2,1)}) %all-gather.10.cloned.1.call-update) | async-done | bytes 2097168 | tf_op jit(solution)/shard_map/all_gather | solution.py:20
  137.8 7.7 %convert_reduce_fusion.4 = (f32[128]{0:T(128)S(1)}, bf16[128,512]{1,0:T(8,128)(2,1)}, f32[128,512]{1,0:T(8,128)}) fusion(f32[512,128,8]{0,1,2:T(8,128)S(1)} %get-tuple-element.18, f32[128]{0:T(128)S(1)} %psum.57, bf16[128,8192]{1,0:T(8,128)(2,1)} %all-gather.10.cloned.1.call-done, bf16[512,8192]{1,0:T(8,128)(2,1)} %param.6), kind=kOutput, calls=%fused_computation.68 | convolution fusion | flops 1074069376 | bytes 11142144 | tf_op jit(solution)/shard_map/dot_general | solution.py:22
  145.6 0.0 all-gather.14.cloned.1.call-start
  145.6 31.7 %psum.58 = f32[128]{0:T(128)S(1)} all-reduce(f32[128]{0:T(128)S(1)} %get-tuple-element.14), channel_id=1, replica_groups=mesh['groups'=2,'state'=16] {'state'}, use_global_device_ids=true, to_apply=%region_5.6 | all-reduce | flops 128 | bytes 1024 | tf_op jit(solution)/shard_map/psum | solution.py:21
  177.3 8.5 %all-gather.12.cloned.1.call-done = bf16[128,8192]{1,0:T(8,128)(2,1)} async-done(((bf16[128,512]{1,0:T(8,128)(2,1)}), bf16[128,8192]{1,0:T(8,128)(2,1)}) %all-gather.12.cloned.1.call-update) | async-done | bytes 2097168 | tf_op jit(solution)/shard_map/all_gather | solution.py:20
  185.9 7.7 %convert_reduce_fusion.3 = (f32[128]{0:T(128)S(1)}, bf16[128,512]{1,0:T(8,128)(2,1)}, f32[128,512]{1,0:T(8,128)}) fusion(f32[512,128,8]{0,1,2:T(8,128)S(1)} %get-tuple-element.18, f32[128]{0:T(128)S(1)} %psum.58, bf16[128,8192]{1,0:T(8,128)(2,1)} %all-gather.12.cloned.1.call-done, bf16[512,8192]{1,0:T(8,128)(2,1)} %param.6), kind=kOutput, calls=%fused_computation.67 | convolution fusion | flops 1074069376 | bytes 11142144 | tf_op jit(solution)/shard_map/dot_general | solution.py:22
  193.6 32.3 %psum.59 = f32[128]{0:T(128)S(1)} all-reduce(f32[128]{0:T(128)S(1)} %get-tuple-element.12), channel_id=1, replica_groups=mesh['groups'=2,'state'=16] {'state'}, use_global_device_ids=true, to_apply=%region_7.8 | all-reduce | flops 128 | bytes 1024 | tf_op jit(solution)/shard_map/psum | solution.py:21
  226.0 8.0 %all-gather.14.cloned.1.call-done = bf16[128,8192]{1,0:T(8,128)(2,1)} async-done(((bf16[128,512]{1,0:T(8,128)(2,1)}), bf16[128,8192]{1,0:T(8,128)(2,1)}) %all-gather.14.cloned.1.call-update) | async-done | bytes 2097168 | tf_op jit(solution)/shard_map/all_gather | solution.py:20
  233.9 7.7 %convert_reduce_fusion.2 = (f32[128]{0:T(128)S(1)}, bf16[128,512]{1,0:T(8,128)(2,1)}, f32[128,512]{1,0:T(8,128)}) fusion(f32[512,128,8]{0,1,2:T(8,128)S(1)} %get-tuple-element.18, f32[128]{0:T(128)S(1)} %psum.59, bf16[128,8192]{1,0:T(8,128)(2,1)} %all-gather.14.cloned.1.call-done, bf16[512,8192]{1,0:T(8,128)(2,1)} %param.6), kind=kOutput, calls=%fused_computation.66 | convolution fusion | flops 1074069376 | bytes 11142144 | tf_op jit(solution)/shard_map/dot_general | solution.py:22
  241.7 32.2 %psum.60 = f32[128]{0:T(128)S(1)} all-reduce(f32[128]{0:T(128)S(1)} %get-tuple-element.10), channel_id=1, replica_groups=mesh['groups'=2,'state'=16] {'state'}, use_global_device_ids=true, to_apply=%region_9.10 | all-reduce | flops 128 | bytes 1024 | tf_op jit(solution)/shard_map/psum | solution.py:21
  273.9 8.1 %all-gather.16.cloned.1.call-done = bf16[128,8192]{1,0:T(8,128)(2,1)} async-done(((bf16[128,512]{1,0:T(8,128)(2,1)}), bf16[128,8192]{1,0:T(8,128)(2,1)}) %all-gather.16.cloned.1.call-update) | async-done | bytes 2097168 | tf_op jit(solution)/shard_map/all_gather | solution.py:20
  282.0 7.7 %convert_reduce_fusion.1 = (f32[128]{0:T(128)S(1)}, bf16[128,512]{1,0:T(8,128)(2,1)}, f32[128,512]{1,0:T(8,128)}) fusion(f32[512,128,8]{0,1,2:T(8,128)S(1)} %get-tuple-element.18, f32[128]{0:T(128)S(1)} %psum.60, bf16[128,8192]{1,0:T(8,128)(2,1)} %all-gather.16.cloned.1.call-done, bf16[512,8192]{1,0:T(8,128)(2,1)} %param.6), kind=kOutput, calls=%fused_computation.65 | convolution fusion | flops 1074069376 | bytes 11142144 | tf_op jit(solution)/shard_map/dot_general | solution.py:22
  289.8 32.1 %psum.61 = f32[128]{0:T(128)S(1)} all-reduce(f32[128]{0:T(128)S(1)} %get-tuple-element.8), channel_id=1, replica_groups=mesh['groups'=2,'state'=16] {'state'}, use_global_device_ids=true, to_apply=%region_11.12 | all-reduce | flops 128 | bytes 1024 | tf_op jit(solution)/shard_map/psum | solution.py:21
  321.9 8.1 %all-gather.18.cloned.1.call-done = bf16[128,8192]{1,0:T(8,128)(2,1)} async-done(((bf16[128,512]{1,0:T(8,128)(2,1)}), bf16[128,8192]{1,0:T(8,128)(2,1)}) %all-gather.18.cloned.1.call-update) | async-done | bytes 2097168 | tf_op jit(solution)/shard_map/all_gather | solution.py:20
  330.0 7.6 %convert_reduce_fusion = (f32[128]{0:T(128)S(1)}, bf16[128,512]{1,0:T(8,128)(2,1)}, f32[128,512]{1,0:T(8,128)}) fusion(f32[512,128,8]{0,1,2:T(8,128)} %copy-done.8, f32[128]{0:T(128)S(1)} %psum.61, bf16[128,8192]{1,0:T(8,128)(2,1)} %all-gather.18.cloned.1.call-done, bf16[512,8192]{1,0:T(8,128)(2,1)} %param.6), kind=kOutput, calls=%fused_computation.64 | convolution fusion | flops 1074069376 | bytes 11142144 | tf_op jit(solution)/shard_map/dot_general | solution.py:22
  337.7 1.9 fusion.42
  339.7 32.0 %psum.62 = f32[128]{0:T(128)S(1)} all-reduce(f32[128]{0:T(128)S(1)} %get-tuple-element.6), channel_id=1, replica_groups=mesh['groups'=2,'state'=16] {'state'}, use_global_device_ids=true, to_apply=%region_13.14 | all-reduce | flops 128 | bytes 1024 | tf_op jit(solution)/shard_map/psum | solution.py:21
  371.7 6.4 %all-gather.20.cloned.1.call-done = bf16[128,8192]{1,0:T(8,128)(2,1)} async-done(((bf16[128,512]{1,0:T(8,128)(2,1)}), bf16[128,8192]{1,0:T(8,128)(2,1)}) %all-gather.20.cloned.1.call-update) | async-done | bytes 2097168 | tf_op jit(solution)/shard_map/all_gather | solution.py:20
  378.1 7.7 %constant_dynamic-update-slice_fusion.1 = (f32[128,7,512]{2,0,1:T(8,128)S(1)}, f32[128,8,512]{2,0,1:T(8,128)}) fusion(f32[128]{0:T(128)S(1)} %psum.62, bf16[128,8192]{1,0:T(8,128)(2,1)} %all-gather.20.cloned.1.call-done, bf16[512,8192]{1,0:T(8,128)(2,1)} %param.6), kind=kOutput, calls=%fused_computation.81 | convolution fusion | flops 1073807360 | bytes 11010560 | tf_op jit(solution)/shard_map/dot_general | solution.py:22
  385.9 0.7 bitcast_dynamic-update-slice_fusion.10
  386.6 0.7 bitcast_dynamic-update-slice_fusion.8
  387.4 0.7 bitcast_dynamic-update-slice_fusion.6
  388.1 0.7 bitcast_dynamic-update-slice_fusion.4
  388.9 0.7 bitcast_dynamic-update-slice_fusion.2
  389.6 0.7 bitcast_dynamic-update-slice_fusion
  390.4 1.2 fusion
  391.5 31.5 %psum.63 = f32[128,7]{0,1:T(8,128)S(1)} all-reduce(f32[128,7]{0,1:T(8,128)S(1)} %fusion), channel_id=1, replica_groups=mesh['groups'=2,'state'=16] {'state'}, use_global_device_ids=true, to_apply=%region_15.16 | all-reduce | flops 896 | bytes 7168 | tf_op jit(solution)/shard_map/psum | solution.py:38
  423.1 0.7 broadcast_dynamic-update-slice_fusion
  423.8 4.2 copy.26
  428.0 0.1 fusion.28
  428.1 0.1 fusion.29
  428.2 0.1 fusion.30
  428.3 0.1 fusion.31
  428.4 0.1 fusion.32
  428.5 0.1 fusion.33
  428.6 0.1 fusion.34
  428.7 0.9 copy-done.6
  429.6 1.5 constant_dynamic-update-slice_fusion.8
  431.1 0.9 copy-done.5
  431.9 1.5 constant_dynamic-update-slice_fusion.7
  433.4 0.9 copy-done.4
  434.3 1.5 constant_dynamic-update-slice_fusion.6
  435.8 0.9 copy-done.3
  436.6 1.5 constant_dynamic-update-slice_fusion.5
  438.1 1.5 constant_dynamic-update-slice_fusion.4
  439.6 1.3 copy-done.1
  440.9 1.5 constant_dynamic-update-slice_fusion.3
  442.4 1.5 constant_dynamic-update-slice_fusion.2
  443.9 0.8 slice-done.1
  444.6 15.9 %multiply_multiply_fusion = f32[512,8192]{1,0:T(8,128)} fusion(bf16[512,8192]{1,0:T(8,128)(2,1)S(1)} %bitcast.172, bf16[896,512]{1,0:T(8,128)(2,1)S(1)} %fusion.34, bf16[896,8192]{1,0:T(8,128)(2,1)} %constant_dynamic-update-slice_fusion.2), kind=kOutput, calls=%fused_computation.1 | convolution fusion | flops 7528775680 | bytes 40763392 | tf_op jit(solution)/shard_map/dot_general | solution.py:46
  (49 shorter events, 0.4 us)
Async XLA Ops:
  7.2 82.5 %all-gather.8.cloned.1.call-start = ((), (), s32[]{:S(2)}) async-start(), calls=%async_computation | async-start | bytes 2228224 | tf_op jit(solution)/shard_map/all_gather | solution.py:20
  43.9 1.0 copy-start.9
  43.9 238.1 %copy-start.8 = (f32[512,128,8]{0,1,2:T(8,128)}, f32[512,128,8]{0,1,2:T(8,128)S(1)}, u32[]{:S(2)}) copy-start(f32[512,128,8]{0,1,2:T(8,128)S(1)} %get-tuple-element.18) | copy-start | bytes 6291460
  45.6 92.2 %all-gather.10.cloned.1.call-start = ((), (), s32[]{:S(2)}) async-start(), calls=%async_computation.1 | async-start | bytes 2228224 | tf_op jit(solution)/shard_map/all_gather | solution.py:20
  97.4 88.5 %all-gather.12.cloned.1.call-start = ((), (), s32[]{:S(2)}) async-start(), calls=%async_computation.2 | async-start | bytes 2228224 | tf_op jit(solution)/shard_map/all_gather | solution.py:20
  145.6 88.4 %all-gather.14.cloned.1.call-start = ((), (), s32[]{:S(2)}) async-start(), calls=%async_computation.3 | async-start | bytes 2228224 | tf_op jit(solution)/shard_map/all_gather | solution.py:20
  193.6 88.4 %all-gather.16.cloned.1.call-start = ((), (), s32[]{:S(2)}) async-start(), calls=%async_computation.4 | async-start | bytes 2228224 | tf_op jit(solution)/shard_map/all_gather | solution.py:20
  241.6 88.4 %all-gather.18.cloned.1.call-start = ((), (), s32[]{:S(2)}) async-start(), calls=%async_computation.5 | async-start | bytes 2228224 | tf_op jit(solution)/shard_map/all_gather | solution.py:20
  289.7 88.4 %all-gather.20.cloned.1.call-start = ((), (), s32[]{:S(2)}) async-start(), calls=%async_computation.6 | async-start | bytes 2228224 | tf_op jit(solution)/shard_map/all_gather | solution.py:20
  321.9 15.8 %copy-start.7 = (f32[128,8,512]{2,1,0:T(8,128)S(1)}, f32[128,8,512]{2,1,0:T(8,128)}, u32[]{:S(2)}) copy-start(f32[128,8,512]{2,1,0:T(8,128)} %param.4) | copy-start | bytes 6291460
  378.1 7.7 %copy-start.17 = (f32[128,512]{1,0:T(8,128)S(1)}, f32[128,512]{1,0:T(8,128)}, u32[]{:S(2)}) copy-start(f32[128,512]{1,0:T(8,128)} %get-tuple-element.53) | copy-start | bytes 786436
  378.1 8.5 %copy-start.16 = (f32[128,512]{1,0:T(8,128)S(1)}, f32[128,512]{1,0:T(8,128)}, u32[]{:S(2)}) copy-start(f32[128,512]{1,0:T(8,128)} %get-tuple-element.52) | copy-start | bytes 786436
  378.1 9.2 %copy-start.15 = (f32[128,512]{1,0:T(8,128)S(1)}, f32[128,512]{1,0:T(8,128)}, u32[]{:S(2)}) copy-start(f32[128,512]{1,0:T(8,128)} %get-tuple-element.51) | copy-start | bytes 786436
  385.9 2.3 copy-start.14
  385.9 3.0 copy-start.13
  385.9 3.7 copy-start.12
  423.8 4.2 copy-start.11
  423.8 4.3 copy-start.10
  428.0 1.6 copy-start.6
  429.6 2.3 copy-start.5
  431.9 2.3 copy-start.4
  434.3 2.3 copy-start.3
  434.3 3.8 copy-start.2
  436.6 7.3 %slice-start = ((s8[8388608]{0:T(1024)(128)(4,1)}), s8[4194304]{0:T(1024)(128)(4,1)S(1)}, s32[]{:S(2)}) async-start(s8[8388608]{0:T(1024)(128)(4,1)} %bitcast.171), calls=%async_computation.7 | async-start | bytes 8388608
  438.1 2.8 copy-start.1
  438.1 4.3 copy-start
  440.9 3.7 slice-start.1
Sparse Core Ops, SparseCore 0:
  45.7 43.8 all-gather.7
  97.5 40.2 all-gather.9
  145.7 40.1 all-gather.11
  193.7 40.1 all-gather.13
  241.8 40.1 all-gather.15
  289.8 40.1 all-gather.17
  337.8 40.2 all-gather.19
where the time goes:
time: 468 us; the launch traced here: 467 us
  blocking collectives  260 us (56%)
  matrix products  69.7 us (15%)
  local copies, waits for them, and re-layouts  64.2 us (14%)
  waiting for transfers between devices  55 us (12%)
  between operations  14.3 us (3%)
    psum x7, blocking collectives, on_device(): scale_sum = lax.psum(jnp.sum(weighted.astype(jnp.float32), axis=1), 'state')  228 us
    all_gather x7, waiting for transfers between devices, on_device(): whole = lax.all_gather(weighted, 'state', axis=1, tiled=True)  54.9 us
    dot_general x7, matrix products, on_device(): lax.dot_general(whole, transition, (((1,), (1,)), ((), ())), preferred_el...  53.8 us
    unnamed x54, local copies, waits for them, and re-layouts  46.6 us
    psum x1, blocking collectives, on_device(): norm_sums = lax.psum(partial_norms, 'state')  31.5 us
    dot_general x1, matrix products, on_device(): lax.dot_general(share_mat, vector_mat, (((0,), (0,)), ((), ())), preferre...  15.9 us
    gather x1, local copies, waits for them, and re-layouts, on_device(): jnp.take(emission, token_ids.reshape(-1), axis=1).astype(jnp.float32)  11.9 us
  transfers between devices with their start and end apart: 7, of which 7 were waited for; matrix products, arithmetic and copies ran while one was open for 1% of the time, Pallas kernels for 0%

commit v1 on v0

--- a/solution.py
+++ b/solution.py
@@ -2,6 +2,14 @@
 import jax.numpy as jnp
 from jax import lax
 from jax.sharding import PartitionSpec as P
+
+
+def emitted_rows(token_ids_flat, emission):
+    vocab = emission.shape[1]
+    onehot = (token_ids_flat[:, None] == lax.broadcasted_iota(jnp.int32, (1, vocab), 1)).astype(emission.dtype)
+    return lax.dot_general(
+        onehot, emission, (((1,), (1,)), ((), ())), preferred_element_type=jnp.float32
+    )
 
 
 def on_device(forward_probs, token_ids, transition, emission):
@@ -9,16 +17,18 @@
     states = transition.shape[1]
     seq_count = token_ids.shape[0]
     step_count = token_ids.shape[1]
-    emitted = jnp.take(emission, token_ids.reshape(-1), axis=1).astype(jnp.float32)
-    emitted = emitted.reshape(state_rows, seq_count, step_count)
+    last = step_count - 1
+    emitted_last = emitted_rows(token_ids[:, last], emission)
+    early_ids = token_ids[:, :last].T.reshape(-1)
+    emitted_early = emitted_rows(early_ids, emission).reshape(last, seq_count, state_rows)
     backward = jnp.ones((seq_count, state_rows), jnp.float32)
-    weighted = (emitted[:, :, step_count - 1].T * backward).astype(jnp.bfloat16)
+    weighted = (emitted_last * backward).astype(jnp.bfloat16)
     backs = [backward]
     stored = []
     scales = []
     for t in range(step_count - 2, -1, -1):
         whole = lax.all_gather(weighted, "state", axis=1, tiled=True)
-        scale_sum = lax.psum(jnp.sum(weighted.astype(jnp.float32), axis=1), "state")
+        scale_sum = jnp.sum(whole.astype(jnp.float32), axis=1)
         product = lax.dot_general(
             whole, transition, (((1,), (1,)), ((), ())), preferred_element_type=jnp.float32
         )
@@ -27,7 +37,7 @@
         scales.append(scale_sum)
         backs.append(backward)
         if t > 0:
-            weighted = (emitted[:, :, t].T * backward).astype(jnp.bfloat16)
+            weighted = (emitted_early[t] * backward).astype(jnp.bfloat16)
     backs = backs[::-1]
     stored = stored[::-1]
     scales = scales[::-1]
@@ -35,7 +45,8 @@
     partial_norms = jnp.sum(
         forward_probs[:, : step_count - 1, :] * backward_probs[:, : step_count - 1, :], axis=2
     )
-    norm_sums = lax.psum(partial_norms, "state")
+    norm_parts = lax.all_gather(partial_norms, "state", axis=0, tiled=False)
+    norm_sums = jnp.sum(norm_parts, axis=0)
     shares = []
     for t in range(step_count - 1):
         shares.append(

time: 468 us -> 435 us (0.929)
  blocking collectives: 260 us -> 19.8 us
  waiting for transfers between devices: 55 us -> 257 us
  local copies, waits for them, and re-layouts: 64.2 us -> 29.7 us
  matrix products: 69.7 us -> 96.7 us
  other arithmetic: 4.29 us -> 16.5 us
    psum x8 -> x0, blocking collectives: 260 us -> none  [the longest x7 228 us: on_device(): scale_sum = lax.psum(jnp.sum(weighted.astype(jnp.float32), axis=1), 'state')]
    all_gather x7, waiting for transfers between devices: 54.9 us -> 257 us  [on_device(): whole = lax.all_gather(weighted, 'state', axis=1, tiled=True)]
    dot_general x0 -> x2, matrix products: none -> 31.5 us  [emitted_rows(): lax.dot_general(onehot, emission, (((1,), (1,)), ((), ())), preferred_ele...]
    unnamed x54 -> x60, local copies, waits for them, and re-layouts: 46.6 us -> 18.7 us
    all_gather x0 -> x1, blocking collectives: none -> 19.8 us  [on_device(): norm_parts = lax.all_gather(partial_norms, 'state', axis=0, tiled=False)]
    reduce_sum x1 -> x8, other arithmetic: 1.01 us -> 14.7 us  [the longest x7 14.6 us: on_device(): scale_sum = jnp.sum(whole.astype(jnp.float32), axis=1)]
    gather x1 -> x0, local copies, waits for them, and re-layouts: 11.9 us -> none  [on_device(): jnp.take(emission, token_ids.reshape(-1), axis=1).astype(jnp.float32)]
    slice x1, local copies, waits for them, and re-layouts: 1.94 us -> 8.75 us  [on_device(): forward_probs[:, t, :] / (scales[t] * norm_sums[:, t])[:, None]]
  transfers between devices with their start and end apart: 7 -> 7, of which waited for: 7 -> 7; matrix products, arithmetic and copies ran while one was open for 1% -> 6% of each run, Pallas kernels for 0% -> 0%
where the time goes in v1:
time: 435 us
  waiting for transfers between devices  257 us (59%)
  matrix products  96.7 us (22%)
  local copies, waits for them, and re-layouts  29.7 us (7%)
  blocking collectives  19.8 us (5%)
  other arithmetic  16.5 us (4%)
  between operations  14.4 us (3%)
    all_gather x7, waiting for transfers between devices, on_device(): whole = lax.all_gather(weighted, 'state', axis=1, tiled=True)  257 us
    dot_general x7, matrix products, on_device(): lax.dot_general(whole, transition, (((1,), (1,)), ((), ())), preferred_el...  49.4 us
    dot_general x2, matrix products, emitted_rows(): lax.dot_general(onehot, emission, (((1,), (1,)), ((), ())), preferred_ele...  31.5 us
    all_gather x1, blocking collectives, on_device(): norm_parts = lax.all_gather(partial_norms, 'state', axis=0, tiled=False)  19.8 us
    unnamed x60, local copies, waits for them, and re-layouts  18.7 us
    dot_general x1, matrix products, on_device(): lax.dot_general(share_mat, vector_mat, (((0,), (0,)), ((), ())), preferre...  15.9 us
    reduce_sum x7, other arithmetic, on_device(): scale_sum = jnp.sum(whole.astype(jnp.float32), axis=1)  14.6 us
    slice x1, local copies, waits for them, and re-layouts, on_device(): forward_probs[:, t, :] / (scales[t] * norm_sums[:, t])[:, None]  8.75 us
  transfers between devices with their start and end apart: 7, of which 7 were waited for; matrix products, arithmetic and copies ran while one was open for 6% of the time, Pallas kernels for 0%

profile of v1, /device:TPU:0, one launch (start us, length us, event | category | flops | bytes accessed | tf_op | source)
XLA Modules:
  0.0 434.6 jit_solution(1525988632692193601)
XLA Ops:
  7.2 0.7 slice_bitcast_fusion.1
  7.9 12.0 %fusion.5 = bf16[128,512]{1,0:T(8,128)(2,1)} fusion(bf16[512,16384]{1,0:T(8,128)(2,1)} %param.7, s32[128]{0:T(128)S(1)} %slice_bitcast_fusion.1), kind=kOutput, calls=%fused_computation.16 | convolution fusion | flops 2149646336 | bytes 16908800 | tf_op jit(solution)/shard_map/dot_general | solution.py:10
  20.0 19.5 %fusion = f32[896,512]{1,0:T(8,128)} fusion(bf16[512,16384]{1,0:T(8,128)(2,1)} %param.7, s32[896]{0:T(1024)S(1)} %slice_bitcast_fusion), kind=kOutput, calls=%fused_computation.1 | convolution fusion | flops 15047065600 | bytes 18615808 | tf_op jit(solution)/shard_map/dot_general | solution.py:10
  39.5 24.5 %all-gather.9.cloned.1.call-done = bf16[128,8192]{1,0:T(8,128)(2,1)} async-done(((bf16[128,512]{1,0:T(8,128)(2,1)}), bf16[128,8192]{1,0:T(8,128)(2,1)}) %all-gather.9.cloned.1.call-update) | async-done | bytes 2097168 | tf_op jit(solution)/shard_map/all_gather | solution.py:30
  64.0 2.1 convert_reduce_fusion.6
  66.1 0.1 copy-done
  66.2 7.0 %fusion.7 = (bf16[128,512]{1,0:T(8,128)(2,1)}, f32[128,512]{1,0:T(8,128)}) fusion(f32[896,512]{1,0:T(8,128)} %fusion, f32[128]{0:T(128)S(1)} %convert_reduce_fusion.6, bf16[128,8192]{1,0:T(8,128)(2,1)S(1)} %copy-done, bf16[512,8192]{1,0:T(8,128)(2,1)} %param.6), kind=kOutput, calls=%fused_computation.26 | convolution fusion | flops 1073938432 | bytes 11141632 | tf_op jit(solution)/shard_map/dot_general | solution.py:32
  73.3 0.2 all-gather.13.cloned.1.call-start
  73.5 40.0 %all-gather.11.cloned.1.call-done = bf16[128,8192]{1,0:T(8,128)(2,1)} async-done(((bf16[128,512]{1,0:T(8,128)(2,1)}), bf16[128,8192]{1,0:T(8,128)(2,1)}) %all-gather.11.cloned.1.call-update) | async-done | bytes 2097168 | tf_op jit(solution)/shard_map/all_gather | solution.py:30
  113.6 2.1 convert_reduce_fusion.5
  115.7 0.1 copy-done.1
  115.8 7.2 %fusion.8 = (bf16[128,512]{1,0:T(8,128)(2,1)}, f32[128,512]{1,0:T(8,128)}) fusion(f32[896,512]{1,0:T(8,128)} %fusion, f32[128]{0:T(128)S(1)} %convert_reduce_fusion.5, bf16[128,8192]{1,0:T(8,128)(2,1)S(1)} %copy-done.1, bf16[512,8192]{1,0:T(8,128)(2,1)} %param.6), kind=kOutput, calls=%fused_computation.28 | convolution fusion | flops 1073938432 | bytes 11141632 | tf_op jit(solution)/shard_map/dot_general | solution.py:32
  123.0 0.0 all-gather.15.cloned.1.call-start
  123.0 40.2 %all-gather.13.cloned.1.call-done = bf16[128,8192]{1,0:T(8,128)(2,1)} async-done(((bf16[128,512]{1,0:T(8,128)(2,1)}), bf16[128,8192]{1,0:T(8,128)(2,1)}) %all-gather.13.cloned.1.call-update) | async-done | bytes 2097168 | tf_op jit(solution)/shard_map/all_gather | solution.py:30
  163.3 2.1 convert_reduce_fusion.4
  165.4 0.1 copy-done.3
  165.5 7.2 %fusion.9 = (bf16[128,512]{1,0:T(8,128)(2,1)}, f32[128,512]{1,0:T(8,128)}) fusion(f32[896,512]{1,0:T(8,128)} %fusion, f32[128]{0:T(128)S(1)} %convert_reduce_fusion.4, bf16[128,8192]{1,0:T(8,128)(2,1)S(1)} %copy-done.3, bf16[512,8192]{1,0:T(8,128)(2,1)} %param.6), kind=kOutput, calls=%fused_computation.30 | convolution fusion | flops 1073938432 | bytes 11141632 | tf_op jit(solution)/shard_map/dot_general | solution.py:32
  172.7 0.0 all-gather.17.cloned.1.call-start
  172.7 40.2 %all-gather.15.cloned.1.call-done = bf16[128,8192]{1,0:T(8,128)(2,1)} async-done(((bf16[128,512]{1,0:T(8,128)(2,1)}), bf16[128,8192]{1,0:T(8,128)(2,1)}) %all-gather.15.cloned.1.call-update) | async-done | bytes 2097168 | tf_op jit(solution)/shard_map/all_gather | solution.py:30
  213.0 2.1 convert_reduce_fusion.3
  215.0 0.1 copy-done.5
  215.2 7.2 %fusion.10 = (bf16[128,512]{1,0:T(8,128)(2,1)}, f32[128,512]{1,0:T(8,128)}) fusion(f32[896,512]{1,0:T(8,128)} %fusion, f32[128]{0:T(128)S(1)} %convert_reduce_fusion.3, bf16[128,8192]{1,0:T(8,128)(2,1)S(1)} %copy-done.5, bf16[512,8192]{1,0:T(8,128)(2,1)} %param.6), kind=kOutput, calls=%fused_computation.32 | convolution fusion | flops 1073938432 | bytes 11141632 | tf_op jit(solution)/shard_map/dot_general | solution.py:32
  222.4 40.2 %all-gather.17.cloned.1.call-done = bf16[128,8192]{1,0:T(8,128)(2,1)} async-done(((bf16[128,512]{1,0:T(8,128)(2,1)}), bf16[128,8192]{1,0:T(8,128)(2,1)}) %all-gather.17.cloned.1.call-update) | async-done | bytes 2097168 | tf_op jit(solution)/shard_map/all_gather | solution.py:30
  262.6 2.1 convert_reduce_fusion.2
  264.7 0.1 copy-done.7
  264.9 7.2 %fusion.11 = (bf16[128,512]{1,0:T(8,128)(2,1)}, f32[128,512]{1,0:T(8,128)}) fusion(f32[896,512]{1,0:T(8,128)} %fusion, f32[128]{0:T(128)S(1)} %convert_reduce_fusion.2, bf16[128,8192]{1,0:T(8,128)(2,1)S(1)} %copy-done.7, bf16[512,8192]{1,0:T(8,128)(2,1)} %param.6), kind=kOutput, calls=%fused_computation.34 | convolution fusion | flops 1073938432 | bytes 11141632 | tf_op jit(solution)/shard_map/dot_general | solution.py:32
  272.0 0.3 all-gather.21.cloned.1.call-start
  272.3 40.0 %all-gather.19.cloned.1.call-done = bf16[128,8192]{1,0:T(8,128)(2,1)} async-done(((bf16[128,512]{1,0:T(8,128)(2,1)}), bf16[128,8192]{1,0:T(8,128)(2,1)}) %all-gather.19.cloned.1.call-update) | async-done | bytes 2097168 | tf_op jit(solution)/shard_map/all_gather | solution.py:30
  312.3 2.1 convert_reduce_fusion.1
  314.4 0.1 copy-done.9
  314.5 7.2 %fusion.12 = (bf16[128,512]{1,0:T(8,128)(2,1)}, f32[128,512]{1,0:T(8,128)}) fusion(f32[896,512]{1,0:T(8,128)} %fusion, f32[128]{0:T(128)S(1)} %convert_reduce_fusion.1, bf16[128,8192]{1,0:T(8,128)(2,1)S(1)} %copy-done.9, bf16[512,8192]{1,0:T(8,128)(2,1)} %param.6), kind=kOutput, calls=%fused_computation.36 | convolution fusion | flops 1073938432 | bytes 11141632 | tf_op jit(solution)/shard_map/dot_general | solution.py:32
  321.7 8.8 %fusion.41 = (f32[128,1,512]{2,1,0:T(1,128)S(1)}, f32[128,1,512]{2,1,0:T(1,128)S(1)}, f32[128,1,512]{2,1,0:T(1,128)S(1)}, f32[128,1,512]{2,1,0:T(1,128)S(1)}, f3...) fusion(f32[128,8,512]{2,1,0:T(8,128)} %param.4), kind=kLoop, calls=%fused_computation.104 | loop fusion | bytes 3670016 | tf_op jit(solution)/shard_map/slice | solution.py:53
  330.5 31.5 %all-gather.21.cloned.1.call-done = bf16[128,8192]{1,0:T(8,128)(2,1)} async-done(((bf16[128,512]{1,0:T(8,128)(2,1)}), bf16[128,8192]{1,0:T(8,128)(2,1)}) %all-gather.21.cloned.1.call-update) | async-done | bytes 2097168 | tf_op jit(solution)/shard_map/all_gather | solution.py:30
  362.0 2.1 convert_reduce_fusion
  364.1 0.1 copy-done.11
  364.2 6.5 %constant_dynamic-update-slice_fusion.1 = (f32[128,7,512]{2,0,1:T(8,128)S(1)}, f32[128,8,512]{2,0,1:T(8,128)S(1)}) fusion(f32[128]{0:T(128)S(1)} %convert_reduce_fusion, bf16[128,8192]{1,0:T(8,128)(2,1)S(1)} %copy-done.11, bf16[512,8192]{1,0:T(8,128)(2,1)} %param.6), kind=kOutput, calls=%fused_computation.79 | convolution fusion | flops 1073807360 | bytes 11010560 | tf_op jit(solution)/shard_map/dot_general | solution.py:32
  370.8 0.1 bitcast_dynamic-update-slice_fusion.10
  370.9 0.1 bitcast_dynamic-update-slice_fusion.8
  370.9 0.1 bitcast_dynamic-update-slice_fusion.6
  371.0 0.7 copy-done.17
  371.9 0.7 copy-done.12
  372.6 1.2 fusion.4
  373.8 19.8 %all-gather = f32[2048,7]{0,1:T(8,128)S(1)} all-gather(f32[128,7]{0,1:T(8,128)S(1)} %fusion.4), channel_id=2, replica_groups=mesh['groups'=2,'state'=16] {'state'}, dimensions={0}, use_global_device_ids=true | all-gather | bytes 60928 | tf_op jit(solution)/shard_map/all_gather | solution.py:48
  393.6 2.5 copy.31
  396.2 0.1 fusion.27
  396.3 0.1 fusion.28
  396.4 0.1 fusion.29
  396.5 0.1 fusion.30
  396.6 0.1 fusion.31
  396.7 0.1 fusion.32
  396.8 0.1 fusion.33
  396.9 1.5 constant_dynamic-update-slice_fusion.8
  398.4 0.8 copy-done.10
  399.2 1.5 constant_dynamic-update-slice_fusion.7
  400.7 0.9 copy-done.8
  401.6 1.5 constant_dynamic-update-slice_fusion.6
  403.1 0.8 copy-done.6
  403.9 1.5 constant_dynamic-update-slice_fusion.5
  405.5 1.5 constant_dynamic-update-slice_fusion.4
  407.0 1.3 copy-done.2
  408.2 1.5 constant_dynamic-update-slice_fusion.3
  409.7 1.5 constant_dynamic-update-slice_fusion.2
  411.2 0.7 slice-done.1
  411.9 15.9 %multiply_multiply_fusion = f32[512,8192]{1,0:T(8,128)} fusion(bf16[512,8192]{1,0:T(8,128)(2,1)S(1)} %bitcast.149, bf16[896,512]{1,0:T(8,128)(2,1)S(1)} %fusion.33, bf16[896,8192]{1,0:T(8,128)(2,1)} %constant_dynamic-update-slice_fusion.2), kind=kOutput, calls=%fused_computation.3 | convolution fusion | flops 7528775680 | bytes 40763392 | tf_op jit(solution)/shard_map/dot_general | solution.py:57
  (52 shorter events, 0.5 us)
Async XLA Ops:
  7.2 56.8 %all-gather.9.cloned.1.call-start = ((), (), s32[]{:S(2)}) async-start(), calls=%async_computation | async-start | bytes 2228224 | tf_op jit(solution)/shard_map/all_gather | solution.py:30
  7.9 12.1 %copy-start.21 = (s32[128,8]{0,1:T(8,128)S(1)}, s32[128,8]{0,1:T(8,128)}, u32[]{:S(2)}) copy-start(s32[128,8]{0,1:T(8,128)} %param.5) | copy-start | bytes 12292
  20.0 93.6 %all-gather.11.cloned.1.call-start = ((), (), s32[]{:S(2)}) async-start(), calls=%async_computation.1 | async-start | bytes 2228224 | tf_op jit(solution)/shard_map/all_gather | solution.py:30
  64.0 2.2 copy-start
  73.3 90.0 %all-gather.13.cloned.1.call-start = ((), (), s32[]{:S(2)}) async-start(), calls=%async_computation.2 | async-start | bytes 2228224 | tf_op jit(solution)/shard_map/all_gather | solution.py:30
  113.6 2.2 copy-start.1
  123.0 90.0 %all-gather.15.cloned.1.call-start = ((), (), s32[]{:S(2)}) async-start(), calls=%async_computation.3 | async-start | bytes 2228224 | tf_op jit(solution)/shard_map/all_gather | solution.py:30
  163.3 2.2 copy-start.3
  172.7 90.0 %all-gather.17.cloned.1.call-start = ((), (), s32[]{:S(2)}) async-start(), calls=%async_computation.4 | async-start | bytes 2228224 | tf_op jit(solution)/shard_map/all_gather | solution.py:30
  213.0 2.2 copy-start.5
  222.4 90.0 %all-gather.19.cloned.1.call-start = ((), (), s32[]{:S(2)}) async-start(), calls=%async_computation.5 | async-start | bytes 2228224 | tf_op jit(solution)/shard_map/all_gather | solution.py:30
  262.6 2.2 copy-start.7
  272.0 90.0 %all-gather.21.cloned.1.call-start = ((), (), s32[]{:S(2)}) async-start(), calls=%async_computation.6 | async-start | bytes 2228224 | tf_op jit(solution)/shard_map/all_gather | solution.py:30
  312.3 2.2 copy-start.9
  362.0 2.2 copy-start.11
  364.2 6.5 %copy-start.20 = (f32[128,512]{1,0:T(8,128)S(1)}, f32[128,512]{1,0:T(8,128)}, u32[]{:S(2)}) copy-start(f32[128,512]{1,0:T(8,128)} %get-tuple-element.47) | copy-start | bytes 786436
  364.2 6.6 %copy-start.19 = (f32[128,512]{1,0:T(8,128)S(1)}, f32[128,512]{1,0:T(8,128)}, u32[]{:S(2)}) copy-start(f32[128,512]{1,0:T(8,128)} %get-tuple-element.45) | copy-start | bytes 786436
  364.2 6.7 %copy-start.18 = (f32[128,512]{1,0:T(8,128)S(1)}, f32[128,512]{1,0:T(8,128)}, u32[]{:S(2)}) copy-start(f32[128,512]{1,0:T(8,128)} %get-tuple-element.43) | copy-start | bytes 786436
  370.7 1.0 copy-start.17
  370.7 1.0 copy-start.16
  370.7 1.1 copy-start.15
  370.8 1.8 copy-start.12
  393.6 2.6 copy-start.14
  393.6 2.6 copy-start.13
  396.9 2.3 copy-start.10
  399.2 2.3 copy-start.8
  401.6 2.3 copy-start.6
  401.6 3.9 copy-start.4
  403.9 7.3 %slice-start = ((s8[8388608]{0:T(1024)(128)(4,1)}), s8[4194304]{0:T(1024)(128)(4,1)S(1)}, s32[]{:S(2)}) async-start(s8[8388608]{0:T(1024)(128)(4,1)} %bitcast.148), calls=%async_computation.7 | async-start | bytes 8388608
  405.4 2.8 copy-start.2
  408.2 3.7 slice-start.1
Sparse Core Ops, SparseCore 0:
  20.1 43.8 all-gather.8
  73.4 40.1 all-gather.10
  123.1 40.1 all-gather.12
  172.8 40.1 all-gather.14
  222.5 40.1 all-gather.16
  272.2 40.1 all-gather.18
  321.9 40.1 all-gather.20

commit v2 on v1

v2 whole, which is shorter than its diff:
```python
import functools

import jax
import jax.numpy as jnp
from jax import lax
from jax.experimental import pallas as pl
from jax.experimental.pallas import tpu as pltpu
from jax.sharding import PartitionSpec as P

NT = (((1,), (1,)), ((), ()))


def _emit_kernel(ids_ref, em_ref, out_ref):
    k = pl.program_id(0)
    tv = em_ref.shape[1]

    @pl.when(k == 0)
    def _():
        out_ref[...] = jnp.zeros_like(out_ref)

    cols = lax.broadcasted_iota(jnp.int32, (ids_ref.shape[0], tv), 1) + k * tv
    onehot = (ids_ref[...] == cols).astype(em_ref.dtype)
    out_ref[...] += lax.dot_general(onehot, em_ref[...], NT, preferred_element_type=jnp.float32)


def emitted_rows(ids, emission, tv=1024):
    n = ids.shape[0]
    rows, vocab = emission.shape
    return pl.pallas_call(
        _emit_kernel,
        grid=(vocab // tv,),
        in_specs=[
            pl.BlockSpec((n, 1), lambda k: (0, 0)),
            pl.BlockSpec((rows, tv), lambda k: (0, k)),
        ],
        out_specs=pl.BlockSpec((n, rows), lambda k: (0, 0)),
        out_shape=jax.ShapeDtypeStruct((n, rows), jnp.float32),
        cost_estimate=pl.CostEstimate(
            flops=2 * n * rows * vocab, bytes_accessed=rows * vocab * 2 + n * rows * 4, transcendentals=0
        ),
    )(ids.reshape(n, 1), emission)


def _step_kernel(whole_ref, trans_ref, emit_ref, fwd_ref, back_ref, wnext_ref, scale_ref, norm_ref, acc_ref, ssum_ref):
    k = pl.program_id(0)

    @pl.when(k == 0)
    def _():
        acc_ref[...] = jnp.zeros_like(acc_ref)
        ssum_ref[...] = jnp.zeros_like(ssum_ref)

    w = whole_ref[...]
    acc_ref[...] += lax.dot_general(w, trans_ref[...], NT, preferred_element_type=jnp.float32)
    ssum_ref[...] += jnp.sum(w.astype(jnp.float32), axis=1, keepdims=True)

    @pl.when(k == pl.num_programs(0) - 1)
    def _():
        s = ssum_ref[...]
        back = acc_ref[...] / s
        back_ref[...] = back
        wnext_ref[...] = (emit_ref[...] * back).astype(wnext_ref.dtype)
        scale_ref[...] = s
        norm_ref[...] = jnp.sum(fwd_ref[...] * back, axis=1, keepdims=True)


def backward_step(whole, transition, emit_next, fwd, tk=2048):
    b, states = whole.shape
    rows = transition.shape[0]
    full = lambda k: (0, 0)
    return pl.pallas_call(
        _step_kernel,
        grid=(states // tk,),
        in_specs=[
            pl.BlockSpec((b, tk), lambda k: (0, k)),
            pl.BlockSpec((rows, tk), lambda k: (0, k)),
            pl.BlockSpec((b, rows), full),
            pl.BlockSpec((b, rows), full),
        ],
        out_specs=[
            pl.BlockSpec((b, rows), full),
            pl.BlockSpec((b, rows), full),
            pl.BlockSpec((b, 1), full),
            pl.BlockSpec((b, 1), full),
        ],
        out_shape=[
            jax.ShapeDtypeStruct((b, rows), jnp.float32),
            jax.ShapeDtypeStruct((b, rows), jnp.bfloat16),
            jax.ShapeDtypeStruct((b, 1), jnp.float32),
            jax.ShapeDtypeStruct((b, 1), jnp.float32),
        ],
        scratch_shapes=[pltpu.VMEM((b, rows), jnp.float32), pltpu.VMEM((b, 1), jnp.float32)],
        cost_estimate=pl.CostEstimate(
            flops=2 * b * rows * states, bytes_accessed=rows * states * 2 + b * states * 2, transcendentals=0
        ),
    )(whole, transition, emit_next, fwd)


def _counts_kernel(factor, steps, share_ref, *refs):
    w_refs = refs[:steps]
    trans_ref = refs[steps]
    out_ref = refs[steps + 1]
    acc = jnp.dot(share_ref[0], w_refs[0][...], preferred_element_type=jnp.float32)
    for t in range(1, steps):
        acc += jnp.dot(share_ref[t], w_refs[t][...], preferred_element_type=jnp.float32)
    out_ref[...] = trans_ref[...].astype(jnp.float32) * acc * factor


def trans_counts_of(share_t, stored, transition, factor, tn=512):
    steps, rows, b = share_t.shape
    states = transition.shape[1]
    return pl.pallas_call(
        functools.partial(_counts_kernel, factor, steps),
        grid=(states // tn,),
        in_specs=[pl.BlockSpec((steps, rows, b), lambda j: (0, 0, 0))]
        + [pl.BlockSpec((b, tn), lambda j: (0, j)) for _ in range(steps)]
        + [pl.BlockSpec((rows, tn), lambda j: (0, j))],
        out_specs=pl.BlockSpec((rows, tn), lambda j: (0, j)),
        out_shape=jax.ShapeDtypeStruct((rows, states), jnp.float32),
        cost_estimate=pl.CostEstimate(
            flops=2 * steps * b * rows * states,
            bytes_accessed=steps * b * states * 2 + rows * states * 6,
            transcendentals=0,
        ),
    )(share_t, *stored, transition)


def on_device(forward_probs, token_ids, transition, emission):
    state_rows = transition.shape[0]
    states = transition.shape[1]
    seq_count = token_ids.shape[0]
    step_count = token_ids.shape[1]
    last = step_count - 1
    emitted_last = emitted_rows(token_ids[:, last], emission)
    early_ids = token_ids[:, :last].T.reshape(-1)
    emitted_early = emitted_rows(early_ids, emission).reshape(last, seq_count, state_rows)
    weighted = emitted_last.astype(jnp.bfloat16)
    backs = [jnp.ones((seq_count, state_rows), jnp.float32)]
    stored = []
    scales = []
    norms = []
    for t in range(step_count - 2, -1, -1):
        whole = lax.all_gather(weighted, "state", axis=1, tiled=True)
        backward, weighted, scale_sum, norm_part = backward_step(
            whole, transition, emitted_early[t], forward_probs[:, t, :]
        )
        stored.append(whole)
        scales.append(scale_sum)
        backs.append(backward)
        norms.append(norm_part)
    backs = backs[::-1]
    stored = stored[::-1]
    scales = jnp.concatenate(scales[::-1], axis=1)
    partial_norms = jnp.concatenate(norms[::-1], axis=1)
    backward_probs = jnp.stack(backs, axis=1)
    norm_parts = lax.all_gather(partial_norms, "state", axis=0, tiled=False)
    norm_sums = jnp.sum(norm_parts, axis=0)
    denom = scales * norm_sums
    share_t = (forward_probs[:, :last, :] / denom[:, :, None]).astype(jnp.bfloat16)
    share_t = jnp.transpose(share_t, (1, 2, 0))
    factor = float(states) * float(states) / float(seq_count * (step_count - 1))
    trans_counts = trans_counts_of(share_t, stored, transition, factor)
    return (backward_probs, trans_counts)


def solution(mesh):
    placed = (P("groups", None, "state"), P("groups", None), P("state", None), P("state", None))
    return jax.shard_map(
        on_device,
        mesh=mesh,
        in_specs=placed,
        out_specs=(P("groups", None, "state"), P(("groups", "state"), None)),
        check_vma=False,
    )
```

time: 435 us -> 424 us (0.975)
  Pallas kernels: 0 us -> 114 us
  matrix products: 96.7 us -> 0 us
  other arithmetic: 16.5 us -> 2.73 us
  local copies, waits for them, and re-layouts: 29.7 us -> 21.5 us
  waiting for transfers between devices: 257 us -> 249 us
    pallas_call x0 -> x10, Pallas kernels: none -> 114 us  [the longest x7 51.5 us: backward_step(): pl.pallas_call(_step_kernel, grid=(states // tk,), in_specs=[pl.BlockSpec...]
    dot_general x10 -> x0, matrix products: 96.7 us -> none  [the longest x7 49.4 us: on_device(): lax.dot_general(whole, transition, (((1,), (1,)), ((), ())), preferred_el...]
    reduce_sum x8 -> x0, other arithmetic: 15.8 us -> none  [the longest x7 14.6 us: on_device(): scale_sum = jnp.sum(whole.astype(jnp.float32), axis=1)]
    all_gather x7, waiting for transfers between devices: 257 us -> 249 us  [on_device(): whole = lax.all_gather(weighted, 'state', axis=1, tiled=True)]
    unnamed x60 -> x62, local copies, waits for them, and re-layouts: 18.7 us -> 13.3 us
    slice x1 -> x3, local copies, waits for them, and re-layouts: 8.75 us -> 5.28 us  [the longest x1 2.67 us: on_device(): emitted_early[t]]
  transfers between devices with their start and end apart: 7 -> 7, of which waited for: 7 -> 7; matrix products, arithmetic and copies ran while one was open for 6% -> 3% of each run, Pallas kernels for 0% -> 5%
where the time goes in v2:
time: 424 us; the launch traced here: 422 us
  waiting for transfers between devices  249 us (59%)
  Pallas kernels  114 us (27%)
  local copies, waits for them, and re-layouts  21.5 us (5%)
  blocking collectives  19.5 us (5%)
  between operations  14.4 us (3%)
    all_gather x7, waiting for transfers between devices, on_device(): whole = lax.all_gather(weighted, 'state', axis=1, tiled=True)  249 us
    pallas_call x7, Pallas kernels, backward_step(): pl.pallas_call(_step_kernel, grid=(states // tk,), in_specs=[pl.BlockSpec...  51.5 us
    pallas_call x2, Pallas kernels, emitted_rows(): pl.pallas_call(_emit_kernel, grid=(vocab // tv,), in_specs=[pl.BlockSpec(...  37.5 us
    pallas_call x1, Pallas kernels, trans_counts_of(): pl.pallas_call(functools.partial(_counts_kernel, factor, steps), grid=(st...  25.4 us
    all_gather x1, blocking collectives, on_device(): norm_parts = lax.all_gather(partial_norms, 'state', axis=0, tiled=False)  19.5 us
    unnamed x62, local copies, waits for them, and re-layouts  13.3 us
  transfers between devices with their start and end apart: 7, of which 7 were waited for; matrix products, arithmetic and copies ran while one was open for 3% of the time, Pallas kernels for 5%

profile of v2, /device:TPU:0, one launch (start us, length us, event | category | flops | bytes accessed | tf_op | source)
XLA Modules:
  0.0 422.0 jit_solution(18285408464975075150)
XLA Ops:
  7.2 0.0 all-gather.9.cloned.1.call-start
  7.2 0.7 slice.58
  7.9 0.7 copy.54.ids_ref
  8.6 15.7 %shard_map.59 = f32[128,512]{1,0:T(8,128)} custom-call(s32[128,1]{1,0:T(8,128)} %copy.54.ids_ref, bf16[512,16384]{1,0:T(8,128)(2,1)} %em_ref.3), custom_call_target="tpu_custom_call" | custom-call | flops 2147483648 | bytes 17039360 | tf_op jit(solution)/shard_map/pallas_call | solution.py:29
  24.4 1.6 convert_element_type.6
  26.0 0.0 all-gather.9.cloned.1.call-update
  26.0 0.0 all-gather.11.cloned.1.call-start
  26.1 1.0 copy.64
  27.1 1.9 fusion.1
  29.0 0.8 copy.81
  29.8 21.8 %shard_map.60 = f32[896,512]{1,0:T(8,128)} custom-call(s32[896,1]{1,0:T(8,128)} %bitcast.59, bf16[512,16384]{1,0:T(8,128)(2,1)} %em_ref.3), custom_call_target="tpu_custom_call" | custom-call | flops 15032385536 | bytes 18612224 | tf_op jit(solution)/shard_map/pallas_call | solution.py:29
  51.6 2.7 fusion.2
  54.3 15.8 %all-gather.9.cloned.1.call-done.whole_ref.refs_6_ = bf16[128,8192]{1,0:T(8,128)(2,1)} async-done(((bf16[128,512]{1,0:T(8,128)(2,1)}), bf16[128,8192]{1,0:T(8,128)(2,1)}) %all-gather.9.cloned.1.call-update) | async-done | bytes 2097168 | tf_op jit(solution)/shard_map/all_gather | solution.py:142
  70.1 7.3 %shard_map.61 = (f32[128,512]{1,0:T(8,128)}, bf16[128,512]{1,0:T(8,128)(2,1)}, f32[128,1]{1,0:T(8,128)}, f32[128,1]{1,0:T(8,128)}) custom-call(bf16[128,8192]{1,0:T(8,128)(2,1)} %all-gather.9.cloned.1.call-done.whole_ref.refs_6_, bf16[512,8192]{1,0:T(8,128)(2,1)} %refs_7_.1, f32[128,512]{1,0:T(8,128)} %get-tuple-element.75.emit_ref, f32[128,512]{1,0:T(8,128)} %bitcast.53), custom_call_target="tpu_custom_call" | custom-call | flops 1073741824 | bytes 10485760 | tf_op jit(solution)/shard_map/pallas_call | solution.py:70
  77.4 0.0 all-gather.11.cloned.1.call-update
  77.4 0.0 all-gather.13.cloned.1.call-start
  77.5 1.7 copy.80
  79.1 38.5 %all-gather.11.cloned.1.call-done.whole_ref.refs_5_ = bf16[128,8192]{1,0:T(8,128)(2,1)} async-done(((bf16[128,512]{1,0:T(8,128)(2,1)}), bf16[128,8192]{1,0:T(8,128)(2,1)}) %all-gather.11.cloned.1.call-update) | async-done | bytes 2097168 | tf_op jit(solution)/shard_map/all_gather | solution.py:142
  117.7 7.4 %shard_map.62 = (f32[128,512]{1,0:T(8,128)}, bf16[128,512]{1,0:T(8,128)(2,1)}, f32[128,1]{1,0:T(8,128)}, f32[128,1]{1,0:T(8,128)}) custom-call(bf16[128,8192]{1,0:T(8,128)(2,1)} %all-gather.11.cloned.1.call-done.whole_ref.refs_5_, bf16[512,8192]{1,0:T(8,128)(2,1)} %refs_7_.1, f32[128,512]{1,0:T(8,128)} %get-tuple-element.74.emit_ref, f32[128,512]{1,0:T(8,128)} %bitcast.54), custom_call_target="tpu_custom_call" | custom-call | flops 1073741824 | bytes 10485760 | tf_op jit(solution)/shard_map/pallas_call | solution.py:70
  125.1 0.0 all-gather.13.cloned.1.call-update
  125.1 0.0 all-gather.15.cloned.1.call-start
  125.1 0.7 copy.79
  125.9 39.5 %all-gather.13.cloned.1.call-done.whole_ref.refs_4_ = bf16[128,8192]{1,0:T(8,128)(2,1)} async-done(((bf16[128,512]{1,0:T(8,128)(2,1)}), bf16[128,8192]{1,0:T(8,128)(2,1)}) %all-gather.13.cloned.1.call-update) | async-done | bytes 2097168 | tf_op jit(solution)/shard_map/all_gather | solution.py:142
  165.4 7.3 %shard_map.63 = (f32[128,512]{1,0:T(8,128)}, bf16[128,512]{1,0:T(8,128)(2,1)}, f32[128,1]{1,0:T(8,128)}, f32[128,1]{1,0:T(8,128)}) custom-call(bf16[128,8192]{1,0:T(8,128)(2,1)} %all-gather.13.cloned.1.call-done.whole_ref.refs_4_, bf16[512,8192]{1,0:T(8,128)(2,1)} %refs_7_.1, f32[128,512]{1,0:T(8,128)} %get-tuple-element.73.emit_ref, f32[128,512]{1,0:T(8,128)} %bitcast.55), custom_call_target="tpu_custom_call" | custom-call | flops 1073741824 | bytes 10485760 | tf_op jit(solution)/shard_map/pallas_call | solution.py:70
  172.7 0.0 all-gather.15.cloned.1.call-update
  172.7 0.0 all-gather.17.cloned.1.call-start
  172.8 0.7 copy.78
  173.5 39.5 %all-gather.15.cloned.1.call-done.whole_ref.refs_3_ = bf16[128,8192]{1,0:T(8,128)(2,1)} async-done(((bf16[128,512]{1,0:T(8,128)(2,1)}), bf16[128,8192]{1,0:T(8,128)(2,1)}) %all-gather.15.cloned.1.call-update) | async-done | bytes 2097168 | tf_op jit(solution)/shard_map/all_gather | solution.py:142
  213.0 7.3 %shard_map.64 = (f32[128,512]{1,0:T(8,128)}, bf16[128,512]{1,0:T(8,128)(2,1)}, f32[128,1]{1,0:T(8,128)}, f32[128,1]{1,0:T(8,128)}) custom-call(bf16[128,8192]{1,0:T(8,128)(2,1)} %all-gather.15.cloned.1.call-done.whole_ref.refs_3_, bf16[512,8192]{1,0:T(8,128)(2,1)} %refs_7_.1, f32[128,512]{1,0:T(8,128)} %get-tuple-element.72.emit_ref, f32[128,512]{1,0:T(8,128)} %bitcast.56), custom_call_target="tpu_custom_call" | custom-call | flops 1073741824 | bytes 10485760 | tf_op jit(solution)/shard_map/pallas_call | solution.py:70
  220.4 0.0 all-gather.17.cloned.1.call-update
  220.4 0.0 all-gather.19.cloned.1.call-start
  220.4 0.7 copy.77
  221.2 39.5 %all-gather.17.cloned.1.call-done.whole_ref.refs_2_ = bf16[128,8192]{1,0:T(8,128)(2,1)} async-done(((bf16[128,512]{1,0:T(8,128)(2,1)}), bf16[128,8192]{1,0:T(8,128)(2,1)}) %all-gather.17.cloned.1.call-update) | async-done | bytes 2097168 | tf_op jit(solution)/shard_map/all_gather | solution.py:142
  260.7 7.3 %shard_map.65 = (f32[128,512]{1,0:T(8,128)}, bf16[128,512]{1,0:T(8,128)(2,1)}, f32[128,1]{1,0:T(8,128)}, f32[128,1]{1,0:T(8,128)}) custom-call(bf16[128,8192]{1,0:T(8,128)(2,1)} %all-gather.17.cloned.1.call-done.whole_ref.refs_2_, bf16[512,8192]{1,0:T(8,128)(2,1)} %refs_7_.1, f32[128,512]{1,0:T(8,128)} %get-tuple-element.71.emit_ref, f32[128,512]{1,0:T(8,128)} %bitcast.57), custom_call_target="tpu_custom_call" | custom-call | flops 1073741824 | bytes 10485760 | tf_op jit(solution)/shard_map/pallas_call | solution.py:70
  268.0 0.0 all-gather.19.cloned.1.call-update
  268.0 0.0 all-gather.21.cloned.1.call-start
  268.1 0.7 copy.76
  268.8 39.5 %all-gather.19.cloned.1.call-done.whole_ref.refs_1_ = bf16[128,8192]{1,0:T(8,128)(2,1)} async-done(((bf16[128,512]{1,0:T(8,128)(2,1)}), bf16[128,8192]{1,0:T(8,128)(2,1)}) %all-gather.19.cloned.1.call-update) | async-done | bytes 2097168 | tf_op jit(solution)/shard_map/all_gather | solution.py:142
  308.3 7.3 %shard_map.66 = (f32[128,512]{1,0:T(8,128)}, bf16[128,512]{1,0:T(8,128)(2,1)}, f32[128,1]{1,0:T(8,128)}, f32[128,1]{1,0:T(8,128)}) custom-call(bf16[128,8192]{1,0:T(8,128)(2,1)} %all-gather.19.cloned.1.call-done.whole_ref.refs_1_, bf16[512,8192]{1,0:T(8,128)(2,1)} %refs_7_.1, f32[128,512]{1,0:T(8,128)} %get-tuple-element.70.emit_ref, f32[128,512]{1,0:T(8,128)} %bitcast.58), custom_call_target="tpu_custom_call" | custom-call | flops 1073741824 | bytes 10485760 | tf_op jit(solution)/shard_map/pallas_call | solution.py:70
  315.6 0.0 all-gather.21.cloned.1.call-update
  315.8 1.7 copy.62
  317.5 0.7 copy.75
  318.3 0.1 copy.45
  318.3 0.1 copy.52
  318.4 0.1 copy.44
  318.5 0.1 copy.51
  318.6 0.1 copy.43
  318.7 0.1 copy.50
  318.7 0.1 copy.42
  318.8 0.0 copy-done.14
  318.8 0.1 copy.49
  318.9 0.1 copy.41
  319.0 0.1 copy.48
  319.1 0.1 copy.40
  319.2 0.1 copy.47
  319.3 36.7 %all-gather.21.cloned.1.call-done.whole_ref.refs_0_ = bf16[128,8192]{1,0:T(8,128)(2,1)} async-done(((bf16[128,512]{1,0:T(8,128)(2,1)}), bf16[128,8192]{1,0:T(8,128)(2,1)}) %all-gather.21.cloned.1.call-update) | async-done | bytes 2097168 | tf_op jit(solution)/shard_map/all_gather | solution.py:142
  356.0 7.4 %shard_map.67 = (f32[128,512]{1,0:T(8,128)}, bf16[128,512]{1,0:T(8,128)(2,1)}, f32[128,1]{1,0:T(8,128)}, f32[128,1]{1,0:T(8,128)}) custom-call(bf16[128,8192]{1,0:T(8,128)(2,1)} %all-gather.21.cloned.1.call-done.whole_ref.refs_0_, bf16[512,8192]{1,0:T(8,128)(2,1)} %refs_7_.1, f32[128,512]{1,0:T(8,128)} %get-tuple-element.69.emit_ref, f32[128,512]{1,0:T(8,128)} %bitcast.52), custom_call_target="tpu_custom_call" | custom-call | flops 1073741824 | bytes 10485760 | tf_op jit(solution)/shard_map/pallas_call | solution.py:70
  363.4 1.0 copy.39
  364.4 0.9 copy.46
  365.3 19.5 %all-gather = f32[2048,7]{0,1:T(8,128)S(1)} all-gather(f32[128,7]{0,1:T(8,128)S(1)} %concatenate.11), channel_id=2, replica_groups=mesh['groups'=2,'state'=16] {'state'}, dimensions={0}, use_global_device_ids=true | all-gather | bytes 60928 | tf_op jit(solution)/shard_map/all_gather | solution.py:155
  384.9 1.0 bitcast_dynamic-update-slice_fusion.6
  386.1 2.5 copy.53
  388.7 1.1 fusion.share_ref
  389.8 25.4 %shard_map.68 = f32[512,8192]{1,0:T(8,128)} custom-call(bf16[7,512,128]{2,1,0:T(8,128)(2,1)} %fusion.share_ref, bf16[128,8192]{1,0:T(8,128)(2,1)} %all-gather.21.cloned.1.call-done.whole_ref.refs_0_, bf16[128,8192]{1,0:T(8,128)(2,1)} %all-gather.19.cloned.1.call-done.whole_ref.refs_1_, bf16[128,8192]{1,0:T(8,128)(2,1)} %all-gather.17.cloned.1.call-done.whole_ref.refs_2_, ...), custom_call_target="tpu_custom_call" | custom-call | flops 7516192768 | bytes 39845888 | tf_op jit(solution)/shard_map/pallas_call | solution.py:111
  (54 shorter events, 0.3 us)
Async XLA Ops:
  7.2 62.9 %all-gather.9.cloned.1.call-start = ((), (), s32[]{:S(2)}) async-start(), calls=%async_computation | async-start | bytes 2228224 | tf_op jit(solution)/shard_map/all_gather | solution.py:142
  8.6 17.4 %copy-start.20 = (s32[128,8]{0,1:T(8,128)S(1)}, s32[128,8]{0,1:T(8,128)}, u32[]{:S(2)}) copy-start(s32[128,8]{0,1:T(8,128)} %param.5) | copy-start | bytes 12292
  8.6 18.4 %copy-start = (f32[128,8,512]{2,1,0:T(8,128)S(1)}, f32[128,8,512]{2,1,0:T(8,128)}, u32[]{:S(2)}) copy-start(f32[128,8,512]{2,1,0:T(8,128)} %param.4) | copy-start | bytes 6291460
  26.0 91.7 %all-gather.11.cloned.1.call-start = ((), (), s32[]{:S(2)}) async-start(), calls=%async_computation.1 | async-start | bytes 2228224 | tf_op jit(solution)/shard_map/all_gather | solution.py:142
  77.4 88.0 %all-gather.13.cloned.1.call-start = ((), (), s32[]{:S(2)}) async-start(), calls=%async_computation.2 | async-start | bytes 2228224 | tf_op jit(solution)/shard_map/all_gather | solution.py:142
  125.1 87.9 %all-gather.15.cloned.1.call-start = ((), (), s32[]{:S(2)}) async-start(), calls=%async_computation.3 | async-start | bytes 2228224 | tf_op jit(solution)/shard_map/all_gather | solution.py:142
  172.7 87.9 %all-gather.17.cloned.1.call-start = ((), (), s32[]{:S(2)}) async-start(), calls=%async_computation.4 | async-start | bytes 2228224 | tf_op jit(solution)/shard_map/all_gather | solution.py:142
  220.4 87.9 %all-gather.19.cloned.1.call-start = ((), (), s32[]{:S(2)}) async-start(), calls=%async_computation.5 | async-start | bytes 2228224 | tf_op jit(solution)/shard_map/all_gather | solution.py:142
  268.0 87.9 %all-gather.21.cloned.1.call-start = ((), (), s32[]{:S(2)}) async-start(), calls=%async_computation.6 | async-start | bytes 2228224 | tf_op jit(solution)/shard_map/all_gather | solution.py:142
  315.7 2.6 copy-start.9
  315.7 2.6 copy-start.8
  315.7 2.7 copy-start.11
  315.7 2.8 copy-start.10
  315.7 2.9 copy-start.13
  315.7 3.0 copy-start.12
  315.7 3.0 copy-start.15
  315.7 3.1 copy-start.14
  315.8 3.2 copy-start.17
  315.8 3.2 copy-start.16
  315.8 3.3 copy-start.19
  315.8 3.4 copy-start.18
  355.9 29.9 %copy-start.7 = (f32[128,512]{1,0:T(8,128)S(1)}, f32[128,512]{1,0:T(8,128)}, u32[]{:S(2)}) copy-start(f32[128,512]{1,0:T(8,128)} %get-tuple-element.36) | copy-start | bytes 786436
  356.0 29.9 %copy-start.6 = (f32[128,512]{1,0:T(8,128)S(1)}, f32[128,512]{1,0:T(8,128)}, u32[]{:S(2)}) copy-start(f32[128,512]{1,0:T(8,128)} %get-tuple-element.37) | copy-start | bytes 786436
  356.0 30.0 %copy-start.5 = (f32[128,512]{1,0:T(8,128)S(1)}, f32[128,512]{1,0:T(8,128)}, u32[]{:S(2)}) copy-start(f32[128,512]{1,0:T(8,128)} %get-tuple-element.38) | copy-start | bytes 786436
  363.4 22.6 %copy-start.4 = (f32[128,512]{1,0:T(8,128)S(1)}, f32[128,512]{1,0:T(8,128)}, u32[]{:S(2)}) copy-start(f32[128,512]{1,0:T(8,128)} %get-tuple-element.39) | copy-start | bytes 786436
  363.4 22.6 %copy-start.3 = (f32[128,512]{1,0:T(8,128)S(1)}, f32[128,512]{1,0:T(8,128)}, u32[]{:S(2)}) copy-start(f32[128,512]{1,0:T(8,128)} %get-tuple-element.40) | copy-start | bytes 786436
  363.4 22.6 %copy-start.2 = (f32[128,512]{1,0:T(8,128)S(1)}, f32[128,512]{1,0:T(8,128)}, u32[]{:S(2)}) copy-start(f32[128,512]{1,0:T(8,128)} %get-tuple-element.41) | copy-start | bytes 786436
  386.1 2.6 copy-start.1
Sparse Core Ops, SparseCore 0:
  26.1 43.8 all-gather.8
  77.5 40.1 all-gather.10
  125.2 40.1 all-gather.12
  172.9 40.1 all-gather.14
  220.5 40.1 all-gather.16
  268.1 40.1 all-gather.18
  315.8 40.1 all-gather.20

commit v3 on v2

--- a/solution.py
+++ b/solution.py
@@ -10,20 +10,24 @@
 NT = (((1,), (1,)), ((), ()))
 
 
-def _emit_kernel(ids_ref, em_ref, out_ref):
+def _emit_kernel(ids_ref, em_ref, out_ref, acc_ref):
     k = pl.program_id(0)
     tv = em_ref.shape[1]
 
     @pl.when(k == 0)
     def _():
-        out_ref[...] = jnp.zeros_like(out_ref)
+        acc_ref[...] = jnp.zeros_like(acc_ref)
 
     cols = lax.broadcasted_iota(jnp.int32, (ids_ref.shape[0], tv), 1) + k * tv
     onehot = (ids_ref[...] == cols).astype(em_ref.dtype)
-    out_ref[...] += lax.dot_general(onehot, em_ref[...], NT, preferred_element_type=jnp.float32)
+    acc_ref[...] += lax.dot_general(em_ref[...], onehot, NT, preferred_element_type=jnp.float32)
+
+    @pl.when(k == pl.num_programs(0) - 1)
+    def _():
+        out_ref[...] = acc_ref[...].T.astype(out_ref.dtype)
 
 
-def emitted_rows(ids, emission, tv=1024):
+def emitted_rows(ids, emission, dtype=jnp.float32, tv=1024):
     n = ids.shape[0]
     rows, vocab = emission.shape
     return pl.pallas_call(
@@ -34,7 +38,8 @@
             pl.BlockSpec((rows, tv), lambda k: (0, k)),
         ],
         out_specs=pl.BlockSpec((n, rows), lambda k: (0, 0)),
-        out_shape=jax.ShapeDtypeStruct((n, rows), jnp.float32),
+        out_shape=jax.ShapeDtypeStruct((n, rows), dtype),
+        scratch_shapes=[pltpu.VMEM((rows, n), jnp.float32)],
         cost_estimate=pl.CostEstimate(
             flops=2 * n * rows * vocab, bytes_accessed=rows * vocab * 2 + n * rows * 4, transcendentals=0
         ),
@@ -50,20 +55,20 @@
         ssum_ref[...] = jnp.zeros_like(ssum_ref)
 
     w = whole_ref[...]
-    acc_ref[...] += lax.dot_general(w, trans_ref[...], NT, preferred_element_type=jnp.float32)
+    acc_ref[...] += lax.dot_general(trans_ref[...], w, NT, preferred_element_type=jnp.float32)
     ssum_ref[...] += jnp.sum(w.astype(jnp.float32), axis=1, keepdims=True)
 
     @pl.when(k == pl.num_programs(0) - 1)
     def _():
         s = ssum_ref[...]
-        back = acc_ref[...] / s
+        back = acc_ref[...].T / s
         back_ref[...] = back
         wnext_ref[...] = (emit_ref[...] * back).astype(wnext_ref.dtype)
         scale_ref[...] = s
         norm_ref[...] = jnp.sum(fwd_ref[...] * back, axis=1, keepdims=True)
 
 
-def backward_step(whole, transition, emit_next, fwd, tk=2048):
+def backward_step(whole, transition, emit_next, fwd, tk=1024):
     b, states = whole.shape
     rows = transition.shape[0]
     full = lambda k: (0, 0)
@@ -88,7 +93,7 @@
             jax.ShapeDtypeStruct((b, 1), jnp.float32),
             jax.ShapeDtypeStruct((b, 1), jnp.float32),
         ],
-        scratch_shapes=[pltpu.VMEM((b, rows), jnp.float32), pltpu.VMEM((b, 1), jnp.float32)],
+        scratch_shapes=[pltpu.VMEM((rows, b), jnp.float32), pltpu.VMEM((b, 1), jnp.float32)],
         cost_estimate=pl.CostEstimate(
             flops=2 * b * rows * states, bytes_accessed=rows * states * 2 + b * states * 2, transcendentals=0
         ),
@@ -99,29 +104,34 @@
     w_refs = refs[:steps]
     trans_ref = refs[steps]
     out_ref = refs[steps + 1]
-    acc = jnp.dot(share_ref[0], w_refs[0][...], preferred_element_type=jnp.float32)
-    for t in range(1, steps):
-        acc += jnp.dot(share_ref[t], w_refs[t][...], preferred_element_type=jnp.float32)
+    cat_ref = refs[steps + 2]
+    b = w_refs[0].shape[0]
+    for t in range(steps):
+        cat_ref[t * b:(t + 1) * b, :] = w_refs[t][...]
+    acc = jnp.dot(share_ref[...], cat_ref[...], preferred_element_type=jnp.float32)
     out_ref[...] = trans_ref[...].astype(jnp.float32) * acc * factor
 
 
-def trans_counts_of(share_t, stored, transition, factor, tn=512):
-    steps, rows, b = share_t.shape
+def trans_counts_of(share_cat, stored, transition, factor, tn=512):
+    rows, depth = share_cat.shape
+    steps = len(stored)
+    b = stored[0].shape[0]
     states = transition.shape[1]
     return pl.pallas_call(
         functools.partial(_counts_kernel, factor, steps),
         grid=(states // tn,),
-        in_specs=[pl.BlockSpec((steps, rows, b), lambda j: (0, 0, 0))]
+        in_specs=[pl.BlockSpec((rows, depth), lambda j: (0, 0))]
         + [pl.BlockSpec((b, tn), lambda j: (0, j)) for _ in range(steps)]
         + [pl.BlockSpec((rows, tn), lambda j: (0, j))],
         out_specs=pl.BlockSpec((rows, tn), lambda j: (0, j)),
         out_shape=jax.ShapeDtypeStruct((rows, states), jnp.float32),
+        scratch_shapes=[pltpu.VMEM((depth, tn), stored[0].dtype)],
         cost_estimate=pl.CostEstimate(
-            flops=2 * steps * b * rows * states,
-            bytes_accessed=steps * b * states * 2 + rows * states * 6,
+            flops=2 * depth * rows * states,
+            bytes_accessed=depth * states * 2 + rows * states * 6,
             transcendentals=0,
         ),
-    )(share_t, *stored, transition)
+    )(share_cat, *stored, transition)
 
 
 def on_device(forward_probs, token_ids, transition, emission):
@@ -130,10 +140,10 @@
     seq_count = token_ids.shape[0]
     step_count = token_ids.shape[1]
     last = step_count - 1
-    emitted_last = emitted_rows(token_ids[:, last], emission)
+    emitted_last = emitted_rows(token_ids[:, last], emission, jnp.bfloat16)
     early_ids = token_ids[:, :last].T.reshape(-1)
     emitted_early = emitted_rows(early_ids, emission).reshape(last, seq_count, state_rows)
-    weighted = emitted_last.astype(jnp.bfloat16)
+    weighted = emitted_last
     backs = [jnp.ones((seq_count, state_rows), jnp.float32)]
     stored = []
     scales = []
@@ -156,9 +166,9 @@
     norm_sums = jnp.sum(norm_parts, axis=0)
     denom = scales * norm_sums
     share_t = (forward_probs[:, :last, :] / denom[:, :, None]).astype(jnp.bfloat16)
-    share_t = jnp.transpose(share_t, (1, 2, 0))
+    share_cat = jnp.transpose(share_t, (2, 1, 0)).reshape(state_rows, last * seq_count)
     factor = float(states) * float(states) / float(seq_count * (step_count - 1))
-    trans_counts = trans_counts_of(share_t, stored, transition, factor)
+    trans_counts = trans_counts_of(share_cat, stored, transition, factor)
     return (backward_probs, trans_counts)
 
 

time: 424 us -> 439 us (1.035)
  Pallas kernels: 114 us -> 129 us
  local copies, waits for them, and re-layouts: 21.5 us -> 26.3 us
    pallas_call x7, Pallas kernels: 51.5 us -> 63.5 us  [backward_step(): pl.pallas_call(_step_kernel, grid=(states // tk,), in_specs=[pl.BlockSpec...]
    unnamed x62 -> x47, local copies, waits for them, and re-layouts: 13.3 us -> 15.2 us
  transfers between devices with their start and end apart: 7 -> 7, of which waited for: 7 -> 7; matrix products, arithmetic and copies ran while one was open for 3% -> 3% of each run, Pallas kernels for 5% -> 6%
where the time goes in v3:
time: 439 us; the launch traced here: 437 us
  waiting for transfers between devices  246 us (56%)
  Pallas kernels  129 us (29%)
  local copies, waits for them, and re-layouts  26.3 us (6%)
  blocking collectives  19.7 us (4%)
  between operations  14.3 us (3%)
    all_gather x7, waiting for transfers between devices, on_device(): whole = lax.all_gather(weighted, 'state', axis=1, tiled=True)  246 us
    pallas_call x7, Pallas kernels, backward_step(): pl.pallas_call(_step_kernel, grid=(states // tk,), in_specs=[pl.BlockSpec...  63.5 us
    pallas_call x2, Pallas kernels, emitted_rows(): pl.pallas_call(_emit_kernel, grid=(vocab // tv,), in_specs=[pl.BlockSpec(...  41.3 us
    pallas_call x1, Pallas kernels, trans_counts_of(): pl.pallas_call(functools.partial(_counts_kernel, factor, steps), grid=(st...  24.6 us
    all_gather x1, blocking collectives, on_device(): norm_parts = lax.all_gather(partial_norms, 'state', axis=0, tiled=False)  19.7 us
    unnamed x47, local copies, waits for them, and re-layouts  15.2 us
  transfers between devices with their start and end apart: 7, of which 7 were waited for; matrix products, arithmetic and copies ran while one was open for 3% of the time, Pallas kernels for 6%

profile of v3, /device:TPU:0, one launch (start us, length us, event | category | flops | bytes accessed | tf_op | source)
XLA Modules:
  0.0 437.0 jit_solution(13416228718458360262)
XLA Ops:
  7.2 0.0 all-gather.9.cloned.1.call-start
  7.2 0.7 slice.58
  7.9 0.7 copy.55.ids_ref
  8.6 16.0 %shard_map.59 = bf16[128,512]{1,0:T(8,128)(2,1)} custom-call(s32[128,1]{1,0:T(8,128)} %copy.55.ids_ref, bf16[512,16384]{1,0:T(8,128)(2,1)} %em_ref.3), custom_call_target="tpu_custom_call" | custom-call | flops 2147483648 | bytes 17039360 | tf_op jit(solution)/shard_map/pallas_call | solution.py:33
  24.7 0.0 all-gather.11.cloned.1.call-start
  24.7 1.0 copy.65
  25.7 1.9 fusion.1
  27.6 0.7 copy.85
  28.3 25.3 %shard_map.60 = f32[896,512]{1,0:T(8,128)} custom-call(s32[896,1]{1,0:T(8,128)} %bitcast.61, bf16[512,16384]{1,0:T(8,128)(2,1)} %em_ref.3), custom_call_target="tpu_custom_call" | custom-call | flops 15032385536 | bytes 18612224 | tf_op jit(solution)/shard_map/pallas_call | solution.py:33
  53.6 2.7 fusion.2
  56.3 12.4 %all-gather.9.cloned.1.call-done.whole_ref.refs_6_ = bf16[128,8192]{1,0:T(8,128)(2,1)} async-done(((bf16[128,512]{1,0:T(8,128)(2,1)}), bf16[128,8192]{1,0:T(8,128)(2,1)}) %all-gather.9.cloned.1.call-update) | async-done | bytes 2097168 | tf_op jit(solution)/shard_map/all_gather | solution.py:152
  68.7 9.0 %shard_map.61 = (f32[128,512]{1,0:T(8,128)}, bf16[128,512]{1,0:T(8,128)(2,1)}, f32[128,1]{1,0:T(8,128)}, f32[128,1]{1,0:T(8,128)}) custom-call(bf16[128,8192]{1,0:T(8,128)(2,1)} %all-gather.9.cloned.1.call-done.whole_ref.refs_6_, bf16[512,8192]{1,0:T(8,128)(2,1)} %refs_7_.1, f32[128,512]{1,0:T(8,128)} %get-tuple-element.75.emit_ref, f32[128,512]{1,0:T(8,128)} %bitcast.55), custom_call_target="tpu_custom_call" | custom-call | flops 1073741824 | bytes 10485760 | tf_op jit(solution)/shard_map/pallas_call | solution.py:75
  77.7 0.0 all-gather.11.cloned.1.call-update
  77.8 0.0 all-gather.13.cloned.1.call-start
  77.8 1.7 copy.84
  79.5 38.6 %all-gather.11.cloned.1.call-done.whole_ref.refs_5_ = bf16[128,8192]{1,0:T(8,128)(2,1)} async-done(((bf16[128,512]{1,0:T(8,128)(2,1)}), bf16[128,8192]{1,0:T(8,128)(2,1)}) %all-gather.11.cloned.1.call-update) | async-done | bytes 2097168 | tf_op jit(solution)/shard_map/all_gather | solution.py:152
  118.0 9.0 %shard_map.62 = (f32[128,512]{1,0:T(8,128)}, bf16[128,512]{1,0:T(8,128)(2,1)}, f32[128,1]{1,0:T(8,128)}, f32[128,1]{1,0:T(8,128)}) custom-call(bf16[128,8192]{1,0:T(8,128)(2,1)} %all-gather.11.cloned.1.call-done.whole_ref.refs_5_, bf16[512,8192]{1,0:T(8,128)(2,1)} %refs_7_.1, f32[128,512]{1,0:T(8,128)} %get-tuple-element.74.emit_ref, f32[128,512]{1,0:T(8,128)} %bitcast.56), custom_call_target="tpu_custom_call" | custom-call | flops 1073741824 | bytes 10485760 | tf_op jit(solution)/shard_map/pallas_call | solution.py:75
  127.1 0.0 all-gather.13.cloned.1.call-update
  127.1 0.0 all-gather.15.cloned.1.call-start
  127.2 0.7 copy.83
  127.9 39.5 %all-gather.13.cloned.1.call-done.whole_ref.refs_4_ = bf16[128,8192]{1,0:T(8,128)(2,1)} async-done(((bf16[128,512]{1,0:T(8,128)(2,1)}), bf16[128,8192]{1,0:T(8,128)(2,1)}) %all-gather.13.cloned.1.call-update) | async-done | bytes 2097168 | tf_op jit(solution)/shard_map/all_gather | solution.py:152
  167.4 9.1 %shard_map.63 = (f32[128,512]{1,0:T(8,128)}, bf16[128,512]{1,0:T(8,128)(2,1)}, f32[128,1]{1,0:T(8,128)}, f32[128,1]{1,0:T(8,128)}) custom-call(bf16[128,8192]{1,0:T(8,128)(2,1)} %all-gather.13.cloned.1.call-done.whole_ref.refs_4_, bf16[512,8192]{1,0:T(8,128)(2,1)} %refs_7_.1, f32[128,512]{1,0:T(8,128)} %get-tuple-element.73.emit_ref, f32[128,512]{1,0:T(8,128)} %bitcast.57), custom_call_target="tpu_custom_call" | custom-call | flops 1073741824 | bytes 10485760 | tf_op jit(solution)/shard_map/pallas_call | solution.py:75
  176.4 0.0 all-gather.15.cloned.1.call-update
  176.5 0.0 all-gather.17.cloned.1.call-start
  176.5 0.7 copy.82
  177.2 39.5 %all-gather.15.cloned.1.call-done.whole_ref.refs_3_ = bf16[128,8192]{1,0:T(8,128)(2,1)} async-done(((bf16[128,512]{1,0:T(8,128)(2,1)}), bf16[128,8192]{1,0:T(8,128)(2,1)}) %all-gather.15.cloned.1.call-update) | async-done | bytes 2097168 | tf_op jit(solution)/shard_map/all_gather | solution.py:152
  216.7 9.1 %shard_map.64 = (f32[128,512]{1,0:T(8,128)}, bf16[128,512]{1,0:T(8,128)(2,1)}, f32[128,1]{1,0:T(8,128)}, f32[128,1]{1,0:T(8,128)}) custom-call(bf16[128,8192]{1,0:T(8,128)(2,1)} %all-gather.15.cloned.1.call-done.whole_ref.refs_3_, bf16[512,8192]{1,0:T(8,128)(2,1)} %refs_7_.1, f32[128,512]{1,0:T(8,128)} %get-tuple-element.72.emit_ref, f32[128,512]{1,0:T(8,128)} %bitcast.58), custom_call_target="tpu_custom_call" | custom-call | flops 1073741824 | bytes 10485760 | tf_op jit(solution)/shard_map/pallas_call | solution.py:75
  225.8 0.0 all-gather.17.cloned.1.call-update
  225.8 0.0 all-gather.19.cloned.1.call-start
  225.9 0.7 copy.81
  226.6 39.5 %all-gather.17.cloned.1.call-done.whole_ref.refs_2_ = bf16[128,8192]{1,0:T(8,128)(2,1)} async-done(((bf16[128,512]{1,0:T(8,128)(2,1)}), bf16[128,8192]{1,0:T(8,128)(2,1)}) %all-gather.17.cloned.1.call-update) | async-done | bytes 2097168 | tf_op jit(solution)/shard_map/all_gather | solution.py:152
  266.1 9.1 %shard_map.65 = (f32[128,512]{1,0:T(8,128)}, bf16[128,512]{1,0:T(8,128)(2,1)}, f32[128,1]{1,0:T(8,128)}, f32[128,1]{1,0:T(8,128)}) custom-call(bf16[128,8192]{1,0:T(8,128)(2,1)} %all-gather.17.cloned.1.call-done.whole_ref.refs_2_, bf16[512,8192]{1,0:T(8,128)(2,1)} %refs_7_.1, f32[128,512]{1,0:T(8,128)} %get-tuple-element.71.emit_ref, f32[128,512]{1,0:T(8,128)} %bitcast.59), custom_call_target="tpu_custom_call" | custom-call | flops 1073741824 | bytes 10485760 | tf_op jit(solution)/shard_map/pallas_call | solution.py:75
  275.2 0.0 all-gather.19.cloned.1.call-update
  275.2 0.0 all-gather.21.cloned.1.call-start
  275.2 0.7 copy.80
  275.9 39.5 %all-gather.19.cloned.1.call-done.whole_ref.refs_1_ = bf16[128,8192]{1,0:T(8,128)(2,1)} async-done(((bf16[128,512]{1,0:T(8,128)(2,1)}), bf16[128,8192]{1,0:T(8,128)(2,1)}) %all-gather.19.cloned.1.call-update) | async-done | bytes 2097168 | tf_op jit(solution)/shard_map/all_gather | solution.py:152
  315.5 9.2 %shard_map.66 = (f32[128,512]{1,0:T(8,128)}, bf16[128,512]{1,0:T(8,128)(2,1)}, f32[128,1]{1,0:T(8,128)}, f32[128,1]{1,0:T(8,128)}) custom-call(bf16[128,8192]{1,0:T(8,128)(2,1)} %all-gather.19.cloned.1.call-done.whole_ref.refs_1_, bf16[512,8192]{1,0:T(8,128)(2,1)} %refs_7_.1, f32[128,512]{1,0:T(8,128)} %get-tuple-element.70.emit_ref, f32[128,512]{1,0:T(8,128)} %bitcast.60), custom_call_target="tpu_custom_call" | custom-call | flops 1073741824 | bytes 10485760 | tf_op jit(solution)/shard_map/pallas_call | solution.py:75
  324.7 0.7 copy.79
  325.5 0.1 copy.45
  325.5 0.1 copy.52
  325.6 0.1 copy.44
  325.7 0.1 copy.51
  325.8 0.1 copy.43
  325.8 0.1 copy.50
  325.9 0.1 copy.42
  326.0 0.1 copy.49
  326.1 0.1 copy.41
  326.2 0.1 copy.48
  326.3 0.9 copy.40
  327.2 0.9 copy.47
  328.1 36.9 %all-gather.21.cloned.1.call-done.whole_ref.refs_0_ = bf16[128,8192]{1,0:T(8,128)(2,1)} async-done(((bf16[128,512]{1,0:T(8,128)(2,1)}), bf16[128,8192]{1,0:T(8,128)(2,1)}) %all-gather.21.cloned.1.call-update) | async-done | bytes 2097168 | tf_op jit(solution)/shard_map/all_gather | solution.py:152
  365.0 9.1 %shard_map.67 = (f32[128,512]{1,0:T(8,128)}, bf16[128,512]{1,0:T(8,128)(2,1)}, f32[128,1]{1,0:T(8,128)}, f32[128,1]{1,0:T(8,128)}) custom-call(bf16[128,8192]{1,0:T(8,128)(2,1)} %all-gather.21.cloned.1.call-done.whole_ref.refs_0_, bf16[512,8192]{1,0:T(8,128)(2,1)} %refs_7_.1, f32[128,512]{1,0:T(8,128)} %get-tuple-element.69.emit_ref, f32[128,512]{1,0:T(8,128)} %bitcast.54), custom_call_target="tpu_custom_call" | custom-call | flops 1073741824 | bytes 10485760 | tf_op jit(solution)/shard_map/pallas_call | solution.py:75
  374.1 0.9 copy.39
  375.0 0.9 copy.46
  375.9 19.7 %all-gather = f32[2048,7]{0,1:T(8,128)S(1)} all-gather(f32[128,7]{0,1:T(8,128)S(1)} %concatenate.11), channel_id=2, replica_groups=mesh['groups'=2,'state'=16] {'state'}, dimensions={0}, use_global_device_ids=true | all-gather | bytes 60928 | tf_op jit(solution)/shard_map/all_gather | solution.py:165
  395.7 1.0 fusion
  396.7 1.3 copy.53.share_ref
  398.0 1.0 bitcast_dynamic-update-slice_fusion.6
  399.0 1.0 bitcast_dynamic-update-slice_fusion.5
  400.0 1.0 bitcast_dynamic-update-slice_fusion.4
  401.0 1.0 bitcast_dynamic-update-slice_fusion.3
  401.9 1.0 bitcast_dynamic-update-slice_fusion.2
  403.0 2.5 copy.54
  405.6 24.6 %shard_map.68 = f32[512,8192]{1,0:T(8,128)} custom-call(bf16[512,896]{1,0:T(8,128)(2,1)} %copy.53.share_ref, bf16[128,8192]{1,0:T(8,128)(2,1)} %all-gather.21.cloned.1.call-done.whole_ref.refs_0_, bf16[128,8192]{1,0:T(8,128)(2,1)} %all-gather.19.cloned.1.call-done.whole_ref.refs_1_, bf16[128,8192]{1,0:T(8,128)(2,1)} %all-gather.17.cloned.1.call-done.whole_ref.refs_2_, ...), custom_call_target="tpu_custom_call" | custom-call | flops 7516192768 | bytes 39845888 | tf_op jit(solution)/shard_map/pallas_call | solution.py:120
  (39 shorter events, 0.2 us)
Async XLA Ops:
  7.2 61.5 %all-gather.9.cloned.1.call-start = ((), (), s32[]{:S(2)}) async-start(), calls=%async_computation | async-start | bytes 2228224 | tf_op jit(solution)/shard_map/all_gather | solution.py:152
  8.6 16.1 %copy-start.13 = (s32[128,8]{0,1:T(8,128)S(1)}, s32[128,8]{0,1:T(8,128)}, u32[]{:S(2)}) copy-start(s32[128,8]{0,1:T(8,128)} %param.5) | copy-start | bytes 12292
  8.6 17.1 %copy-start = (f32[128,8,512]{2,1,0:T(8,128)S(1)}, f32[128,8,512]{2,1,0:T(8,128)}, u32[]{:S(2)}) copy-start(f32[128,8,512]{2,1,0:T(8,128)} %param.4) | copy-start | bytes 6291460
  24.7 93.4 %all-gather.11.cloned.1.call-start = ((), (), s32[]{:S(2)}) async-start(), calls=%async_computation.1 | async-start | bytes 2228224 | tf_op jit(solution)/shard_map/all_gather | solution.py:152
  77.8 89.6 %all-gather.13.cloned.1.call-start = ((), (), s32[]{:S(2)}) async-start(), calls=%async_computation.2 | async-start | bytes 2228224 | tf_op jit(solution)/shard_map/all_gather | solution.py:152
  127.1 89.6 %all-gather.15.cloned.1.call-start = ((), (), s32[]{:S(2)}) async-start(), calls=%async_computation.3 | async-start | bytes 2228224 | tf_op jit(solution)/shard_map/all_gather | solution.py:152
  176.5 89.6 %all-gather.17.cloned.1.call-start = ((), (), s32[]{:S(2)}) async-start(), calls=%async_computation.4 | async-start | bytes 2228224 | tf_op jit(solution)/shard_map/all_gather | solution.py:152
  225.8 89.6 %all-gather.19.cloned.1.call-start = ((), (), s32[]{:S(2)}) async-start(), calls=%async_computation.5 | async-start | bytes 2228224 | tf_op jit(solution)/shard_map/all_gather | solution.py:152
  275.2 89.8 %all-gather.21.cloned.1.call-start = ((), (), s32[]{:S(2)}) async-start(), calls=%async_computation.6 | async-start | bytes 2228224 | tf_op jit(solution)/shard_map/all_gather | solution.py:152
  315.4 10.0 %copy-start.4 = (f32[128,1]{1,0:T(8,128)S(1)}, f32[128,1]{1,0:T(8,128)}, u32[]{:S(2)}) copy-start(f32[128,1]{1,0:T(8,128)} %get-tuple-element.48) | copy-start | bytes 1540
  315.5 10.1 %copy-start.3 = (f32[128,1]{1,0:T(8,128)S(1)}, f32[128,1]{1,0:T(8,128)}, u32[]{:S(2)}) copy-start(f32[128,1]{1,0:T(8,128)} %get-tuple-element.55) | copy-start | bytes 1540
  315.5 10.1 %copy-start.6 = (f32[128,1]{1,0:T(8,128)S(1)}, f32[128,1]{1,0:T(8,128)}, u32[]{:S(2)}) copy-start(f32[128,1]{1,0:T(8,128)} %get-tuple-element.47) | copy-start | bytes 1540
  315.5 10.2 %copy-start.5 = (f32[128,1]{1,0:T(8,128)S(1)}, f32[128,1]{1,0:T(8,128)}, u32[]{:S(2)}) copy-start(f32[128,1]{1,0:T(8,128)} %get-tuple-element.54) | copy-start | bytes 1540
  315.5 10.3 %copy-start.8 = (f32[128,1]{1,0:T(8,128)S(1)}, f32[128,1]{1,0:T(8,128)}, u32[]{:S(2)}) copy-start(f32[128,1]{1,0:T(8,128)} %get-tuple-element.46) | copy-start | bytes 1540
  315.5 10.4 %copy-start.7 = (f32[128,1]{1,0:T(8,128)S(1)}, f32[128,1]{1,0:T(8,128)}, u32[]{:S(2)}) copy-start(f32[128,1]{1,0:T(8,128)} %get-tuple-element.53) | copy-start | bytes 1540
  315.5 10.5 %copy-start.10 = (f32[128,1]{1,0:T(8,128)S(1)}, f32[128,1]{1,0:T(8,128)}, u32[]{:S(2)}) copy-start(f32[128,1]{1,0:T(8,128)} %get-tuple-element.45) | copy-start | bytes 1540
  315.5 10.5 %copy-start.9 = (f32[128,1]{1,0:T(8,128)S(1)}, f32[128,1]{1,0:T(8,128)}, u32[]{:S(2)}) copy-start(f32[128,1]{1,0:T(8,128)} %get-tuple-element.52) | copy-start | bytes 1540
  315.5 10.6 %copy-start.12 = (f32[128,1]{1,0:T(8,128)S(1)}, f32[128,1]{1,0:T(8,128)}, u32[]{:S(2)}) copy-start(f32[128,1]{1,0:T(8,128)} %get-tuple-element.44) | copy-start | bytes 1540
  315.5 10.7 %copy-start.11 = (f32[128,1]{1,0:T(8,128)S(1)}, f32[128,1]{1,0:T(8,128)}, u32[]{:S(2)}) copy-start(f32[128,1]{1,0:T(8,128)} %get-tuple-element.51) | copy-start | bytes 1540
  396.7 6.2 %copy-start.1 = (f32[128,512]{1,0:T(8,128)S(1)}, f32[128,512]{1,0:T(8,128)}, u32[]{:S(2)}) copy-start(f32[128,512]{1,0:T(8,128)} %get-tuple-element.41) | copy-start | bytes 786436
  398.0 4.9 %copy-start.2 = (f32[128,512]{1,0:T(8,128)S(1)}, f32[128,512]{1,0:T(8,128)}, u32[]{:S(2)}) copy-start(f32[128,512]{1,0:T(8,128)} %get-tuple-element.40) | copy-start | bytes 786436
Sparse Core Ops, SparseCore 0:
  24.8 43.8 all-gather.8
  77.9 40.1 all-gather.10
  127.2 40.1 all-gather.12
  176.6 40.1 all-gather.14
  225.9 40.1 all-gather.16
  275.3 40.1 all-gather.18
  324.8 40.1 all-gather.20

commit v4 on v2

--- a/solution.py
+++ b/solution.py
@@ -95,33 +95,10 @@
     )(whole, transition, emit_next, fwd)
 
 
-def _counts_kernel(factor, steps, share_ref, *refs):
-    w_refs = refs[:steps]
-    trans_ref = refs[steps]
-    out_ref = refs[steps + 1]
-    acc = jnp.dot(share_ref[0], w_refs[0][...], preferred_element_type=jnp.float32)
-    for t in range(1, steps):
-        acc += jnp.dot(share_ref[t], w_refs[t][...], preferred_element_type=jnp.float32)
-    out_ref[...] = trans_ref[...].astype(jnp.float32) * acc * factor
-
-
-def trans_counts_of(share_t, stored, transition, factor, tn=512):
-    steps, rows, b = share_t.shape
-    states = transition.shape[1]
-    return pl.pallas_call(
-        functools.partial(_counts_kernel, factor, steps),
-        grid=(states // tn,),
-        in_specs=[pl.BlockSpec((steps, rows, b), lambda j: (0, 0, 0))]
-        + [pl.BlockSpec((b, tn), lambda j: (0, j)) for _ in range(steps)]
-        + [pl.BlockSpec((rows, tn), lambda j: (0, j))],
-        out_specs=pl.BlockSpec((rows, tn), lambda j: (0, j)),
-        out_shape=jax.ShapeDtypeStruct((rows, states), jnp.float32),
-        cost_estimate=pl.CostEstimate(
-            flops=2 * steps * b * rows * states,
-            bytes_accessed=steps * b * states * 2 + rows * states * 6,
-            transcendentals=0,
-        ),
-    )(share_t, *stored, transition)
+def emitted_rows_xla(ids, emission):
+    vocab = emission.shape[1]
+    onehot = (ids[:, None] == lax.broadcasted_iota(jnp.int32, (1, vocab), 1)).astype(emission.dtype)
+    return lax.dot_general(onehot, emission, NT, preferred_element_type=jnp.float32)
 
 
 def on_device(forward_probs, token_ids, transition, emission):
@@ -130,12 +107,12 @@
     seq_count = token_ids.shape[0]
     step_count = token_ids.shape[1]
     last = step_count - 1
-    emitted_last = emitted_rows(token_ids[:, last], emission)
+    emitted_last = emitted_rows_xla(token_ids[:, last], emission)
     early_ids = token_ids[:, :last].T.reshape(-1)
     emitted_early = emitted_rows(early_ids, emission).reshape(last, seq_count, state_rows)
     weighted = emitted_last.astype(jnp.bfloat16)
     backs = [jnp.ones((seq_count, state_rows), jnp.float32)]
-    stored = []
+    vector_mat = jnp.zeros((last * seq_count, states), jnp.bfloat16)
     scales = []
     norms = []
     for t in range(step_count - 2, -1, -1):
@@ -143,12 +120,11 @@
         backward, weighted, scale_sum, norm_part = backward_step(
             whole, transition, emitted_early[t], forward_probs[:, t, :]
         )
-        stored.append(whole)
+        vector_mat = lax.dynamic_update_slice(vector_mat, whole, (t * seq_count, 0))
         scales.append(scale_sum)
         backs.append(backward)
         norms.append(norm_part)
     backs = backs[::-1]
-    stored = stored[::-1]
     scales = jnp.concatenate(scales[::-1], axis=1)
     partial_norms = jnp.concatenate(norms[::-1], axis=1)
     backward_probs = jnp.stack(backs, axis=1)
@@ -156,9 +132,12 @@
     norm_sums = jnp.sum(norm_parts, axis=0)
     denom = scales * norm_sums
     share_t = (forward_probs[:, :last, :] / denom[:, :, None]).astype(jnp.bfloat16)
-    share_t = jnp.transpose(share_t, (1, 2, 0))
+    share_mat = jnp.transpose(share_t, (1, 0, 2)).reshape(last * seq_count, state_rows)
+    moments = lax.dot_general(
+        share_mat, vector_mat, (((0,), (0,)), ((), ())), preferred_element_type=jnp.float32
+    )
     factor = float(states) * float(states) / float(seq_count * (step_count - 1))
-    trans_counts = trans_counts_of(share_t, stored, transition, factor)
+    trans_counts = transition.astype(jnp.float32) * moments * factor
     return (backward_probs, trans_counts)
 
 

time: 424 us -> 414 us (0.976)
  Pallas kernels: 114 us -> 73.7 us
  matrix products: 0 us -> 31.4 us
  local copies, waits for them, and re-layouts: 21.5 us -> 37.9 us
  waiting for transfers between devices: 249 us -> 233 us
    dot_general x0 -> x2, matrix products: none -> 31.4 us  [the longest x1 19.3 us: on_device(): lax.dot_general(share_mat, vector_mat, (((0,), (0,)), ((), ())), preferre...]
    pallas_call x1 -> x0, Pallas kernels: 25.4 us -> none  [trans_counts_of(): pl.pallas_call(functools.partial(_counts_kernel, factor, steps), grid=(st...]
    dynamic_update_slice x0 -> x7, local copies, waits for them, and re-layouts: none -> 20.1 us  [on_device(): vector_mat = lax.dynamic_update_slice(vector_mat, whole, (t * seq_count, 0))]
    all_gather x7, waiting for transfers between devices: 249 us -> 233 us  [on_device(): whole = lax.all_gather(weighted, 'state', axis=1, tiled=True)]
    pallas_call x2 -> x1, Pallas kernels: 37.5 us -> 21.8 us  [emitted_rows(): pl.pallas_call(_emit_kernel, grid=(vocab // tv,), in_specs=[pl.BlockSpec(...]
    unnamed x62 -> x70, local copies, waits for them, and re-layouts: 13.3 us -> 9.75 us
  transfers between devices with their start and end apart: 7 -> 7, of which waited for: 7 -> 7; matrix products, arithmetic and copies ran while one was open for 3% -> 7% of each run, Pallas kernels for 5% -> 5%
where the time goes in v4:
time: 414 us; the launch traced here: 413 us
  waiting for transfers between devices  233 us (56%)
  Pallas kernels  73.7 us (18%)
  local copies, waits for them, and re-layouts  37.9 us (9%)
  matrix products  31.4 us (8%)
  blocking collectives  19.5 us (5%)
  between operations  14.4 us (3%)
    all_gather x7, waiting for transfers between devices, on_device(): whole = lax.all_gather(weighted, 'state', axis=1, tiled=True)  233 us
    pallas_call x7, Pallas kernels, backward_step(): pl.pallas_call(_step_kernel, grid=(states // tk,), in_specs=[pl.BlockSpec...  51.9 us
    pallas_call x1, Pallas kernels, emitted_rows(): pl.pallas_call(_emit_kernel, grid=(vocab // tv,), in_specs=[pl.BlockSpec(...  21.8 us
    dynamic_update_slice x7, local copies, waits for them, and re-layouts, on_device(): vector_mat = lax.dynamic_update_slice(vector_mat, whole, (t * seq_count, 0))  20.1 us
    all_gather x1, blocking collectives, on_device(): norm_parts = lax.all_gather(partial_norms, 'state', axis=0, tiled=False)  19.5 us
    dot_general x1, matrix products, on_device(): lax.dot_general(share_mat, vector_mat, (((0,), (0,)), ((), ())), preferre...  19.3 us
    dot_general x1, matrix products, emitted_rows_xla(): lax.dot_general(onehot, emission, NT, preferred_element_type=jnp.float32)  12.2 us
    unnamed x70, local copies, waits for them, and re-layouts  9.75 us
  transfers between devices with their start and end apart: 7, of which 7 were waited for; matrix products, arithmetic and copies ran while one was open for 7% of the time, Pallas kernels for 5%

profile of v4, /device:TPU:0, one launch (start us, length us, event | category | flops | bytes accessed | tf_op | source)
XLA Modules:
  0.0 413.5 jit_solution(10244450534752723184)
XLA Ops:
  7.2 0.0 all-gather.9.cloned.1.call-start
  7.2 0.7 slice_bitcast_fusion.1
  7.9 12.2 %fusion.3 = bf16[128,512]{1,0:T(8,128)(2,1)} fusion(bf16[512,16384]{1,0:T(8,128)(2,1)} %em_ref.1, s32[128]{0:T(128)S(1)} %slice_bitcast_fusion.1), kind=kOutput, calls=%fused_computation.6 | convolution fusion | flops 2149646336 | bytes 16908800 | tf_op jit(solution)/shard_map/dot_general | solution.py:101
  20.1 0.0 all-gather.11.cloned.1.call-start
  20.2 1.0 copy.58
  21.2 1.9 fusion.4
  23.1 0.7 copy.78
  23.8 21.8 %shard_map.59 = f32[896,512]{1,0:T(8,128)} custom-call(s32[896,1]{1,0:T(8,128)} %bitcast.66, bf16[512,16384]{1,0:T(8,128)(2,1)} %em_ref.1), custom_call_target="tpu_custom_call" | custom-call | flops 15032385536 | bytes 18612224 | tf_op jit(solution)/shard_map/pallas_call | solution.py:29
  45.6 2.7 fusion.5
  48.3 15.9 %all-gather.9.cloned.1.call-done.whole_ref = bf16[128,8192]{1,0:T(8,128)(2,1)} async-done(((bf16[128,512]{1,0:T(8,128)(2,1)}), bf16[128,8192]{1,0:T(8,128)(2,1)}) %all-gather.9.cloned.1.call-update) | async-done | bytes 2097168 | tf_op jit(solution)/shard_map/all_gather | solution.py:119
  64.1 7.4 %shard_map.60 = (f32[128,512]{1,0:T(8,128)}, bf16[128,512]{1,0:T(8,128)(2,1)}, f32[128,1]{1,0:T(8,128)}, f32[128,1]{1,0:T(8,128)}) custom-call(bf16[128,8192]{1,0:T(8,128)(2,1)} %all-gather.9.cloned.1.call-done.whole_ref, bf16[512,8192]{1,0:T(8,128)(2,1)} %trans_ref.13, f32[128,512]{1,0:T(8,128)} %get-tuple-element.75.emit_ref, f32[128,512]{1,0:T(8,128)} %bitcast.60), custom_call_target="tpu_custom_call" | custom-call | flops 1073741824 | bytes 10485760 | tf_op jit(solution)/shard_map/pallas_call | solution.py:70
  71.5 0.0 all-gather.13.cloned.1.call-start
  71.6 0.7 copy.77
  72.3 39.5 %all-gather.11.cloned.1.call-done.whole_ref = bf16[128,8192]{1,0:T(8,128)(2,1)} async-done(((bf16[128,512]{1,0:T(8,128)(2,1)}), bf16[128,8192]{1,0:T(8,128)(2,1)}) %all-gather.11.cloned.1.call-update) | async-done | bytes 2097168 | tf_op jit(solution)/shard_map/all_gather | solution.py:119
  111.8 7.4 %shard_map.61 = (f32[128,512]{1,0:T(8,128)}, bf16[128,512]{1,0:T(8,128)(2,1)}, f32[128,1]{1,0:T(8,128)}, f32[128,1]{1,0:T(8,128)}) custom-call(bf16[128,8192]{1,0:T(8,128)(2,1)} %all-gather.11.cloned.1.call-done.whole_ref, bf16[512,8192]{1,0:T(8,128)(2,1)} %trans_ref.13, f32[128,512]{1,0:T(8,128)} %get-tuple-element.74.emit_ref, f32[128,512]{1,0:T(8,128)} %bitcast.62), custom_call_target="tpu_custom_call" | custom-call | flops 1073741824 | bytes 10485760 | tf_op jit(solution)/shard_map/pallas_call | solution.py:70
  119.2 0.0 all-gather.13.cloned.1.call-update
  119.2 0.0 all-gather.15.cloned.1.call-start
  119.2 0.7 copy.76
  120.0 39.5 %all-gather.13.cloned.1.call-done.whole_ref = bf16[128,8192]{1,0:T(8,128)(2,1)} async-done(((bf16[128,512]{1,0:T(8,128)(2,1)}), bf16[128,8192]{1,0:T(8,128)(2,1)}) %all-gather.13.cloned.1.call-update) | async-done | bytes 2097168 | tf_op jit(solution)/shard_map/all_gather | solution.py:119
  159.5 7.4 %shard_map.62 = (f32[128,512]{1,0:T(8,128)}, bf16[128,512]{1,0:T(8,128)(2,1)}, f32[128,1]{1,0:T(8,128)}, f32[128,1]{1,0:T(8,128)}) custom-call(bf16[128,8192]{1,0:T(8,128)(2,1)} %all-gather.13.cloned.1.call-done.whole_ref, bf16[512,8192]{1,0:T(8,128)(2,1)} %trans_ref.13, f32[128,512]{1,0:T(8,128)} %get-tuple-element.73.emit_ref, f32[128,512]{1,0:T(8,128)} %bitcast.63), custom_call_target="tpu_custom_call" | custom-call | flops 1073741824 | bytes 10485760 | tf_op jit(solution)/shard_map/pallas_call | solution.py:70
  166.8 0.0 all-gather.15.cloned.1.call-update
  166.9 0.0 all-gather.17.cloned.1.call-start
  166.9 0.7 copy.75
  167.6 39.5 %all-gather.15.cloned.1.call-done.whole_ref = bf16[128,8192]{1,0:T(8,128)(2,1)} async-done(((bf16[128,512]{1,0:T(8,128)(2,1)}), bf16[128,8192]{1,0:T(8,128)(2,1)}) %all-gather.15.cloned.1.call-update) | async-done | bytes 2097168 | tf_op jit(solution)/shard_map/all_gather | solution.py:119
  207.1 7.4 %shard_map.63 = (f32[128,512]{1,0:T(8,128)}, bf16[128,512]{1,0:T(8,128)(2,1)}, f32[128,1]{1,0:T(8,128)}, f32[128,1]{1,0:T(8,128)}) custom-call(bf16[128,8192]{1,0:T(8,128)(2,1)} %all-gather.15.cloned.1.call-done.whole_ref, bf16[512,8192]{1,0:T(8,128)(2,1)} %trans_ref.13, f32[128,512]{1,0:T(8,128)} %get-tuple-element.72.emit_ref, f32[128,512]{1,0:T(8,128)} %bitcast.64), custom_call_target="tpu_custom_call" | custom-call | flops 1073741824 | bytes 10485760 | tf_op jit(solution)/shard_map/pallas_call | solution.py:70
  214.5 0.0 all-gather.17.cloned.1.call-update
  214.5 0.0 all-gather.19.cloned.1.call-start
  214.6 0.7 copy.74
  215.3 39.5 %all-gather.17.cloned.1.call-done.whole_ref = bf16[128,8192]{1,0:T(8,128)(2,1)} async-done(((bf16[128,512]{1,0:T(8,128)(2,1)}), bf16[128,8192]{1,0:T(8,128)(2,1)}) %all-gather.17.cloned.1.call-update) | async-done | bytes 2097168 | tf_op jit(solution)/shard_map/all_gather | solution.py:119
  254.8 7.5 %shard_map.64 = (f32[128,512]{1,0:T(8,128)}, bf16[128,512]{1,0:T(8,128)(2,1)}, f32[128,1]{1,0:T(8,128)}, f32[128,1]{1,0:T(8,128)}) custom-call(bf16[128,8192]{1,0:T(8,128)(2,1)} %all-gather.17.cloned.1.call-done.whole_ref, bf16[512,8192]{1,0:T(8,128)(2,1)} %trans_ref.13, f32[128,512]{1,0:T(8,128)} %get-tuple-element.71.emit_ref, f32[128,512]{1,0:T(8,128)} %bitcast.65), custom_call_target="tpu_custom_call" | custom-call | flops 1073741824 | bytes 10485760 | tf_op jit(solution)/shard_map/pallas_call | solution.py:70
  262.3 0.2 all-gather.21.cloned.1.call-start
  262.6 0.7 copy.73
  263.3 0.7 copy.72
  264.0 0.1 copy.47
  264.1 0.1 copy.40
  264.1 7.4 %dynamic_update_slice.21 = bf16[896,8192]{1,0:T(8,128)(2,1)} pad(bf16[128,8192]{1,0:T(8,128)(2,1)S(1)} %copy-done, bf16[]{:T(256)} %constant.1.clone.1), padding=768_0x0_0 | pad | bytes 16777218 | tf_op jit(solution)/shard_map/dynamic_update_slice | solution.py:123
  271.5 31.1 %all-gather.19.cloned.1.call-done.whole_ref = bf16[128,8192]{1,0:T(8,128)(2,1)} async-done(((bf16[128,512]{1,0:T(8,128)(2,1)}), bf16[128,8192]{1,0:T(8,128)(2,1)}) %all-gather.19.cloned.1.call-update) | async-done | bytes 2097168 | tf_op jit(solution)/shard_map/all_gather | solution.py:119
  302.6 7.5 %shard_map.65 = (f32[128,512]{1,0:T(8,128)}, bf16[128,512]{1,0:T(8,128)(2,1)}, f32[128,1]{1,0:T(8,128)}, f32[128,1]{1,0:T(8,128)}) custom-call(bf16[128,8192]{1,0:T(8,128)(2,1)} %all-gather.19.cloned.1.call-done.whole_ref, bf16[512,8192]{1,0:T(8,128)(2,1)} %trans_ref.13, f32[128,512]{1,0:T(8,128)} %get-tuple-element.70.emit_ref, f32[128,512]{1,0:T(8,128)} %bitcast.61), custom_call_target="tpu_custom_call" | custom-call | flops 1073741824 | bytes 10485760 | tf_op jit(solution)/shard_map/pallas_call | solution.py:70
  310.1 0.0 all-gather.21.cloned.1.call-update
  310.2 1.6 constant_dynamic-update-slice_fusion.5
  311.7 0.1 copy.46
  311.8 0.1 copy.39
  311.9 0.1 copy.45
  311.9 0.1 copy.38
  312.0 3.3 constant_dynamic-update-slice_fusion.4
  315.3 0.1 copy.44
  315.4 0.1 copy.37
  315.5 1.5 constant_dynamic-update-slice_fusion.3
  317.0 0.1 copy.43
  317.1 0.1 copy.36
  317.2 3.3 constant_dynamic-update-slice_fusion.2
  320.5 0.1 copy.42
  320.5 0.1 copy.35
  320.6 1.5 constant_dynamic-update-slice_fusion.1
  322.1 28.2 %all-gather.21.cloned.1.call-done.whole_ref = bf16[128,8192]{1,0:T(8,128)(2,1)} async-done(((bf16[128,512]{1,0:T(8,128)(2,1)}), bf16[128,8192]{1,0:T(8,128)(2,1)}) %all-gather.21.cloned.1.call-update) | async-done | bytes 2097168 | tf_op jit(solution)/shard_map/all_gather | solution.py:119
  350.4 7.4 %shard_map.66 = (f32[128,512]{1,0:T(8,128)}, bf16[128,512]{1,0:T(8,128)(2,1)}, f32[128,1]{1,0:T(8,128)}, f32[128,1]{1,0:T(8,128)}) custom-call(bf16[128,8192]{1,0:T(8,128)(2,1)} %all-gather.21.cloned.1.call-done.whole_ref, bf16[512,8192]{1,0:T(8,128)(2,1)} %trans_ref.13, f32[128,512]{1,0:T(8,128)} %get-tuple-element.69.emit_ref, f32[128,512]{1,0:T(8,128)} %bitcast.59), custom_call_target="tpu_custom_call" | custom-call | flops 1073741824 | bytes 10485760 | tf_op jit(solution)/shard_map/pallas_call | solution.py:70
  357.8 1.0 copy.41
  358.9 19.5 %all-gather = f32[2048,7]{0,1:T(8,128)S(1)} all-gather(f32[128,7]{0,1:T(8,128)S(1)} %concatenate.11), channel_id=2, replica_groups=mesh['groups'=2,'state'=16] {'state'}, dimensions={0}, use_global_device_ids=true | all-gather | bytes 60928 | tf_op jit(solution)/shard_map/all_gather | solution.py:131
  378.4 0.9 copy.34
  379.3 1.0 bitcast_dynamic-update-slice_fusion.6
  380.5 2.5 copy.48
  383.1 2.8 fusion.2
  385.9 1.5 constant_dynamic-update-slice_fusion
  387.3 19.3 %multiply_multiply_fusion = f32[512,8192]{1,0:T(8,128)} fusion(bf16[512,8192]{1,0:T(8,128)(2,1)} %trans_ref.13, bf16[896,512]{1,0:T(8,128)(2,1)S(1)} %bitcast.57, bf16[896,8192]{1,0:T(8,128)(2,1)} %constant_dynamic-update-slice_fusion), kind=kOutput, calls=%fused_computation | convolution fusion | flops 7528775680 | bytes 40763392 | tf_op jit(solution)/shard_map/dot_general | solution.py:136
  (68 shorter events, 0.4 us)
Async XLA Ops:
  7.2 57.0 %all-gather.9.cloned.1.call-start = ((), (), s32[]{:S(2)}) async-start(), calls=%async_computation | async-start | bytes 2228224 | tf_op jit(solution)/shard_map/all_gather | solution.py:119
  7.9 12.2 %copy-start.25 = (s32[128,8]{0,1:T(8,128)S(1)}, s32[128,8]{0,1:T(8,128)}, u32[]{:S(2)}) copy-start(s32[128,8]{0,1:T(8,128)} %param.5) | copy-start | bytes 12292
  7.9 13.2 %copy-start.5 = (f32[128,8,512]{2,1,0:T(8,128)S(1)}, f32[128,8,512]{2,1,0:T(8,128)}, u32[]{:S(2)}) copy-start(f32[128,8,512]{2,1,0:T(8,128)} %param.4) | copy-start | bytes 6291460
  20.1 91.7 %all-gather.11.cloned.1.call-start = ((), (), s32[]{:S(2)}) async-start(), calls=%async_computation.1 | async-start | bytes 2228224 | tf_op jit(solution)/shard_map/all_gather | solution.py:119
  64.1 7.4 %copy-start.6 = (f32[128,1,512]{2,1,0:T(1,128)S(1)}, f32[128,1,512]{2,1,0:T(1,128)}, u32[]{:S(2)}) copy-start(f32[128,1,512]{2,1,0:T(1,128)} %get-tuple-element.67) | copy-start | bytes 786436
  71.5 88.0 %all-gather.13.cloned.1.call-start = ((), (), s32[]{:S(2)}) async-start(), calls=%async_computation.2 | async-start | bytes 2228224 | tf_op jit(solution)/shard_map/all_gather | solution.py:119
  119.2 87.9 %all-gather.15.cloned.1.call-start = ((), (), s32[]{:S(2)}) async-start(), calls=%async_computation.3 | async-start | bytes 2228224 | tf_op jit(solution)/shard_map/all_gather | solution.py:119
  166.9 87.9 %all-gather.17.cloned.1.call-start = ((), (), s32[]{:S(2)}) async-start(), calls=%async_computation.4 | async-start | bytes 2228224 | tf_op jit(solution)/shard_map/all_gather | solution.py:119
  214.5 88.1 %all-gather.19.cloned.1.call-start = ((), (), s32[]{:S(2)}) async-start(), calls=%async_computation.5 | async-start | bytes 2228224 | tf_op jit(solution)/shard_map/all_gather | solution.py:119
  254.8 9.2 %copy-start.16 = (f32[128,1]{1,0:T(8,128)S(1)}, f32[128,1]{1,0:T(8,128)}, u32[]{:S(2)}) copy-start(f32[128,1]{1,0:T(8,128)} %get-tuple-element.55) | copy-start | bytes 1540
  254.8 9.3 %copy-start.15 = (f32[128,1]{1,0:T(8,128)S(1)}, f32[128,1]{1,0:T(8,128)}, u32[]{:S(2)}) copy-start(f32[128,1]{1,0:T(8,128)} %get-tuple-element.48) | copy-start | bytes 1540
  254.8 9.3 %copy-start = (bf16[128,8192]{1,0:T(8,128)(2,1)S(1)}, bf16[128,8192]{1,0:T(8,128)(2,1)}, u32[]{:S(2)}) copy-start(bf16[128,8192]{1,0:T(8,128)(2,1)} %all-gather.9.cloned.1.call-done.whole_ref) | copy-start | bytes 6291460
  262.3 88.1 %all-gather.21.cloned.1.call-start = ((), (), s32[]{:S(2)}) async-start(), calls=%async_computation.6 | async-start | bytes 2228224 | tf_op jit(solution)/shard_map/all_gather | solution.py:119
  302.6 7.5 %copy-start.1 = (bf16[128,8192]{1,0:T(8,128)(2,1)S(1)}, bf16[128,8192]{1,0:T(8,128)(2,1)}, u32[]{:S(2)}) copy-start(bf16[128,8192]{1,0:T(8,128)(2,1)} %all-gather.11.cloned.1.call-done.whole_ref) | copy-start | bytes 6291460
  310.1 1.6 copy-start.14
  310.1 1.7 copy-start.13
  310.1 1.7 copy-start.18
  310.1 1.8 copy-start.17
  312.0 3.3 copy-start.20
  312.0 3.3 copy-start.19
  312.0 3.4 copy-start.3
  315.5 1.6 copy-start.22
  315.5 1.6 copy-start.21
  317.2 3.3 copy-start.24
  317.2 3.4 copy-start.23
  317.2 3.5 copy-start.4
  350.4 29.9 %copy-start.12 = (f32[128,512]{1,0:T(8,128)S(1)}, f32[128,512]{1,0:T(8,128)}, u32[]{:S(2)}) copy-start(f32[128,512]{1,0:T(8,128)} %get-tuple-element.36) | copy-start | bytes 786436
  350.4 29.9 %copy-start.11 = (f32[128,512]{1,0:T(8,128)S(1)}, f32[128,512]{1,0:T(8,128)}, u32[]{:S(2)}) copy-start(f32[128,512]{1,0:T(8,128)} %get-tuple-element.37) | copy-start | bytes 786436
  350.4 30.0 %copy-start.10 = (f32[128,512]{1,0:T(8,128)S(1)}, f32[128,512]{1,0:T(8,128)}, u32[]{:S(2)}) copy-start(f32[128,512]{1,0:T(8,128)} %get-tuple-element.38) | copy-start | bytes 786436
  357.8 22.6 %copy-start.9 = (f32[128,512]{1,0:T(8,128)S(1)}, f32[128,512]{1,0:T(8,128)}, u32[]{:S(2)}) copy-start(f32[128,512]{1,0:T(8,128)} %get-tuple-element.39) | copy-start | bytes 786436
  357.8 22.6 %copy-start.8 = (f32[128,512]{1,0:T(8,128)S(1)}, f32[128,512]{1,0:T(8,128)}, u32[]{:S(2)}) copy-start(f32[128,512]{1,0:T(8,128)} %get-tuple-element.40) | copy-start | bytes 786436
  357.8 22.6 %copy-start.7 = (f32[128,512]{1,0:T(8,128)S(1)}, f32[128,512]{1,0:T(8,128)}, u32[]{:S(2)}) copy-start(f32[128,512]{1,0:T(8,128)} %get-tuple-element.41) | copy-start | bytes 786436
  383.1 2.8 copy-start.2
Sparse Core Ops, SparseCore 0:
  20.2 43.8 all-gather.8
  71.6 40.1 all-gather.10
  119.3 40.1 all-gather.12
  167.0 40.1 all-gather.14
  214.6 40.1 all-gather.16
  262.4 40.1 all-gather.18
  310.2 40.1 all-gather.20

commit v5 on v4

--- a/solution.py
+++ b/solution.py
@@ -95,6 +95,30 @@
     )(whole, transition, emit_next, fwd)
 
 
+def _transpose_kernel(x_ref, o_ref):
+    o_ref[...] = x_ref[...].T
+
+
+def transposed(x, tile=512):
+    rows, cols = x.shape
+    return pl.pallas_call(
+        _transpose_kernel,
+        grid=(cols // tile,),
+        in_specs=[pl.BlockSpec((rows, tile), lambda j: (0, j))],
+        out_specs=pl.BlockSpec((tile, rows), lambda j: (j, 0)),
+        out_shape=jax.ShapeDtypeStruct((cols, rows), x.dtype),
+    )(x)
+
+
+def backward_step_xla(whole, transition_t, emit_next, fwd):
+    product = jnp.dot(whole, transition_t, preferred_element_type=jnp.float32)
+    scale_sum = jnp.sum(whole.astype(jnp.float32), axis=1, keepdims=True)
+    backward = product / scale_sum
+    weighted = (emit_next * backward).astype(jnp.bfloat16)
+    norm_part = jnp.sum(fwd * backward, axis=1, keepdims=True)
+    return backward, weighted, scale_sum, norm_part
+
+
 def emitted_rows_xla(ids, emission):
     vocab = emission.shape[1]
     onehot = (ids[:, None] == lax.broadcasted_iota(jnp.int32, (1, vocab), 1)).astype(emission.dtype)
@@ -111,14 +135,15 @@
     early_ids = token_ids[:, :last].T.reshape(-1)
     emitted_early = emitted_rows(early_ids, emission).reshape(last, seq_count, state_rows)
     weighted = emitted_last.astype(jnp.bfloat16)
+    transition_t = transposed(transition)
     backs = [jnp.ones((seq_count, state_rows), jnp.float32)]
     vector_mat = jnp.zeros((last * seq_count, states), jnp.bfloat16)
     scales = []
     norms = []
     for t in range(step_count - 2, -1, -1):
         whole = lax.all_gather(weighted, "state", axis=1, tiled=True)
-        backward, weighted, scale_sum, norm_part = backward_step(
-            whole, transition, emitted_early[t], forward_probs[:, t, :]
+        backward, weighted, scale_sum, norm_part = backward_step_xla(
+            whole, transition_t, emitted_early[t], forward_probs[:, t, :]
         )
         vector_mat = lax.dynamic_update_slice(vector_mat, whole, (t * seq_count, 0))
         scales.append(scale_sum)

time: 414 us -> 414 us (level)
  Pallas kernels: 73.7 us -> 35.1 us
  matrix products: 31.4 us -> 68.9 us
  other arithmetic: 2.78 us -> 17.4 us
  local copies, waits for them, and re-layouts: 37.9 us -> 28 us
    pallas_call x7 -> x1, Pallas kernels: 51.9 us -> 13.2 us  [transposed(): pl.pallas_call(_transpose_kernel, grid=(cols // tile,), in_specs=[pl.Bloc...]
    dot_general x0 -> x7, matrix products: none -> 37.6 us  [backward_step_xla(): product = jnp.dot(whole, transition_t, preferred_element_type=jnp.float32)]
    reduce_sum x0 -> x8, other arithmetic: none -> 14.7 us  [the longest x7 14.6 us: backward_step_xla(): scale_sum = jnp.sum(whole.astype(jnp.float32), axis=1, keepdims=True)]
    all_gather x7, waiting for transfers between devices: 233 us -> 229 us  [on_device(): whole = lax.all_gather(weighted, 'state', axis=1, tiled=True)]
    unnamed x70 -> x44, local copies, waits for them, and re-layouts: 9.75 us -> 8.96 us
  transfers between devices with their start and end apart: 7 -> 7, of which waited for: 7 -> 7; matrix products, arithmetic and copies ran while one was open for 7% -> 4% of each run, Pallas kernels for 5% -> 8%
where the time goes in v5:
time: 414 us; the launch traced here: 413 us
  waiting for transfers between devices  229 us (55%)
  matrix products  68.9 us (17%)
  Pallas kernels  35.1 us (8%)
  local copies, waits for them, and re-layouts  28 us (7%)
  blocking collectives  19.7 us (5%)
  other arithmetic  17.4 us (4%)
  between operations  14.3 us (3%)
    all_gather x7, waiting for transfers between devices, on_device(): whole = lax.all_gather(weighted, 'state', axis=1, tiled=True)  229 us
    dot_general x7, matrix products, backward_step_xla(): product = jnp.dot(whole, transition_t, preferred_element_type=jnp.float32)  37.6 us
    pallas_call x1, Pallas kernels, emitted_rows(): pl.pallas_call(_emit_kernel, grid=(vocab // tv,), in_specs=[pl.BlockSpec(...  21.8 us
    all_gather x1, blocking collectives, on_device(): norm_parts = lax.all_gather(partial_norms, 'state', axis=0, tiled=False)  19.7 us
    dot_general x1, matrix products, on_device(): lax.dot_general(share_mat, vector_mat, (((0,), (0,)), ((), ())), preferre...  19.3 us
    dynamic_update_slice x7, local copies, waits for them, and re-layouts, on_device(): vector_mat = lax.dynamic_update_slice(vector_mat, whole, (t * seq_count, 0))  16.3 us
    reduce_sum x7, other arithmetic, backward_step_xla(): scale_sum = jnp.sum(whole.astype(jnp.float32), axis=1, keepdims=True)  14.6 us
    pallas_call x1, Pallas kernels, transposed(): pl.pallas_call(_transpose_kernel, grid=(cols // tile,), in_specs=[pl.Bloc...  13.2 us
  transfers between devices with their start and end apart: 7, of which 7 were waited for; matrix products, arithmetic and copies ran while one was open for 4% of the time, Pallas kernels for 8%

profile of v5, /device:TPU:0, one launch (start us, length us, event | category | flops | bytes accessed | tf_op | source)
XLA Modules:
  0.0 412.7 jit_solution(4817599604623986873)
XLA Ops:
  7.2 0.0 all-gather.9.cloned.1.call-start
  7.2 0.7 slice_bitcast_fusion.1
  7.9 12.0 %fusion.3 = bf16[128,512]{1,0:T(8,128)(2,1)} fusion(bf16[512,16384]{1,0:T(8,128)(2,1)} %em_ref.1, s32[128]{0:T(128)S(1)} %slice_bitcast_fusion.1), kind=kOutput, calls=%fused_computation.13 | convolution fusion | flops 2149646336 | bytes 16908800 | tf_op jit(solution)/shard_map/dot_general | solution.py:125
  19.9 0.0 all-gather.9.cloned.1.call-update
  19.9 0.0 all-gather.11.cloned.1.call-start
  20.0 1.0 copy.34
  21.0 13.2 %shard_map.60 = bf16[8192,512]{1,0:T(8,128)(2,1)} custom-call(bf16[512,8192]{1,0:T(8,128)(2,1)} %x_ref.1), custom_call_target="tpu_custom_call" | custom-call | tf_op jit(solution)/shard_map/pallas_call | solution.py:104
  34.2 1.9 fusion.24
  36.2 21.8 %shard_map.59 = f32[896,512]{1,0:T(8,128)} custom-call(s32[896,1]{1,0:T(8,128)} %bitcast.108, bf16[512,16384]{1,0:T(8,128)(2,1)} %em_ref.1), custom_call_target="tpu_custom_call" | custom-call | flops 15032385536 | bytes 18612224 | tf_op jit(solution)/shard_map/pallas_call | solution.py:29
  58.0 6.0 %all-gather.9.cloned.1.call-done = bf16[128,8192]{1,0:T(8,128)(2,1)} async-done(((bf16[128,512]{1,0:T(8,128)(2,1)}), bf16[128,8192]{1,0:T(8,128)(2,1)}) %all-gather.9.cloned.1.call-update) | async-done | bytes 2097168 | tf_op jit(solution)/shard_map/all_gather | solution.py:144
  64.0 2.1 convert_reduce_fusion.6
  66.1 0.1 copy-done.1
  66.2 5.5 %fusion.11 = (f32[128]{0:T(128)S(1)}, bf16[128,512]{1,0:T(8,128)(2,1)}, f32[128,512]{1,0:T(8,128)}) fusion(f32[128,1,512]{2,1,0:T(1,128)} %get-tuple-element.6, f32[896,512]{1,0:T(8,128)} %shard_map.59, f32[128]{0:T(128)S(1)} %convert_reduce_fusion.6, bf16[128,8192]{1,0:T(8,128)(2,1)S(1)} %copy-done.1, bf16[8192,512]{1,0:T(8,128)(2,1)} %shard_map.60), kind=kOutput, calls=%fused_computation.35 | convolution fusion | flops 1074069376 | bytes 11404288 | tf_op jit(solution)/shard_map/dot_general | solution.py:114
  71.7 0.0 all-gather.11.cloned.1.call-update
  71.7 0.0 all-gather.13.cloned.1.call-start
  71.8 40.2 %all-gather.11.cloned.1.call-done = bf16[128,8192]{1,0:T(8,128)(2,1)} async-done(((bf16[128,512]{1,0:T(8,128)(2,1)}), bf16[128,8192]{1,0:T(8,128)(2,1)}) %all-gather.11.cloned.1.call-update) | async-done | bytes 2097168 | tf_op jit(solution)/shard_map/all_gather | solution.py:144
  112.0 2.1 convert_reduce_fusion.5
  114.1 0.1 copy-done.2
  114.3 5.5 %fusion.13 = (f32[128]{0:T(128)S(1)}, bf16[128,512]{1,0:T(8,128)(2,1)}, f32[128,512]{1,0:T(8,128)}) fusion(f32[128,1,512]{2,1,0:T(1,128)S(1)} %get-tuple-element.7, f32[896,512]{1,0:T(8,128)} %shard_map.59, f32[128]{0:T(128)S(1)} %convert_reduce_fusion.5, bf16[128,8192]{1,0:T(8,128)(2,1)S(1)} %copy-done.2, bf16[8192,512]{1,0:T(8,128)(2,1)} %shard_map.60), kind=kOutput, calls=%fused_computation.38 | convolution fusion | flops 1074069376 | bytes 11404288 | tf_op jit(solution)/shard_map/dot_general | solution.py:114
  119.8 0.0 all-gather.13.cloned.1.call-update
  119.8 0.0 all-gather.15.cloned.1.call-start
  119.9 40.2 %all-gather.13.cloned.1.call-done = bf16[128,8192]{1,0:T(8,128)(2,1)} async-done(((bf16[128,512]{1,0:T(8,128)(2,1)}), bf16[128,8192]{1,0:T(8,128)(2,1)}) %all-gather.13.cloned.1.call-update) | async-done | bytes 2097168 | tf_op jit(solution)/shard_map/all_gather | solution.py:144
  160.1 2.1 convert_reduce_fusion.4
  162.2 0.1 copy-done.4
  162.3 5.4 %fusion.15 = (f32[128]{0:T(128)S(1)}, bf16[128,512]{1,0:T(8,128)(2,1)}, f32[128,512]{1,0:T(8,128)S(1)}) fusion(f32[128,1,512]{2,1,0:T(1,128)S(1)} %get-tuple-element.8, f32[896,512]{1,0:T(8,128)} %shard_map.59, f32[128]{0:T(128)S(1)} %convert_reduce_fusion.4, bf16[128,8192]{1,0:T(8,128)(2,1)S(1)} %copy-done.4, bf16[8192,512]{1,0:T(8,128)(2,1)} %shard_map.60), kind=kOutput, calls=%fused_computation.41 | convolution fusion | flops 1074069376 | bytes 11404288 | tf_op jit(solution)/shard_map/dot_general | solution.py:114
  167.8 0.2 all-gather.17.cloned.1.call-start
  168.0 40.0 %all-gather.15.cloned.1.call-done = bf16[128,8192]{1,0:T(8,128)(2,1)} async-done(((bf16[128,512]{1,0:T(8,128)(2,1)}), bf16[128,8192]{1,0:T(8,128)(2,1)}) %all-gather.15.cloned.1.call-update) | async-done | bytes 2097168 | tf_op jit(solution)/shard_map/all_gather | solution.py:144
  208.0 2.1 convert_reduce_fusion.3
  210.1 0.1 copy-done.6
  210.3 5.4 %fusion.17 = (f32[128]{0:T(128)S(1)}, bf16[128,512]{1,0:T(8,128)(2,1)}, f32[128,512]{1,0:T(8,128)S(1)}) fusion(f32[128,1,512]{2,1,0:T(1,128)S(1)} %get-tuple-element.9, f32[896,512]{1,0:T(8,128)} %shard_map.59, f32[128]{0:T(128)S(1)} %convert_reduce_fusion.3, bf16[128,8192]{1,0:T(8,128)(2,1)S(1)} %copy-done.6, bf16[8192,512]{1,0:T(8,128)(2,1)} %shard_map.60), kind=kOutput, calls=%fused_computation.44 | convolution fusion | flops 1074069376 | bytes 11404288 | tf_op jit(solution)/shard_map/dot_general | solution.py:114
  215.7 0.0 all-gather.17.cloned.1.call-update
  215.7 0.0 all-gather.19.cloned.1.call-start
  215.8 40.2 %all-gather.17.cloned.1.call-done = bf16[128,8192]{1,0:T(8,128)(2,1)} async-done(((bf16[128,512]{1,0:T(8,128)(2,1)}), bf16[128,8192]{1,0:T(8,128)(2,1)}) %all-gather.17.cloned.1.call-update) | async-done | bytes 2097168 | tf_op jit(solution)/shard_map/all_gather | solution.py:144
  256.0 2.1 convert_reduce_fusion.2
  258.1 0.1 copy-done.8
  258.2 5.4 %fusion.19 = (f32[128]{0:T(128)S(1)}, bf16[128,512]{1,0:T(8,128)(2,1)}, f32[128,512]{1,0:T(8,128)S(1)}) fusion(f32[128,1,512]{2,1,0:T(1,128)S(1)} %get-tuple-element.10, f32[896,512]{1,0:T(8,128)} %shard_map.59, f32[128]{0:T(128)S(1)} %convert_reduce_fusion.2, bf16[128,8192]{1,0:T(8,128)(2,1)S(1)} %copy-done.8, bf16[8192,512]{1,0:T(8,128)(2,1)} %shard_map.60), kind=kOutput, calls=%fused_computation.47 | convolution fusion | flops 1074069376 | bytes 11404288 | tf_op jit(solution)/shard_map/dot_general | solution.py:114
  263.7 0.0 all-gather.19.cloned.1.call-update
  263.7 0.0 all-gather.21.cloned.1.call-start
  263.7 7.5 %dynamic_update_slice.21 = bf16[896,8192]{1,0:T(8,128)(2,1)} pad(bf16[128,8192]{1,0:T(8,128)(2,1)S(1)} %copy-done.1, bf16[]{:T(256)} %constant.1.clone.1), padding=768_0x0_0 | pad | bytes 16777218 | tf_op jit(solution)/shard_map/dynamic_update_slice | solution.py:148
  271.2 32.8 %all-gather.19.cloned.1.call-done = bf16[128,8192]{1,0:T(8,128)(2,1)} async-done(((bf16[128,512]{1,0:T(8,128)(2,1)}), bf16[128,8192]{1,0:T(8,128)(2,1)}) %all-gather.19.cloned.1.call-update) | async-done | bytes 2097168 | tf_op jit(solution)/shard_map/all_gather | solution.py:144
  304.0 2.1 convert_reduce_fusion.1
  306.1 0.1 copy-done.10
  306.2 5.6 %fusion.21 = (f32[128]{0:T(128)S(1)}, bf16[128,512]{1,0:T(8,128)(2,1)}, f32[128,512]{1,0:T(8,128)S(1)}) fusion(f32[128,1,512]{2,1,0:T(1,128)S(1)} %get-tuple-element.11, f32[896,512]{1,0:T(8,128)} %shard_map.59, f32[128]{0:T(128)S(1)} %convert_reduce_fusion.1, bf16[128,8192]{1,0:T(8,128)(2,1)S(1)} %copy-done.10, bf16[8192,512]{1,0:T(8,128)(2,1)} %shard_map.60), kind=kOutput, calls=%fused_computation.50 | convolution fusion | flops 1074069376 | bytes 11404288 | tf_op jit(solution)/shard_map/dot_general | solution.py:114
  311.8 1.4 constant_dynamic-update-slice_fusion.5
  313.3 0.9 copy-done.5
  314.2 1.5 constant_dynamic-update-slice_fusion.4
  315.7 0.8 copy-done.7
  316.5 1.5 constant_dynamic-update-slice_fusion.3
  318.0 0.9 copy-done.9
  318.9 1.5 constant_dynamic-update-slice_fusion.2
  320.3 0.9 copy-done.11
  321.2 1.4 constant_dynamic-update-slice_fusion.1
  322.7 29.4 %all-gather.21.cloned.1.call-done = bf16[128,8192]{1,0:T(8,128)(2,1)} async-done(((bf16[128,512]{1,0:T(8,128)(2,1)}), bf16[128,8192]{1,0:T(8,128)(2,1)}) %all-gather.21.cloned.1.call-update) | async-done | bytes 2097168 | tf_op jit(solution)/shard_map/all_gather | solution.py:144
  352.1 2.1 convert_reduce_fusion
  354.2 0.1 copy-done
  354.3 4.6 %bitcast_dynamic-update-slice_fusion.6 = (f32[128,8,512]{2,0,1:T(8,128)S(1)}, f32[128,512]{1,0:T(8,128)S(1)}) fusion(f32[128]{0:T(128)S(1)} %convert_reduce_fusion, bf16[128,8192]{1,0:T(8,128)(2,1)S(1)} %copy-done, bf16[8192,512]{1,0:T(8,128)(2,1)} %shard_map.60), kind=kOutput, calls=%fused_computation.60 | convolution fusion | flops 1073807360 | bytes 11010560 | tf_op jit(solution)/shard_map/dot_general | solution.py:114
  359.1 0.8 copy-done.14
  359.9 0.1 copy-done.13
  360.0 2.5 copy.24
  362.6 0.1 fusion.23
  362.7 19.7 %all-gather = f32[2048,7]{0,1:T(8,128)S(1)} all-gather(f32[128,7]{0,1:T(8,128)S(1)} %concatenate.32), channel_id=2, replica_groups=mesh['groups'=2,'state'=16] {'state'}, dimensions={0}, use_global_device_ids=true | all-gather | bytes 60928 | tf_op jit(solution)/shard_map/all_gather | solution.py:156
  382.5 2.6 fusion.2
  385.1 1.5 constant_dynamic-update-slice_fusion
  386.6 19.3 %multiply_multiply_fusion = f32[512,8192]{1,0:T(8,128)} fusion(bf16[512,8192]{1,0:T(8,128)(2,1)} %x_ref.1, bf16[896,512]{1,0:T(8,128)(2,1)S(1)} %bitcast.106, bf16[896,8192]{1,0:T(8,128)(2,1)} %constant_dynamic-update-slice_fusion), kind=kOutput, calls=%fused_computation | convolution fusion | flops 7528775680 | bytes 40763392 | tf_op jit(solution)/shard_map/dot_general | solution.py:161
  (36 shorter events, 0.3 us)
Async XLA Ops:
  7.2 56.8 %all-gather.9.cloned.1.call-start = ((), (), s32[]{:S(2)}) async-start(), calls=%async_computation | async-start | bytes 2228224 | tf_op jit(solution)/shard_map/all_gather | solution.py:144
  7.9 12.1 %copy-start.16 = (s32[128,8]{0,1:T(8,128)S(1)}, s32[128,8]{0,1:T(8,128)}, u32[]{:S(2)}) copy-start(s32[128,8]{0,1:T(8,128)} %param.5) | copy-start | bytes 12292
  19.9 92.1 %all-gather.11.cloned.1.call-start = ((), (), s32[]{:S(2)}) async-start(), calls=%async_computation.1 | async-start | bytes 2228224 | tf_op jit(solution)/shard_map/all_gather | solution.py:144
  21.0 13.2 %copy-start.12 = (f32[128,8,512]{2,1,0:T(8,128)S(1)}, f32[128,8,512]{2,1,0:T(8,128)}, u32[]{:S(2)}) copy-start(f32[128,8,512]{2,1,0:T(8,128)} %param.4) | copy-start | bytes 6291460
  64.0 2.2 copy-start.1
  71.7 88.3 %all-gather.13.cloned.1.call-start = ((), (), s32[]{:S(2)}) async-start(), calls=%async_computation.2 | async-start | bytes 2228224 | tf_op jit(solution)/shard_map/all_gather | solution.py:144
  112.0 2.2 copy-start.2
  119.8 88.2 %all-gather.15.cloned.1.call-start = ((), (), s32[]{:S(2)}) async-start(), calls=%async_computation.3 | async-start | bytes 2228224 | tf_op jit(solution)/shard_map/all_gather | solution.py:144
  160.1 2.2 copy-start.4
  167.8 88.2 %all-gather.17.cloned.1.call-start = ((), (), s32[]{:S(2)}) async-start(), calls=%async_computation.4 | async-start | bytes 2228224 | tf_op jit(solution)/shard_map/all_gather | solution.py:144
  208.0 2.2 copy-start.6
  215.7 88.2 %all-gather.19.cloned.1.call-start = ((), (), s32[]{:S(2)}) async-start(), calls=%async_computation.5 | async-start | bytes 2228224 | tf_op jit(solution)/shard_map/all_gather | solution.py:144
  256.0 2.2 copy-start.8
  263.7 88.4 %all-gather.21.cloned.1.call-start = ((), (), s32[]{:S(2)}) async-start(), calls=%async_computation.6 | async-start | bytes 2228224 | tf_op jit(solution)/shard_map/all_gather | solution.py:144
  304.0 2.2 copy-start.10
  306.2 5.6 %copy-start.3 = (bf16[128,8192]{1,0:T(8,128)(2,1)S(1)}, bf16[128,8192]{1,0:T(8,128)(2,1)}, u32[]{:S(2)}) copy-start(bf16[128,8192]{1,0:T(8,128)(2,1)} %all-gather.11.cloned.1.call-done) | copy-start | bytes 6291460
  311.8 2.3 copy-start.5
  314.2 2.3 copy-start.7
  316.5 2.4 copy-start.9
  318.9 2.4 copy-start.11
  352.1 2.2 copy-start
  358.9 1.0 copy-start.14
  359.0 1.0 copy-start.13
  360.0 2.5 copy-start.15
Sparse Core Ops, SparseCore 0:
  20.1 43.8 all-gather.8
  71.9 40.1 all-gather.10
  119.9 40.1 all-gather.12
  167.9 40.0 all-gather.14
  215.8 40.1 all-gather.16
  263.8 40.1 all-gather.18
  311.9 40.1 all-gather.20

commit v6 on v5

--- a/solution.py
+++ b/solution.py
@@ -110,9 +110,25 @@
     )(x)
 
 
-def backward_step_xla(whole, transition_t, emit_next, fwd):
+def with_row_sums(weighted):
+    b, rows = weighted.shape
+    part = jnp.sum(weighted.astype(jnp.float32), axis=1)
+    hi_f32 = lax.reduce_precision(part, exponent_bits=8, mantissa_bits=7)
+    hi = hi_f32.astype(jnp.bfloat16)
+    lo = (part - hi_f32).astype(jnp.bfloat16)
+    extra = jnp.zeros((8, rows), jnp.bfloat16).at[0, :b].set(hi).at[1, :b].set(lo)
+    return jnp.concatenate([weighted, extra], axis=0)
+
+
+def split_gathered(gathered, b, rows):
+    whole = gathered[:b]
+    hi = gathered[b].reshape(-1, rows)[:, :b].astype(jnp.float32)
+    lo = gathered[b + 1].reshape(-1, rows)[:, :b].astype(jnp.float32)
+    return whole, jnp.sum(hi + lo, axis=0)[:, None]
+
+
+def backward_step_xla(whole, scale_sum, transition_t, emit_next, fwd):
     product = jnp.dot(whole, transition_t, preferred_element_type=jnp.float32)
-    scale_sum = jnp.sum(whole.astype(jnp.float32), axis=1, keepdims=True)
     backward = product / scale_sum
     weighted = (emit_next * backward).astype(jnp.bfloat16)
     norm_part = jnp.sum(fwd * backward, axis=1, keepdims=True)
@@ -140,10 +156,16 @@
     vector_mat = jnp.zeros((last * seq_count, states), jnp.bfloat16)
     scales = []
     norms = []
+    packed = state_rows >= seq_count
     for t in range(step_count - 2, -1, -1):
-        whole = lax.all_gather(weighted, "state", axis=1, tiled=True)
+        if packed:
+            gathered = lax.all_gather(with_row_sums(weighted), "state", axis=1, tiled=True)
+            whole, scale_sum = split_gathered(gathered, seq_count, state_rows)
+        else:
+            whole = lax.all_gather(weighted, "state", axis=1, tiled=True)
+            scale_sum = jnp.sum(whole.astype(jnp.float32), axis=1, keepdims=True)
         backward, weighted, scale_sum, norm_part = backward_step_xla(
-            whole, transition_t, emitted_early[t], forward_probs[:, t, :]
+            whole, scale_sum, transition_t, emitted_early[t], forward_probs[:, t, :]
         )
         vector_mat = lax.dynamic_update_slice(vector_mat, whole, (t * seq_count, 0))
         scales.append(scale_sum)

time: 414 us -> 422 us (1.019)
  other arithmetic: 17.4 us -> 6.91 us
  local copies, waits for them, and re-layouts: 28 us -> 38 us
  matrix products: 68.9 us -> 73.9 us
    reduce_sum x7, other arithmetic: 14.6 us -> 0.15 us  [split_gathered(): return (whole, jnp.sum(hi + lo, axis=0)[:, None])]
    slice x0 -> x9, local copies, waits for them, and re-layouts: none -> 9.44 us  [the longest x7 8.14 us: split_gathered(): hi = gathered[b].reshape(-1, rows)[:, :b].astype(jnp.float32)]
    dot_general x7, matrix products: 37.6 us -> 43.2 us  [backward_step_xla(): product = jnp.dot(whole, transition_t, preferred_element_type=jnp.float32)]
    concatenate x0 -> x7, other arithmetic: none -> 5.56 us  [with_row_sums(): return jnp.concatenate([weighted, extra], axis=0)]
    unnamed x44 -> x58, local copies, waits for them, and re-layouts: 8.96 us -> 7.91 us
where the time goes in v6:
time: 422 us; the launch traced here: 421 us
  waiting for transfers between devices  232 us (55%)
  matrix products  73.9 us (18%)
  local copies, waits for them, and re-layouts  38 us (9%)
  Pallas kernels  35.1 us (8%)
  blocking collectives  19.7 us (5%)
  between operations  14.7 us (3%)
  other arithmetic  6.91 us (2%)
    all_gather x7, waiting for transfers between devices, on_device(): lax.all_gather(with_row_sums(weighted), 'state', axis=1, tiled=True)  232 us
    dot_general x7, matrix products, backward_step_xla(): product = jnp.dot(whole, transition_t, preferred_element_type=jnp.float32)  43.2 us
    pallas_call x1, Pallas kernels, emitted_rows(): pl.pallas_call(_emit_kernel, grid=(vocab // tv,), in_specs=[pl.BlockSpec(...  21.9 us
    all_gather x1, blocking collectives, on_device(): norm_parts = lax.all_gather(partial_norms, 'state', axis=0, tiled=False)  19.7 us
    dot_general x1, matrix products, on_device(): lax.dot_general(share_mat, vector_mat, (((0,), (0,)), ((), ())), preferre...  19.3 us
    dynamic_update_slice x7, local copies, waits for them, and re-layouts, on_device(): vector_mat = lax.dynamic_update_slice(vector_mat, whole, (t * seq_count, 0))  16.4 us
    pallas_call x1, Pallas kernels, transposed(): pl.pallas_call(_transpose_kernel, grid=(cols // tile,), in_specs=[pl.Bloc...  13.2 us
    dot_general x1, matrix products, emitted_rows_xla(): lax.dot_general(onehot, emission, NT, preferred_element_type=jnp.float32)  11.4 us
  transfers between devices with their start and end apart: 7, of which 7 were waited for; matrix products, arithmetic and copies ran while one was open for 4% of the time, Pallas kernels for 8%

profile of v6, /device:TPU:0, one launch (start us, length us, event | category | flops | bytes accessed | tf_op | source)
XLA Modules:
  0.0 420.9 jit_solution(9994963094683093915)
XLA Ops:
  7.2 0.7 slice_bitcast_fusion.1
  7.9 11.4 %convert_reduce_fusion.6 = (f32[128]{0:T(128)S(1)}, bf16[128,512]{1,0:T(8,128)(2,1)S(1)}) fusion(bf16[512,16384]{1,0:T(8,128)(2,1)} %em_ref.1, s32[128]{0:T(128)S(1)} %slice_bitcast_fusion.1), kind=kOutput, calls=%fused_computation.78 | convolution fusion | flops 2149777408 | bytes 16909312 | tf_op jit(solution)/shard_map/dot_general | solution.py:141
  19.4 0.2 scatter.49
  19.6 0.7 pad_maximum_fusion
  20.2 0.0 all-gather.11.cloned.1.call-start
  20.3 1.0 copy.34
  21.3 13.2 %shard_map.60 = bf16[8192,512]{1,0:T(8,128)(2,1)} custom-call(bf16[512,8192]{1,0:T(8,128)(2,1)} %x_ref.1), custom_call_target="tpu_custom_call" | custom-call | tf_op jit(solution)/shard_map/pallas_call | solution.py:104
  34.5 2.0 fusion.68
  36.6 21.9 %shard_map.59 = f32[896,512]{1,0:T(8,128)} custom-call(s32[896,1]{1,0:T(8,128)} %bitcast.122, bf16[512,16384]{1,0:T(8,128)(2,1)} %em_ref.1), custom_call_target="tpu_custom_call" | custom-call | flops 15032385536 | bytes 18612224 | tf_op jit(solution)/shard_map/pallas_call | solution.py:29
  58.5 6.5 %all-gather.9.cloned.1.call-done = bf16[136,8192]{1,0:T(8,128)(2,1)} async-done(((bf16[136,512]{1,0:T(8,128)(2,1)}), bf16[136,8192]{1,0:T(8,128)(2,1)}) %all-gather.9.cloned.1.call-update) | async-done | bytes 2228240 | tf_op jit(solution)/shard_map/all_gather | solution.py:162
  64.9 1.2 slice_reduce_fusion.13
  66.2 6.5 %convert_reduce_fusion.5 = (f32[128]{0:T(128)S(1)}, bf16[128,512]{1,0:T(8,128)(2,1)S(1)}, f32[128]{0:T(128)}, f32[128,512]{1,0:T(8,128)}) fusion(f32[896,512]{1,0:T(8,128)} %shard_map.59, f32[128,1,512]{2,1,0:T(1,128)S(1)} %copy-done.9, f32[128]{0:T(128)S(1)} %add_reduce_fusion.6, bf16[8192,512]{1,0:T(8,128)(2,1)} %shard_map.60, ...), kind=kOutput, calls=%fused_computation.77 | convolution fusion | flops 1074200320 | bytes 11404800 | tf_op jit(solution)/shard_map/dot_general | solution.py:131
  72.7 0.2 scatter.51
  72.9 0.7 pad_maximum_fusion.1
  73.6 40.7 %all-gather.11.cloned.1.call-done = bf16[136,8192]{1,0:T(8,128)(2,1)} async-done(((bf16[136,512]{1,0:T(8,128)(2,1)}), bf16[136,8192]{1,0:T(8,128)(2,1)}) %all-gather.11.cloned.1.call-update) | async-done | bytes 2228240 | tf_op jit(solution)/shard_map/all_gather | solution.py:162
  114.3 1.2 slice_reduce_fusion.11
  115.6 6.5 %convert_reduce_fusion.4 = (f32[128]{0:T(128)S(1)}, bf16[128,512]{1,0:T(8,128)(2,1)S(1)}, f32[128]{0:T(128)}, f32[128,512]{1,0:T(8,128)}) fusion(f32[896,512]{1,0:T(8,128)} %shard_map.59, f32[128,1,512]{2,1,0:T(1,128)S(1)} %copy-done.8, f32[128]{0:T(128)S(1)} %add_reduce_fusion.5, bf16[8192,512]{1,0:T(8,128)(2,1)} %shard_map.60, ...), kind=kOutput, calls=%fused_computation.76 | convolution fusion | flops 1074200320 | bytes 11404800 | tf_op jit(solution)/shard_map/dot_general | solution.py:131
  122.1 0.2 scatter.55
  122.3 0.7 pad_maximum_fusion.2
  122.9 0.2 all-gather.15.cloned.1.call-start
  123.2 40.6 %all-gather.13.cloned.1.call-done = bf16[136,8192]{1,0:T(8,128)(2,1)} async-done(((bf16[136,512]{1,0:T(8,128)(2,1)}), bf16[136,8192]{1,0:T(8,128)(2,1)}) %all-gather.13.cloned.1.call-update) | async-done | bytes 2228240 | tf_op jit(solution)/shard_map/all_gather | solution.py:162
  163.8 1.2 slice_reduce_fusion.9
  165.0 6.5 %convert_reduce_fusion.3 = (f32[128]{0:T(128)S(1)}, bf16[128,512]{1,0:T(8,128)(2,1)S(1)}, f32[128]{0:T(128)}, f32[128,512]{1,0:T(8,128)}) fusion(f32[896,512]{1,0:T(8,128)} %shard_map.59, f32[128,1,512]{2,1,0:T(1,128)S(1)} %get-tuple-element.202, f32[128]{0:T(128)S(1)} %add_reduce_fusion.4, bf16[8192,512]{1,0:T(8,128)(2,1)} %shard_map.60, ...), kind=kOutput, calls=%fused_computation.75 | convolution fusion | flops 1074200320 | bytes 11404800 | tf_op jit(solution)/shard_map/dot_general | solution.py:131
  171.6 0.2 scatter.59
  171.7 0.7 pad_maximum_fusion.3
  172.4 0.0 all-gather.17.cloned.1.call-start
  172.5 40.8 %all-gather.15.cloned.1.call-done = bf16[136,8192]{1,0:T(8,128)(2,1)} async-done(((bf16[136,512]{1,0:T(8,128)(2,1)}), bf16[136,8192]{1,0:T(8,128)(2,1)}) %all-gather.15.cloned.1.call-update) | async-done | bytes 2228240 | tf_op jit(solution)/shard_map/all_gather | solution.py:162
  213.3 1.2 slice_reduce_fusion.7
  214.5 5.9 %convert_reduce_fusion.2 = (f32[128]{0:T(128)S(1)}, bf16[128,512]{1,0:T(8,128)(2,1)S(1)}, f32[128]{0:T(128)}, f32[128,512]{1,0:T(8,128)S(1)}) fusion(f32[896,512]{1,0:T(8,128)} %shard_map.59, f32[128,1,512]{2,1,0:T(1,128)S(1)} %get-tuple-element.203, f32[128]{0:T(128)S(1)} %add_reduce_fusion.3, bf16[8192,512]{1,0:T(8,128)(2,1)} %shard_map.60, ...), kind=kOutput, calls=%fused_computation.74 | convolution fusion | flops 1074200320 | bytes 11404800 | tf_op jit(solution)/shard_map/dot_general | solution.py:131
  220.4 0.2 scatter.61
  220.6 0.7 pad_maximum_fusion.4
  221.3 40.8 %all-gather.17.cloned.1.call-done = bf16[136,8192]{1,0:T(8,128)(2,1)} async-done(((bf16[136,512]{1,0:T(8,128)(2,1)}), bf16[136,8192]{1,0:T(8,128)(2,1)}) %all-gather.17.cloned.1.call-update) | async-done | bytes 2228240 | tf_op jit(solution)/shard_map/all_gather | solution.py:162
  262.1 1.2 slice_reduce_fusion.5
  263.4 5.9 %convert_reduce_fusion.1 = (f32[128]{0:T(128)S(1)}, bf16[128,512]{1,0:T(8,128)(2,1)S(1)}, f32[128]{0:T(128)}, f32[128,512]{1,0:T(8,128)S(1)}) fusion(f32[896,512]{1,0:T(8,128)} %shard_map.59, f32[128,1,512]{2,1,0:T(1,128)S(1)} %get-tuple-element.204, f32[128]{0:T(128)S(1)} %add_reduce_fusion.2, bf16[8192,512]{1,0:T(8,128)(2,1)} %shard_map.60, ...), kind=kOutput, calls=%fused_computation.73 | convolution fusion | flops 1074200320 | bytes 11404800 | tf_op jit(solution)/shard_map/dot_general | solution.py:131
  269.3 0.2 scatter.65
  269.5 0.7 pad_maximum_fusion.5
  270.2 0.3 all-gather.21.cloned.1.call-start
  270.4 1.3 slice-done
  271.7 7.5 %dynamic_update_slice.21 = bf16[896,8192]{1,0:T(8,128)(2,1)} pad(bf16[128,8192]{1,0:T(8,128)(2,1)S(1)} %slice-done, bf16[]{:T(256)} %constant.281.clone.1), padding=768_0x0_0 | pad | bytes 16777218 | tf_op jit(solution)/shard_map/dynamic_update_slice | solution.py:170
  279.2 1.4 slice_dynamic-update-slice_fusion.5
  280.7 0.9 copy-done.4
  281.6 1.5 slice_dynamic-update-slice_fusion.4
  283.1 27.8 %all-gather.19.cloned.1.call-done = bf16[136,8192]{1,0:T(8,128)(2,1)} async-done(((bf16[136,512]{1,0:T(8,128)(2,1)}), bf16[136,8192]{1,0:T(8,128)(2,1)}) %all-gather.19.cloned.1.call-update) | async-done | bytes 2228240 | tf_op jit(solution)/shard_map/all_gather | solution.py:162
  311.0 1.2 slice_reduce_fusion.3
  312.2 6.6 %convert_reduce_fusion = (f32[128]{0:T(128)S(1)}, bf16[128,512]{1,0:T(8,128)(2,1)}, f32[128]{0:T(128)}, f32[128,512]{1,0:T(8,128)S(1)}) fusion(f32[896,512]{1,0:T(8,128)} %shard_map.59, f32[128,1,512]{2,1,0:T(1,128)S(1)} %get-tuple-element.205, f32[128]{0:T(128)S(1)} %add_reduce_fusion.1, bf16[8192,512]{1,0:T(8,128)(2,1)} %shard_map.60, ...), kind=kOutput, calls=%fused_computation.72 | convolution fusion | flops 1074200320 | bytes 11404800 | tf_op jit(solution)/shard_map/dot_general | solution.py:131
  318.8 0.2 scatter.69
  319.0 1.6 pad_maximum_fusion.6
  320.6 1.5 slice_dynamic-update-slice_fusion.3
  322.1 0.9 copy-done.5
  323.0 1.5 slice_dynamic-update-slice_fusion.2
  324.5 0.9 copy-done.7
  325.4 1.4 slice_dynamic-update-slice_fusion.1
  326.8 34.6 %all-gather.21.cloned.1.call-done = bf16[136,8192]{1,0:T(8,128)(2,1)} async-done(((bf16[136,512]{1,0:T(8,128)(2,1)}), bf16[136,8192]{1,0:T(8,128)(2,1)}) %all-gather.21.cloned.1.call-update) | async-done | bytes 2228240 | tf_op jit(solution)/shard_map/all_gather | solution.py:162
  361.4 1.2 slice_reduce_fusion.1
  362.7 5.3 %bitcast_dynamic-update-slice_fusion.6 = (f32[128,8,512]{2,0,1:T(8,128)S(1)}, f32[128,512]{1,0:T(8,128)S(1)}) fusion(f32[128]{0:T(128)S(1)} %add_reduce_fusion, bf16[8192,512]{1,0:T(8,128)(2,1)} %shard_map.60, bf16[136,8192]{1,0:T(8,128)(2,1)} %all-gather.21.cloned.1.call-done), kind=kOutput, calls=%fused_computation.71 | convolution fusion | flops 1073807360 | bytes 11010560 | tf_op jit(solution)/shard_map/dot_general | solution.py:131
  368.2 0.8 copy-done.11
  369.0 0.1 copy-done.10
  369.2 2.5 copy.24
  371.7 0.1 fusion.53
  371.9 19.7 %all-gather = f32[2048,7]{0,1:T(8,128)S(1)} all-gather(f32[128,7]{0,1:T(8,128)S(1)} %concatenate.88), channel_id=2, replica_groups=mesh['groups'=2,'state'=16] {'state'}, dimensions={0}, use_global_device_ids=true | all-gather | bytes 60928 | tf_op jit(solution)/shard_map/all_gather | solution.py:178
  391.7 1.0 fusion.14
  392.7 0.6 copy-done.6
  393.3 1.5 slice_dynamic-update-slice_fusion
  394.8 19.3 %multiply_multiply_fusion = f32[512,8192]{1,0:T(8,128)} fusion(bf16[512,8192]{1,0:T(8,128)(2,1)} %x_ref.1, bf16[896,512]{1,0:T(8,128)(2,1)S(1)} %bitcast.120, bf16[896,8192]{1,0:T(8,128)(2,1)} %slice_dynamic-update-slice_fusion), kind=kOutput, calls=%fused_computation | convolution fusion | flops 7528775680 | bytes 40763392 | tf_op jit(solution)/shard_map/dot_general | solution.py:183
  (101 shorter events, 1.1 us)
Async XLA Ops:
  7.2 57.8 %all-gather.9.cloned.1.call-start = ((), (), s32[]{:S(2)}) async-start(), calls=%async_computation | async-start | bytes 2367488 | tf_op jit(solution)/shard_map/all_gather | solution.py:162
  7.9 12.4 %copy-start.13 = (s32[128,8]{0,1:T(8,128)S(1)}, s32[128,8]{0,1:T(8,128)}, u32[]{:S(2)}) copy-start(s32[128,8]{0,1:T(8,128)} %param.33) | copy-start | bytes 12292
  20.2 94.1 %all-gather.11.cloned.1.call-start = ((), (), s32[]{:S(2)}) async-start(), calls=%async_computation.1 | async-start | bytes 2367488 | tf_op jit(solution)/shard_map/all_gather | solution.py:162
  21.3 13.2 %copy-start = (f32[128,8,512]{2,1,0:T(8,128)S(1)}, f32[128,8,512]{2,1,0:T(8,128)}, u32[]{:S(2)}) copy-start(f32[128,8,512]{2,1,0:T(8,128)} %param.32) | copy-start | bytes 6291460
  36.6 29.6 %copy-start.9 = (f32[128,1,512]{2,1,0:T(1,128)S(1)}, f32[128,1,512]{2,1,0:T(1,128)}, u32[]{:S(2)}) copy-start(f32[128,1,512]{2,1,0:T(1,128)} %get-tuple-element.200) | copy-start | bytes 786436
  66.2 49.4 %copy-start.8 = (f32[128,1,512]{2,1,0:T(1,128)S(1)}, f32[128,1,512]{2,1,0:T(1,128)}, u32[]{:S(2)}) copy-start(f32[128,1,512]{2,1,0:T(1,128)} %get-tuple-element.201) | copy-start | bytes 786436
  73.6 90.2 %all-gather.13.cloned.1.call-start = ((), (), s32[]{:S(2)}) async-start(), calls=%async_computation.2 | async-start | bytes 2367488 | tf_op jit(solution)/shard_map/all_gather | solution.py:162
  122.9 90.3 %all-gather.15.cloned.1.call-start = ((), (), s32[]{:S(2)}) async-start(), calls=%async_computation.3 | async-start | bytes 2367488 | tf_op jit(solution)/shard_map/all_gather | solution.py:162
  172.4 89.7 %all-gather.17.cloned.1.call-start = ((), (), s32[]{:S(2)}) async-start(), calls=%async_computation.4 | async-start | bytes 2367488 | tf_op jit(solution)/shard_map/all_gather | solution.py:162
  221.3 89.7 %all-gather.19.cloned.1.call-start = ((), (), s32[]{:S(2)}) async-start(), calls=%async_computation.5 | async-start | bytes 2367488 | tf_op jit(solution)/shard_map/all_gather | solution.py:162
  263.4 5.9 %copy-start.14 = (f32[128]{0:T(128)}, f32[128]{0:T(128)S(1)}, u32[]{:S(2)}) copy-start(f32[128]{0:T(128)S(1)} %add_reduce_fusion.2) | copy-start | bytes 1540
  270.1 1.6 slice-start
  270.2 91.3 %all-gather.21.cloned.1.call-start = ((), (), s32[]{:S(2)}) async-start(), calls=%async_computation.6 | async-start | bytes 2367488 | tf_op jit(solution)/shard_map/all_gather | solution.py:162
  271.7 7.5 %copy-start.2 = (bf16[136,8192]{1,0:T(8,128)(2,1)S(1)}, bf16[136,8192]{1,0:T(8,128)(2,1)}, u32[]{:S(2)}) copy-start(bf16[136,8192]{1,0:T(8,128)(2,1)} %all-gather.11.cloned.1.call-done) | copy-start | bytes 6684676
  279.2 2.4 copy-start.4
  312.2 6.6 %copy-start.16 = (f32[128]{0:T(128)}, f32[128]{0:T(128)S(1)}, u32[]{:S(2)}) copy-start(f32[128]{0:T(128)S(1)} %add_reduce_fusion.1) | copy-start | bytes 1540
  312.2 8.4 %copy-start.3 = (bf16[136,8192]{1,0:T(8,128)(2,1)S(1)}, bf16[136,8192]{1,0:T(8,128)(2,1)}, u32[]{:S(2)}) copy-start(bf16[136,8192]{1,0:T(8,128)(2,1)} %all-gather.15.cloned.1.call-done) | copy-start | bytes 6684676
  320.6 2.4 copy-start.5
  323.0 2.4 copy-start.7
  362.7 5.4 %copy-start.12 = (f32[128,512]{1,0:T(8,128)S(1)}, f32[128,512]{1,0:T(8,128)}, u32[]{:S(2)}) copy-start(f32[128,512]{1,0:T(8,128)} %get-tuple-element.231) | copy-start | bytes 786436
  368.0 1.0 copy-start.11
  368.0 1.0 copy-start.10
  369.1 2.7 copy-start.18
  369.1 2.7 copy-start.19
  369.1 2.7 copy-start.20
  369.1 2.7 copy-start.21
  369.1 2.7 copy-start.22
  369.1 2.7 copy-start.23
  369.2 22.5 %copy-start.15 = (f32[128]{0:T(128)S(1)}, f32[128]{0:T(128)}, u32[]{:S(2)}) copy-start(f32[128]{0:T(128)} %copy-done.14) | copy-start | bytes 1540
  369.2 22.5 %copy-start.17 = (f32[128]{0:T(128)S(1)}, f32[128]{0:T(128)}, u32[]{:S(2)}) copy-start(f32[128]{0:T(128)} %copy-done.16) | copy-start | bytes 1540
  369.2 22.5 %copy-start.1 = (f32[128,8,512]{2,1,0:T(8,128)S(1)}, f32[128,8,512]{2,1,0:T(8,128)}, u32[]{:S(2)}) copy-start(f32[128,8,512]{2,1,0:T(8,128)} %param.32) | copy-start | bytes 6291460
  391.7 1.6 copy-start.6
Sparse Core Ops, SparseCore 0:
  20.4 44.5 all-gather.8
  73.7 40.5 all-gather.10
  123.1 40.6 all-gather.12
  172.5 40.6 all-gather.14
  221.4 40.6 all-gather.16
  270.3 40.6 all-gather.18
  320.7 40.6 all-gather.20

commit v7 on v5

--- a/solution.py
+++ b/solution.py
@@ -96,24 +96,27 @@
 
 
 def _transpose_kernel(x_ref, o_ref):
-    o_ref[...] = x_ref[...].T
+    rows = x_ref.shape[0]
+    o_ref[:, :rows] = x_ref[...].T
+    o_ref[:, rows:] = jnp.ones((o_ref.shape[0], o_ref.shape[1] - rows), o_ref.dtype)
 
 
-def transposed(x, tile=512):
+def transposed_with_ones(x, tile=512):
     rows, cols = x.shape
     return pl.pallas_call(
         _transpose_kernel,
         grid=(cols // tile,),
         in_specs=[pl.BlockSpec((rows, tile), lambda j: (0, j))],
-        out_specs=pl.BlockSpec((tile, rows), lambda j: (j, 0)),
-        out_shape=jax.ShapeDtypeStruct((cols, rows), x.dtype),
+        out_specs=pl.BlockSpec((tile, rows + 128), lambda j: (j, 0)),
+        out_shape=jax.ShapeDtypeStruct((cols, rows + 128), x.dtype),
     )(x)
 
 
 def backward_step_xla(whole, transition_t, emit_next, fwd):
+    rows = fwd.shape[1]
     product = jnp.dot(whole, transition_t, preferred_element_type=jnp.float32)
-    scale_sum = jnp.sum(whole.astype(jnp.float32), axis=1, keepdims=True)
-    backward = product / scale_sum
+    scale_sum = product[:, rows:rows + 1]
+    backward = product[:, :rows] / scale_sum
     weighted = (emit_next * backward).astype(jnp.bfloat16)
     norm_part = jnp.sum(fwd * backward, axis=1, keepdims=True)
     return backward, weighted, scale_sum, norm_part
@@ -135,7 +138,7 @@
     early_ids = token_ids[:, :last].T.reshape(-1)
     emitted_early = emitted_rows(early_ids, emission).reshape(last, seq_count, state_rows)
     weighted = emitted_last.astype(jnp.bfloat16)
-    transition_t = transposed(transition)
+    transition_t = transposed_with_ones(transition)
     backs = [jnp.ones((seq_count, state_rows), jnp.float32)]
     vector_mat = jnp.zeros((last * seq_count, states), jnp.bfloat16)
     scales = []

time: 414 us -> 421 us (1.017)
  matrix products: 68.9 us -> 76.6 us
    reduce_sum x7 -> x0, other arithmetic: 14.6 us -> none  [backward_step_xla(): scale_sum = jnp.sum(whole.astype(jnp.float32), axis=1, keepdims=True)]
    reduce_sum x1 -> x7, other arithmetic: 0.11 us -> 10 us  [backward_step_xla(): norm_part = jnp.sum(fwd * backward, axis=1, keepdims=True)]
    dot_general x7, matrix products: 37.6 us -> 45.3 us  [backward_step_xla(): product = jnp.dot(whole, transition_t, preferred_element_type=jnp.float32)]
    unnamed x44 -> x64, local copies, waits for them, and re-layouts: 8.96 us -> 3.85 us
    slice x0 -> x14, local copies, waits for them, and re-layouts: none -> 5.07 us  [backward_step_xla(): scale_sum = product[:, rows:rows + 1]]
  transfers between devices with their start and end apart: 7 -> 7, of which waited for: 7 -> 7; matrix products, arithmetic and copies ran while one was open for 4% -> 6% of each run, Pallas kernels for 8% -> 8%
where the time goes in v7:
time: 421 us; the launch traced here: 420 us
  waiting for transfers between devices  226 us (54%)
  matrix products  76.6 us (18%)
  Pallas kernels  35.4 us (8%)
  local copies, waits for them, and re-layouts  31.8 us (8%)
  blocking collectives  19.7 us (5%)
  other arithmetic  15.4 us (4%)
  between operations  14.5 us (3%)
    all_gather x7, waiting for transfers between devices, on_device(): whole = lax.all_gather(weighted, 'state', axis=1, tiled=True)  226 us
    dot_general x7, matrix products, backward_step_xla(): product = jnp.dot(whole, transition_t, preferred_element_type=jnp.float32)  45.3 us
    pallas_call x1, Pallas kernels, emitted_rows(): pl.pallas_call(_emit_kernel, grid=(vocab // tv,), in_specs=[pl.BlockSpec(...  21.8 us
    dynamic_update_slice x7, local copies, waits for them, and re-layouts, on_device(): vector_mat = lax.dynamic_update_slice(vector_mat, whole, (t * seq_count, 0))  20 us
    all_gather x1, blocking collectives, on_device(): norm_parts = lax.all_gather(partial_norms, 'state', axis=0, tiled=False)  19.7 us
    dot_general x1, matrix products, on_device(): lax.dot_general(share_mat, vector_mat, (((0,), (0,)), ((), ())), preferre...  19.3 us
    pallas_call x1, Pallas kernels, transposed_with_ones(): pl.pallas_call(_transpose_kernel, grid=(cols // tile,), in_specs=[pl.Bloc...  13.5 us
    dot_general x1, matrix products, emitted_rows_xla(): lax.dot_general(onehot, emission, NT, preferred_element_type=jnp.float32)  12 us
  transfers between devices with their start and end apart: 7, of which 7 were waited for; matrix products, arithmetic and copies ran while one was open for 6% of the time, Pallas kernels for 8%

profile of v7, /device:TPU:0, one launch (start us, length us, event | category | flops | bytes accessed | tf_op | source)
XLA Modules:
  0.0 419.9 jit_solution(12737993211908730697)
XLA Ops:
  7.2 0.7 slice_bitcast_fusion.1
  7.9 12.0 %fusion.3 = bf16[128,512]{1,0:T(8,128)(2,1)} fusion(bf16[512,16384]{1,0:T(8,128)(2,1)} %em_ref.1, s32[128]{0:T(128)S(1)} %slice_bitcast_fusion.1), kind=kOutput, calls=%fused_computation.6 | convolution fusion | flops 2149646336 | bytes 16908800 | tf_op jit(solution)/shard_map/dot_general | solution.py:128
  20.0 1.0 copy.51
  21.1 13.5 %shard_map.60 = bf16[8192,640]{1,0:T(8,128)(2,1)} custom-call(bf16[512,8192]{1,0:T(8,128)(2,1)} %x_ref.1), custom_call_target="tpu_custom_call" | custom-call | tf_op jit(solution)/shard_map/pallas_call | solution.py:106
  34.6 2.1 fusion.24
  36.7 21.8 %shard_map.59 = f32[896,512]{1,0:T(8,128)} custom-call(s32[896,1]{1,0:T(8,128)} %bitcast.101, bf16[512,16384]{1,0:T(8,128)(2,1)} %em_ref.1), custom_call_target="tpu_custom_call" | custom-call | flops 15032385536 | bytes 18612224 | tf_op jit(solution)/shard_map/pallas_call | solution.py:29
  58.6 5.4 %all-gather.9.cloned.1.call-done = bf16[128,8192]{1,0:T(8,128)(2,1)} async-done(((bf16[128,512]{1,0:T(8,128)(2,1)}), bf16[128,8192]{1,0:T(8,128)(2,1)}) %all-gather.9.cloned.1.call-update) | async-done | bytes 2097168 | tf_op jit(solution)/shard_map/all_gather | solution.py:147
  64.0 6.4 %fusion.32 = f32[128,640]{1,0:T(8,128)S(1)} fusion(bf16[128,8192]{1,0:T(8,128)(2,1)} %all-gather.9.cloned.1.call-done, bf16[8192,640]{1,0:T(8,128)(2,1)} %shard_map.60), kind=kOutput, calls=%fused_computation.80 | convolution fusion | flops 1342177280 | bytes 12910592 | tf_op jit(solution)/shard_map/dot_general | solution.py:117
  70.4 0.1 fusion.25
  70.6 1.3 fusion.11
  71.9 0.0 all-gather.13.cloned.1.call-start
  72.0 40.2 %all-gather.11.cloned.1.call-done = bf16[128,8192]{1,0:T(8,128)(2,1)} async-done(((bf16[128,512]{1,0:T(8,128)(2,1)}), bf16[128,8192]{1,0:T(8,128)(2,1)}) %all-gather.11.cloned.1.call-update) | async-done | bytes 2097168 | tf_op jit(solution)/shard_map/all_gather | solution.py:147
  112.2 6.4 %fusion.33 = f32[128,640]{1,0:T(8,128)S(1)} fusion(bf16[128,8192]{1,0:T(8,128)(2,1)} %all-gather.11.cloned.1.call-done, bf16[8192,640]{1,0:T(8,128)(2,1)} %shard_map.60), kind=kOutput, calls=%fused_computation.81 | convolution fusion | flops 1342177280 | bytes 12910592 | tf_op jit(solution)/shard_map/dot_general | solution.py:117
  118.6 0.1 fusion.26
  118.7 1.4 fusion.13
  120.1 0.2 all-gather.15.cloned.1.call-start
  120.4 40.0 %all-gather.13.cloned.1.call-done = bf16[128,8192]{1,0:T(8,128)(2,1)} async-done(((bf16[128,512]{1,0:T(8,128)(2,1)}), bf16[128,8192]{1,0:T(8,128)(2,1)}) %all-gather.13.cloned.1.call-update) | async-done | bytes 2097168 | tf_op jit(solution)/shard_map/all_gather | solution.py:147
  160.4 6.4 %fusion.34 = f32[128,640]{1,0:T(8,128)S(1)} fusion(bf16[128,8192]{1,0:T(8,128)(2,1)} %all-gather.13.cloned.1.call-done, bf16[8192,640]{1,0:T(8,128)(2,1)} %shard_map.60), kind=kOutput, calls=%fused_computation.82 | convolution fusion | flops 1342177280 | bytes 12910592 | tf_op jit(solution)/shard_map/dot_general | solution.py:117
  166.8 0.6 fusion.27
  167.5 1.3 fusion.15
  168.8 40.2 %all-gather.15.cloned.1.call-done = bf16[128,8192]{1,0:T(8,128)(2,1)} async-done(((bf16[128,512]{1,0:T(8,128)(2,1)}), bf16[128,8192]{1,0:T(8,128)(2,1)}) %all-gather.15.cloned.1.call-update) | async-done | bytes 2097168 | tf_op jit(solution)/shard_map/all_gather | solution.py:147
  209.0 6.4 %fusion.35 = f32[128,640]{1,0:T(8,128)S(1)} fusion(bf16[128,8192]{1,0:T(8,128)(2,1)} %all-gather.15.cloned.1.call-done, bf16[8192,640]{1,0:T(8,128)(2,1)} %shard_map.60), kind=kOutput, calls=%fused_computation.83 | convolution fusion | flops 1342177280 | bytes 12910592 | tf_op jit(solution)/shard_map/dot_general | solution.py:117
  215.5 0.6 fusion.28
  216.1 1.3 fusion.17
  217.4 40.2 %all-gather.17.cloned.1.call-done = bf16[128,8192]{1,0:T(8,128)(2,1)} async-done(((bf16[128,512]{1,0:T(8,128)(2,1)}), bf16[128,8192]{1,0:T(8,128)(2,1)}) %all-gather.17.cloned.1.call-update) | async-done | bytes 2097168 | tf_op jit(solution)/shard_map/all_gather | solution.py:147
  257.6 6.6 %fusion.36 = f32[128,640]{1,0:T(8,128)S(1)} fusion(bf16[128,8192]{1,0:T(8,128)(2,1)} %all-gather.17.cloned.1.call-done, bf16[8192,640]{1,0:T(8,128)(2,1)} %shard_map.60), kind=kOutput, calls=%fused_computation.84 | convolution fusion | flops 1342177280 | bytes 12910592 | tf_op jit(solution)/shard_map/dot_general | solution.py:117
  264.2 0.7 fusion.29
  264.9 0.1 copy-done.6
  265.0 2.3 fusion.19
  267.3 0.0 all-gather.21.cloned.1.call-start
  267.4 0.6 copy.33
  268.0 7.4 %dynamic_update_slice.21 = bf16[896,8192]{1,0:T(8,128)(2,1)} pad(bf16[128,8192]{1,0:T(8,128)(2,1)S(1)} %copy-done, bf16[]{:T(256)} %constant.1.clone.1), padding=768_0x0_0 | pad | bytes 16777218 | tf_op jit(solution)/shard_map/dynamic_update_slice | solution.py:151
  275.4 32.2 %all-gather.19.cloned.1.call-done = bf16[128,8192]{1,0:T(8,128)(2,1)} async-done(((bf16[128,512]{1,0:T(8,128)(2,1)}), bf16[128,8192]{1,0:T(8,128)(2,1)}) %all-gather.19.cloned.1.call-update) | async-done | bytes 2097168 | tf_op jit(solution)/shard_map/all_gather | solution.py:147
  307.6 6.6 %fusion.37 = f32[128,640]{1,0:T(8,128)S(1)} fusion(bf16[128,8192]{1,0:T(8,128)(2,1)} %all-gather.19.cloned.1.call-done, bf16[8192,640]{1,0:T(8,128)(2,1)} %shard_map.60), kind=kOutput, calls=%fused_computation.85 | convolution fusion | flops 1342177280 | bytes 12910592 | tf_op jit(solution)/shard_map/dot_general | solution.py:117
  314.2 0.7 fusion.30
  314.9 0.1 copy-done.7
  314.9 2.3 fusion.21
  317.3 1.5 constant_dynamic-update-slice_fusion.5
  318.8 0.6 copy.32
  319.4 0.7 copy.31
  320.1 3.2 constant_dynamic-update-slice_fusion.4
  323.3 0.1 copy.30
  323.4 1.5 constant_dynamic-update-slice_fusion.3
  324.9 0.1 copy.29
  325.0 3.3 constant_dynamic-update-slice_fusion.2
  328.3 0.1 copy.28
  328.4 1.5 constant_dynamic-update-slice_fusion.1
  329.9 27.6 %all-gather.21.cloned.1.call-done = bf16[128,8192]{1,0:T(8,128)(2,1)} async-done(((bf16[128,512]{1,0:T(8,128)(2,1)}), bf16[128,8192]{1,0:T(8,128)(2,1)}) %all-gather.21.cloned.1.call-update) | async-done | bytes 2097168 | tf_op jit(solution)/shard_map/all_gather | solution.py:147
  357.5 6.5 %fusion.38 = f32[128,640]{1,0:T(8,128)S(1)} fusion(bf16[128,8192]{1,0:T(8,128)(2,1)} %all-gather.21.cloned.1.call-done, bf16[8192,640]{1,0:T(8,128)(2,1)} %shard_map.60), kind=kOutput, calls=%fused_computation.86 | convolution fusion | flops 1342177280 | bytes 12910592 | tf_op jit(solution)/shard_map/dot_general | solution.py:117
  364.0 0.1 fusion.31
  364.1 0.1 bitcast_dynamic-update-slice_fusion.6
  364.2 0.2 fusion.23
  364.4 0.1 copy.27
  364.6 19.7 %all-gather = f32[2048,7]{0,1:T(8,128)S(1)} all-gather(f32[128,7]{0,1:T(8,128)S(1)} %concatenate.11), channel_id=2, replica_groups=mesh['groups'=2,'state'=16] {'state'}, dimensions={0}, use_global_device_ids=true | all-gather | bytes 60928 | tf_op jit(solution)/shard_map/all_gather | solution.py:159
  384.3 1.0 bitcast_dynamic-update-slice_fusion.5
  385.4 1.0 bitcast_dynamic-update-slice_fusion.4
  386.4 0.1 bitcast_dynamic-update-slice_fusion.3
  386.5 0.1 bitcast_dynamic-update-slice_fusion.2
  386.6 0.1 bitcast_dynamic-update-slice_fusion.1
  386.7 0.1 bitcast_dynamic-update-slice_fusion
  386.9 2.5 copy.41
  389.5 2.8 fusion.2
  392.2 1.5 constant_dynamic-update-slice_fusion
  393.7 19.3 %multiply_multiply_fusion = f32[512,8192]{1,0:T(8,128)} fusion(bf16[512,8192]{1,0:T(8,128)(2,1)} %x_ref.1, bf16[896,512]{1,0:T(8,128)(2,1)S(1)} %bitcast.99, bf16[896,8192]{1,0:T(8,128)(2,1)} %constant_dynamic-update-slice_fusion), kind=kOutput, calls=%fused_computation | convolution fusion | flops 7528775680 | bytes 40763392 | tf_op jit(solution)/shard_map/dot_general | solution.py:164
  (76 shorter events, 0.5 us)
Async XLA Ops:
  7.2 56.8 %all-gather.9.cloned.1.call-start = ((), (), s32[]{:S(2)}) async-start(), calls=%async_computation | async-start | bytes 2228224 | tf_op jit(solution)/shard_map/all_gather | solution.py:147
  7.9 12.1 %copy-start.20 = (s32[128,8]{0,1:T(8,128)S(1)}, s32[128,8]{0,1:T(8,128)}, u32[]{:S(2)}) copy-start(s32[128,8]{0,1:T(8,128)} %param.5) | copy-start | bytes 12292
  20.0 92.3 %all-gather.11.cloned.1.call-start = ((), (), s32[]{:S(2)}) async-start(), calls=%async_computation.1 | async-start | bytes 2228224 | tf_op jit(solution)/shard_map/all_gather | solution.py:147
  21.1 13.5 %copy-start.5 = (f32[128,8,512]{2,1,0:T(8,128)S(1)}, f32[128,8,512]{2,1,0:T(8,128)}, u32[]{:S(2)}) copy-start(f32[128,8,512]{2,1,0:T(8,128)} %param.4) | copy-start | bytes 6291460
  58.6 12.0 %copy-start.8 = (f32[896,512]{1,0:T(8,128)S(1)}, f32[896,512]{1,0:T(8,128)}, u32[]{:S(2)}) copy-start(f32[896,512]{1,0:T(8,128)} %shard_map.59) | copy-start | bytes 5505028
  71.9 88.5 %all-gather.13.cloned.1.call-start = ((), (), s32[]{:S(2)}) async-start(), calls=%async_computation.2 | async-start | bytes 2228224 | tf_op jit(solution)/shard_map/all_gather | solution.py:147
  120.1 88.9 %all-gather.15.cloned.1.call-start = ((), (), s32[]{:S(2)}) async-start(), calls=%async_computation.3 | async-start | bytes 2228224 | tf_op jit(solution)/shard_map/all_gather | solution.py:147
  168.8 47.3 %copy-start.11 = (f32[128,1,512]{2,1,0:T(1,128)S(1)}, f32[128,1,512]{2,1,0:T(1,128)}, u32[]{:S(2)}) copy-start(f32[128,1,512]{2,1,0:T(1,128)} %get-tuple-element.11) | copy-start | bytes 786436
  168.8 88.9 %all-gather.17.cloned.1.call-start = ((), (), s32[]{:S(2)}) async-start(), calls=%async_computation.4 | async-start | bytes 2228224 | tf_op jit(solution)/shard_map/all_gather | solution.py:147
  217.4 90.2 %all-gather.19.cloned.1.call-start = ((), (), s32[]{:S(2)}) async-start(), calls=%async_computation.5 | async-start | bytes 2228224 | tf_op jit(solution)/shard_map/all_gather | solution.py:147
  257.6 10.4 %copy-start = (bf16[128,8192]{1,0:T(8,128)(2,1)S(1)}, bf16[128,8192]{1,0:T(8,128)(2,1)}, u32[]{:S(2)}) copy-start(bf16[128,8192]{1,0:T(8,128)(2,1)} %all-gather.9.cloned.1.call-done) | copy-start | bytes 6291460
  264.2 0.8 copy-start.6
  264.9 2.4 copy-start.16
  267.3 90.2 %all-gather.21.cloned.1.call-start = ((), (), s32[]{:S(2)}) async-start(), calls=%async_computation.6 | async-start | bytes 2228224 | tf_op jit(solution)/shard_map/all_gather | solution.py:147
  307.6 7.3 %copy-start.10 = (f32[128,1,512]{2,1,0:T(1,128)S(1)}, f32[128,1,512]{2,1,0:T(1,128)}, u32[]{:S(2)}) copy-start(f32[128,1,512]{2,1,0:T(1,128)} %get-tuple-element.13) | copy-start | bytes 786436
  307.6 9.7 %copy-start.1 = (bf16[128,8192]{1,0:T(8,128)(2,1)S(1)}, bf16[128,8192]{1,0:T(8,128)(2,1)}, u32[]{:S(2)}) copy-start(bf16[128,8192]{1,0:T(8,128)(2,1)} %all-gather.11.cloned.1.call-done) | copy-start | bytes 6291460
  314.2 0.8 copy-start.7
  314.9 2.4 copy-start.18
  317.3 2.1 copy-start.12
  320.1 3.2 copy-start.13
  320.1 3.3 copy-start.3
  323.4 1.5 copy-start.14
  325.0 3.3 copy-start.15
  325.0 3.4 copy-start.4
  329.9 34.6 %copy-start.21 = (f32[128]{0:T(128)S(1)}, f32[128]{0:T(128)}, u32[]{:S(2)}) copy-start(f32[128]{0:T(128)} %get-tuple-element.15) | copy-start | bytes 1540
  329.9 34.6 %copy-start.22 = (f32[128]{0:T(128)S(1)}, f32[128]{0:T(128)}, u32[]{:S(2)}) copy-start(f32[128]{0:T(128)} %get-tuple-element.17) | copy-start | bytes 1540
  329.9 34.6 %copy-start.23 = (f32[128]{0:T(128)S(1)}, f32[128]{0:T(128)}, u32[]{:S(2)}) copy-start(f32[128]{0:T(128)} %get-tuple-element.19) | copy-start | bytes 1540
  329.9 34.6 %copy-start.25 = (f32[128]{0:T(128)S(1)}, f32[128]{0:T(128)}, u32[]{:S(2)}) copy-start(f32[128]{0:T(128)} %get-tuple-element.21) | copy-start | bytes 1540
  329.9 34.6 %copy-start.26 = (f32[128]{0:T(128)S(1)}, f32[128]{0:T(128)}, u32[]{:S(2)}) copy-start(f32[128]{0:T(128)} %get-tuple-element.23) | copy-start | bytes 1540
  329.9 34.6 %copy-start.29 = (f32[128]{0:T(128)S(1)}, f32[128]{0:T(128)}, u32[]{:S(2)}) copy-start(f32[128]{0:T(128)} %get-tuple-element.25) | copy-start | bytes 1540
  329.9 54.4 %copy-start.19 = (f32[128]{0:T(128)S(1)}, f32[128]{0:T(128)}, u32[]{:S(2)}) copy-start(f32[128]{0:T(128)} %copy-done.18) | copy-start | bytes 1540
  329.9 55.5 %copy-start.17 = (f32[128]{0:T(128)S(1)}, f32[128]{0:T(128)}, u32[]{:S(2)}) copy-start(f32[128]{0:T(128)} %copy-done.16) | copy-start | bytes 1540
  357.5 6.7 %copy-start.9 = (f32[128,1,512]{2,1,0:T(1,128)S(1)}, f32[128,1,512]{2,1,0:T(1,128)}, u32[]{:S(2)}) copy-start(f32[128,1,512]{2,1,0:T(1,128)} %get-tuple-element.14) | copy-start | bytes 786436
  386.9 2.6 copy-start.24
  386.9 2.6 copy-start.27
  386.9 2.6 copy-start.28
  389.4 2.8 copy-start.2
Sparse Core Ops, SparseCore 0:
  20.1 43.8 all-gather.8
  72.0 40.1 all-gather.10
  120.2 40.1 all-gather.12
  168.9 40.1 all-gather.14
  217.5 40.1 all-gather.16
  267.5 40.1 all-gather.18
  317.4 40.1 all-gather.20

commit v8 on v4

--- a/solution.py
+++ b/solution.py
@@ -63,7 +63,7 @@
         norm_ref[...] = jnp.sum(fwd_ref[...] * back, axis=1, keepdims=True)
 
 
-def backward_step(whole, transition, emit_next, fwd, tk=2048):
+def backward_step(whole, transition, emit_next, fwd, tk=4096):
     b, states = whole.shape
     rows = transition.shape[0]
     full = lambda k: (0, 0)

time: 414 us -> 410 us (level)
  Pallas kernels: 73.7 us -> 69.4 us
    pallas_call x7, Pallas kernels: 51.9 us -> 47.5 us  [backward_step(): pl.pallas_call(_step_kernel, grid=(states // tk,), in_specs=[pl.BlockSpec...]
where the time goes in v8:
time: 410 us; the launch traced here: 409 us
  waiting for transfers between devices  233 us (57%)
  Pallas kernels  69.4 us (17%)
  local copies, waits for them, and re-layouts  37.9 us (9%)
  matrix products  31.4 us (8%)
  blocking collectives  19.5 us (5%)
  between operations  14.4 us (4%)
    all_gather x7, waiting for transfers between devices, on_device(): whole = lax.all_gather(weighted, 'state', axis=1, tiled=True)  233 us
    pallas_call x7, Pallas kernels, backward_step(): pl.pallas_call(_step_kernel, grid=(states // tk,), in_specs=[pl.BlockSpec...  47.5 us
    pallas_call x1, Pallas kernels, emitted_rows(): pl.pallas_call(_emit_kernel, grid=(vocab // tv,), in_specs=[pl.BlockSpec(...  21.8 us
    dynamic_update_slice x7, local copies, waits for them, and re-layouts, on_device(): vector_mat = lax.dynamic_update_slice(vector_mat, whole, (t * seq_count, 0))  20.1 us
    all_gather x1, blocking collectives, on_device(): norm_parts = lax.all_gather(partial_norms, 'state', axis=0, tiled=False)  19.5 us
    dot_general x1, matrix products, on_device(): lax.dot_general(share_mat, vector_mat, (((0,), (0,)), ((), ())), preferre...  19.3 us
    dot_general x1, matrix products, emitted_rows_xla(): lax.dot_general(onehot, emission, NT, preferred_element_type=jnp.float32)  12.2 us
    unnamed x70, local copies, waits for them, and re-layouts  9.75 us
  transfers between devices with their start and end apart: 7, of which 7 were waited for; matrix products, arithmetic and copies ran while one was open for 7% of the time, Pallas kernels for 5%

profile of v8, /device:TPU:0, one launch (start us, length us, event | category | flops | bytes accessed | tf_op | source)
XLA Modules:
  0.0 409.1 jit_solution(14584593422045320680)
XLA Ops:
  7.2 0.0 all-gather.9.cloned.1.call-start
  7.2 0.7 slice_bitcast_fusion.1
  7.9 12.2 %fusion.3 = bf16[128,512]{1,0:T(8,128)(2,1)} fusion(bf16[512,16384]{1,0:T(8,128)(2,1)} %em_ref.1, s32[128]{0:T(128)S(1)} %slice_bitcast_fusion.1), kind=kOutput, calls=%fused_computation.6 | convolution fusion | flops 2149646336 | bytes 16908800 | tf_op jit(solution)/shard_map/dot_general | solution.py:101
  20.1 0.0 all-gather.9.cloned.1.call-update
  20.1 0.0 all-gather.11.cloned.1.call-start
  20.2 1.0 copy.58
  21.2 1.9 fusion.4
  23.1 0.7 copy.78
  23.8 21.8 %shard_map.59 = f32[896,512]{1,0:T(8,128)} custom-call(s32[896,1]{1,0:T(8,128)} %bitcast.66, bf16[512,16384]{1,0:T(8,128)(2,1)} %em_ref.1), custom_call_target="tpu_custom_call" | custom-call | flops 15032385536 | bytes 18612224 | tf_op jit(solution)/shard_map/pallas_call | solution.py:29
  45.6 2.7 fusion.5
  48.3 15.9 %all-gather.9.cloned.1.call-done.whole_ref = bf16[128,8192]{1,0:T(8,128)(2,1)} async-done(((bf16[128,512]{1,0:T(8,128)(2,1)}), bf16[128,8192]{1,0:T(8,128)(2,1)}) %all-gather.9.cloned.1.call-update) | async-done | bytes 2097168 | tf_op jit(solution)/shard_map/all_gather | solution.py:119
  64.1 6.7 %shard_map.60 = (f32[128,512]{1,0:T(8,128)}, bf16[128,512]{1,0:T(8,128)(2,1)}, f32[128,1]{1,0:T(8,128)}, f32[128,1]{1,0:T(8,128)}) custom-call(bf16[128,8192]{1,0:T(8,128)(2,1)} %all-gather.9.cloned.1.call-done.whole_ref, bf16[512,8192]{1,0:T(8,128)(2,1)} %trans_ref.13, f32[128,512]{1,0:T(8,128)} %get-tuple-element.75.emit_ref, f32[128,512]{1,0:T(8,128)} %bitcast.60), custom_call_target="tpu_custom_call" | custom-call | flops 1073741824 | bytes 10485760 | tf_op jit(solution)/shard_map/pallas_call | solution.py:70
  70.9 0.0 all-gather.11.cloned.1.call-update
  70.9 0.0 all-gather.13.cloned.1.call-start
  71.0 0.7 copy.77
  71.7 39.5 %all-gather.11.cloned.1.call-done.whole_ref = bf16[128,8192]{1,0:T(8,128)(2,1)} async-done(((bf16[128,512]{1,0:T(8,128)(2,1)}), bf16[128,8192]{1,0:T(8,128)(2,1)}) %all-gather.11.cloned.1.call-update) | async-done | bytes 2097168 | tf_op jit(solution)/shard_map/all_gather | solution.py:119
  111.2 6.8 %shard_map.61 = (f32[128,512]{1,0:T(8,128)}, bf16[128,512]{1,0:T(8,128)(2,1)}, f32[128,1]{1,0:T(8,128)}, f32[128,1]{1,0:T(8,128)}) custom-call(bf16[128,8192]{1,0:T(8,128)(2,1)} %all-gather.11.cloned.1.call-done.whole_ref, bf16[512,8192]{1,0:T(8,128)(2,1)} %trans_ref.13, f32[128,512]{1,0:T(8,128)} %get-tuple-element.74.emit_ref, f32[128,512]{1,0:T(8,128)} %bitcast.62), custom_call_target="tpu_custom_call" | custom-call | flops 1073741824 | bytes 10485760 | tf_op jit(solution)/shard_map/pallas_call | solution.py:70
  117.9 0.0 all-gather.13.cloned.1.call-update
  118.0 0.0 all-gather.15.cloned.1.call-start
  118.0 0.7 copy.76
  118.7 39.5 %all-gather.13.cloned.1.call-done.whole_ref = bf16[128,8192]{1,0:T(8,128)(2,1)} async-done(((bf16[128,512]{1,0:T(8,128)(2,1)}), bf16[128,8192]{1,0:T(8,128)(2,1)}) %all-gather.13.cloned.1.call-update) | async-done | bytes 2097168 | tf_op jit(solution)/shard_map/all_gather | solution.py:119
  158.2 6.8 %shard_map.62 = (f32[128,512]{1,0:T(8,128)}, bf16[128,512]{1,0:T(8,128)(2,1)}, f32[128,1]{1,0:T(8,128)}, f32[128,1]{1,0:T(8,128)}) custom-call(bf16[128,8192]{1,0:T(8,128)(2,1)} %all-gather.13.cloned.1.call-done.whole_ref, bf16[512,8192]{1,0:T(8,128)(2,1)} %trans_ref.13, f32[128,512]{1,0:T(8,128)} %get-tuple-element.73.emit_ref, f32[128,512]{1,0:T(8,128)} %bitcast.63), custom_call_target="tpu_custom_call" | custom-call | flops 1073741824 | bytes 10485760 | tf_op jit(solution)/shard_map/pallas_call | solution.py:70
  165.0 0.0 all-gather.15.cloned.1.call-update
  165.0 0.0 all-gather.17.cloned.1.call-start
  165.1 0.7 copy.75
  165.8 39.5 %all-gather.15.cloned.1.call-done.whole_ref = bf16[128,8192]{1,0:T(8,128)(2,1)} async-done(((bf16[128,512]{1,0:T(8,128)(2,1)}), bf16[128,8192]{1,0:T(8,128)(2,1)}) %all-gather.15.cloned.1.call-update) | async-done | bytes 2097168 | tf_op jit(solution)/shard_map/all_gather | solution.py:119
  205.3 6.7 %shard_map.63 = (f32[128,512]{1,0:T(8,128)}, bf16[128,512]{1,0:T(8,128)(2,1)}, f32[128,1]{1,0:T(8,128)}, f32[128,1]{1,0:T(8,128)}) custom-call(bf16[128,8192]{1,0:T(8,128)(2,1)} %all-gather.15.cloned.1.call-done.whole_ref, bf16[512,8192]{1,0:T(8,128)(2,1)} %trans_ref.13, f32[128,512]{1,0:T(8,128)} %get-tuple-element.72.emit_ref, f32[128,512]{1,0:T(8,128)} %bitcast.64), custom_call_target="tpu_custom_call" | custom-call | flops 1073741824 | bytes 10485760 | tf_op jit(solution)/shard_map/pallas_call | solution.py:70
  212.0 0.2 all-gather.19.cloned.1.call-start
  212.3 0.7 copy.74
  213.0 39.3 %all-gather.17.cloned.1.call-done.whole_ref = bf16[128,8192]{1,0:T(8,128)(2,1)} async-done(((bf16[128,512]{1,0:T(8,128)(2,1)}), bf16[128,8192]{1,0:T(8,128)(2,1)}) %all-gather.17.cloned.1.call-update) | async-done | bytes 2097168 | tf_op jit(solution)/shard_map/all_gather | solution.py:119
  252.3 6.9 %shard_map.64 = (f32[128,512]{1,0:T(8,128)}, bf16[128,512]{1,0:T(8,128)(2,1)}, f32[128,1]{1,0:T(8,128)}, f32[128,1]{1,0:T(8,128)}) custom-call(bf16[128,8192]{1,0:T(8,128)(2,1)} %all-gather.17.cloned.1.call-done.whole_ref, bf16[512,8192]{1,0:T(8,128)(2,1)} %trans_ref.13, f32[128,512]{1,0:T(8,128)} %get-tuple-element.71.emit_ref, f32[128,512]{1,0:T(8,128)} %bitcast.65), custom_call_target="tpu_custom_call" | custom-call | flops 1073741824 | bytes 10485760 | tf_op jit(solution)/shard_map/pallas_call | solution.py:70
  259.2 0.0 all-gather.21.cloned.1.call-start
  259.3 0.7 copy.73
  260.0 0.7 copy.72
  260.7 0.1 copy.47
  260.8 0.1 copy.40
  260.8 7.4 %dynamic_update_slice.21 = bf16[896,8192]{1,0:T(8,128)(2,1)} pad(bf16[128,8192]{1,0:T(8,128)(2,1)S(1)} %copy-done, bf16[]{:T(256)} %constant.1.clone.1), padding=768_0x0_0 | pad | bytes 16777218 | tf_op jit(solution)/shard_map/dynamic_update_slice | solution.py:123
  268.3 31.2 %all-gather.19.cloned.1.call-done.whole_ref = bf16[128,8192]{1,0:T(8,128)(2,1)} async-done(((bf16[128,512]{1,0:T(8,128)(2,1)}), bf16[128,8192]{1,0:T(8,128)(2,1)}) %all-gather.19.cloned.1.call-update) | async-done | bytes 2097168 | tf_op jit(solution)/shard_map/all_gather | solution.py:119
  299.5 6.9 %shard_map.65 = (f32[128,512]{1,0:T(8,128)}, bf16[128,512]{1,0:T(8,128)(2,1)}, f32[128,1]{1,0:T(8,128)}, f32[128,1]{1,0:T(8,128)}) custom-call(bf16[128,8192]{1,0:T(8,128)(2,1)} %all-gather.19.cloned.1.call-done.whole_ref, bf16[512,8192]{1,0:T(8,128)(2,1)} %trans_ref.13, f32[128,512]{1,0:T(8,128)} %get-tuple-element.70.emit_ref, f32[128,512]{1,0:T(8,128)} %bitcast.61), custom_call_target="tpu_custom_call" | custom-call | flops 1073741824 | bytes 10485760 | tf_op jit(solution)/shard_map/pallas_call | solution.py:70
  306.4 1.6 constant_dynamic-update-slice_fusion.5
  308.0 0.1 copy.46
  308.1 0.1 copy.39
  308.1 0.1 copy.45
  308.2 0.1 copy.38
  308.3 3.3 constant_dynamic-update-slice_fusion.4
  311.6 0.1 copy.44
  311.6 0.1 copy.37
  311.7 1.5 constant_dynamic-update-slice_fusion.3
  313.3 0.1 copy.43
  313.4 0.1 copy.36
  313.4 3.3 constant_dynamic-update-slice_fusion.2
  316.7 0.1 copy.42
  316.8 0.1 copy.35
  316.9 1.5 constant_dynamic-update-slice_fusion.1
  318.4 28.2 %all-gather.21.cloned.1.call-done.whole_ref = bf16[128,8192]{1,0:T(8,128)(2,1)} async-done(((bf16[128,512]{1,0:T(8,128)(2,1)}), bf16[128,8192]{1,0:T(8,128)(2,1)}) %all-gather.21.cloned.1.call-update) | async-done | bytes 2097168 | tf_op jit(solution)/shard_map/all_gather | solution.py:119
  346.7 6.8 %shard_map.66 = (f32[128,512]{1,0:T(8,128)}, bf16[128,512]{1,0:T(8,128)(2,1)}, f32[128,1]{1,0:T(8,128)}, f32[128,1]{1,0:T(8,128)}) custom-call(bf16[128,8192]{1,0:T(8,128)(2,1)} %all-gather.21.cloned.1.call-done.whole_ref, bf16[512,8192]{1,0:T(8,128)(2,1)} %trans_ref.13, f32[128,512]{1,0:T(8,128)} %get-tuple-element.69.emit_ref, f32[128,512]{1,0:T(8,128)} %bitcast.59), custom_call_target="tpu_custom_call" | custom-call | flops 1073741824 | bytes 10485760 | tf_op jit(solution)/shard_map/pallas_call | solution.py:70
  353.5 1.0 copy.41
  354.5 19.5 %all-gather = f32[2048,7]{0,1:T(8,128)S(1)} all-gather(f32[128,7]{0,1:T(8,128)S(1)} %concatenate.11), channel_id=2, replica_groups=mesh['groups'=2,'state'=16] {'state'}, dimensions={0}, use_global_device_ids=true | all-gather | bytes 60928 | tf_op jit(solution)/shard_map/all_gather | solution.py:131
  374.0 0.9 copy.34
  374.9 1.0 bitcast_dynamic-update-slice_fusion.6
  376.2 2.5 copy.48
  378.8 2.8 fusion.2
  381.5 1.5 constant_dynamic-update-slice_fusion
  383.0 19.3 %multiply_multiply_fusion = f32[512,8192]{1,0:T(8,128)} fusion(bf16[512,8192]{1,0:T(8,128)(2,1)} %trans_ref.13, bf16[896,512]{1,0:T(8,128)(2,1)S(1)} %bitcast.57, bf16[896,8192]{1,0:T(8,128)(2,1)} %constant_dynamic-update-slice_fusion), kind=kOutput, calls=%fused_computation | convolution fusion | flops 7528775680 | bytes 40763392 | tf_op jit(solution)/shard_map/dot_general | solution.py:136
  (68 shorter events, 0.4 us)
Async XLA Ops:
  7.2 57.0 %all-gather.9.cloned.1.call-start = ((), (), s32[]{:S(2)}) async-start(), calls=%async_computation | async-start | bytes 2228224 | tf_op jit(solution)/shard_map/all_gather | solution.py:119
  7.9 12.2 %copy-start.25 = (s32[128,8]{0,1:T(8,128)S(1)}, s32[128,8]{0,1:T(8,128)}, u32[]{:S(2)}) copy-start(s32[128,8]{0,1:T(8,128)} %param.5) | copy-start | bytes 12292
  7.9 13.2 %copy-start.5 = (f32[128,8,512]{2,1,0:T(8,128)S(1)}, f32[128,8,512]{2,1,0:T(8,128)}, u32[]{:S(2)}) copy-start(f32[128,8,512]{2,1,0:T(8,128)} %param.4) | copy-start | bytes 6291460
  20.1 91.1 %all-gather.11.cloned.1.call-start = ((), (), s32[]{:S(2)}) async-start(), calls=%async_computation.1 | async-start | bytes 2228224 | tf_op jit(solution)/shard_map/all_gather | solution.py:119
  64.1 6.8 %copy-start.6 = (f32[128,1,512]{2,1,0:T(1,128)S(1)}, f32[128,1,512]{2,1,0:T(1,128)}, u32[]{:S(2)}) copy-start(f32[128,1,512]{2,1,0:T(1,128)} %get-tuple-element.67) | copy-start | bytes 786436
  70.9 87.3 %all-gather.13.cloned.1.call-start = ((), (), s32[]{:S(2)}) async-start(), calls=%async_computation.2 | async-start | bytes 2228224 | tf_op jit(solution)/shard_map/all_gather | solution.py:119
  118.0 87.3 %all-gather.15.cloned.1.call-start = ((), (), s32[]{:S(2)}) async-start(), calls=%async_computation.3 | async-start | bytes 2228224 | tf_op jit(solution)/shard_map/all_gather | solution.py:119
  165.0 87.3 %all-gather.17.cloned.1.call-start = ((), (), s32[]{:S(2)}) async-start(), calls=%async_computation.4 | async-start | bytes 2228224 | tf_op jit(solution)/shard_map/all_gather | solution.py:119
  212.0 87.5 %all-gather.19.cloned.1.call-start = ((), (), s32[]{:S(2)}) async-start(), calls=%async_computation.5 | async-start | bytes 2228224 | tf_op jit(solution)/shard_map/all_gather | solution.py:119
  252.3 8.4 %copy-start.16 = (f32[128,1]{1,0:T(8,128)S(1)}, f32[128,1]{1,0:T(8,128)}, u32[]{:S(2)}) copy-start(f32[128,1]{1,0:T(8,128)} %get-tuple-element.55) | copy-start | bytes 1540
  252.3 8.5 %copy-start.15 = (f32[128,1]{1,0:T(8,128)S(1)}, f32[128,1]{1,0:T(8,128)}, u32[]{:S(2)}) copy-start(f32[128,1]{1,0:T(8,128)} %get-tuple-element.48) | copy-start | bytes 1540
  252.3 8.5 %copy-start = (bf16[128,8192]{1,0:T(8,128)(2,1)S(1)}, bf16[128,8192]{1,0:T(8,128)(2,1)}, u32[]{:S(2)}) copy-start(bf16[128,8192]{1,0:T(8,128)(2,1)} %all-gather.9.cloned.1.call-done.whole_ref) | copy-start | bytes 6291460
  259.2 87.4 %all-gather.21.cloned.1.call-start = ((), (), s32[]{:S(2)}) async-start(), calls=%async_computation.6 | async-start | bytes 2228224 | tf_op jit(solution)/shard_map/all_gather | solution.py:119
  299.5 6.9 %copy-start.1 = (bf16[128,8192]{1,0:T(8,128)(2,1)S(1)}, bf16[128,8192]{1,0:T(8,128)(2,1)}, u32[]{:S(2)}) copy-start(bf16[128,8192]{1,0:T(8,128)(2,1)} %all-gather.11.cloned.1.call-done.whole_ref) | copy-start | bytes 6291460
  306.4 1.6 copy-start.14
  306.4 1.7 copy-start.13
  306.4 1.7 copy-start.18
  306.4 1.8 copy-start.17
  308.3 3.3 copy-start.20
  308.3 3.3 copy-start.19
  308.3 3.4 copy-start.3
  311.7 1.6 copy-start.22
  311.7 1.6 copy-start.21
  313.4 3.3 copy-start.24
  313.4 3.4 copy-start.23
  313.4 3.5 copy-start.4
  346.6 29.3 %copy-start.12 = (f32[128,512]{1,0:T(8,128)S(1)}, f32[128,512]{1,0:T(8,128)}, u32[]{:S(2)}) copy-start(f32[128,512]{1,0:T(8,128)} %get-tuple-element.36) | copy-start | bytes 786436
  346.6 29.3 %copy-start.11 = (f32[128,512]{1,0:T(8,128)S(1)}, f32[128,512]{1,0:T(8,128)}, u32[]{:S(2)}) copy-start(f32[128,512]{1,0:T(8,128)} %get-tuple-element.37) | copy-start | bytes 786436
  346.7 29.4 %copy-start.10 = (f32[128,512]{1,0:T(8,128)S(1)}, f32[128,512]{1,0:T(8,128)}, u32[]{:S(2)}) copy-start(f32[128,512]{1,0:T(8,128)} %get-tuple-element.38) | copy-start | bytes 786436
  353.5 22.6 %copy-start.9 = (f32[128,512]{1,0:T(8,128)S(1)}, f32[128,512]{1,0:T(8,128)}, u32[]{:S(2)}) copy-start(f32[128,512]{1,0:T(8,128)} %get-tuple-element.39) | copy-start | bytes 786436
  353.5 22.6 %copy-start.8 = (f32[128,512]{1,0:T(8,128)S(1)}, f32[128,512]{1,0:T(8,128)}, u32[]{:S(2)}) copy-start(f32[128,512]{1,0:T(8,128)} %get-tuple-element.40) | copy-start | bytes 786436
  353.5 22.6 %copy-start.7 = (f32[128,512]{1,0:T(8,128)S(1)}, f32[128,512]{1,0:T(8,128)}, u32[]{:S(2)}) copy-start(f32[128,512]{1,0:T(8,128)} %get-tuple-element.41) | copy-start | bytes 786436
  378.7 2.8 copy-start.2
Sparse Core Ops, SparseCore 0:
  20.2 43.8 all-gather.8
  71.0 40.1 all-gather.10
  118.1 40.1 all-gather.12
  165.1 40.1 all-gather.14
  212.2 40.1 all-gather.16
  259.3 40.1 all-gather.18
  306.5 40.1 all-gather.20

commit v9 on v8

--- a/solution.py
+++ b/solution.py
@@ -59,8 +59,10 @@
         back = acc_ref[...] / s
         back_ref[...] = back
         wnext_ref[...] = (emit_ref[...] * back).astype(wnext_ref.dtype)
-        scale_ref[...] = s
-        norm_ref[...] = jnp.sum(fwd_ref[...] * back, axis=1, keepdims=True)
+        lanes = scale_ref.shape[1]
+        scale_ref[...] = jnp.broadcast_to(s, (s.shape[0], lanes))
+        norm = jnp.sum(fwd_ref[...] * back, axis=1, keepdims=True)
+        norm_ref[...] = jnp.broadcast_to(norm, (norm.shape[0], lanes))
 
 
 def backward_step(whole, transition, emit_next, fwd, tk=4096):
@@ -79,14 +81,14 @@
         out_specs=[
             pl.BlockSpec((b, rows), full),
             pl.BlockSpec((b, rows), full),
-            pl.BlockSpec((b, 1), full),
-            pl.BlockSpec((b, 1), full),
+            pl.BlockSpec((b, 128), full),
+            pl.BlockSpec((b, 128), full),
         ],
         out_shape=[
             jax.ShapeDtypeStruct((b, rows), jnp.float32),
             jax.ShapeDtypeStruct((b, rows), jnp.bfloat16),
-            jax.ShapeDtypeStruct((b, 1), jnp.float32),
-            jax.ShapeDtypeStruct((b, 1), jnp.float32),
+            jax.ShapeDtypeStruct((b, 128), jnp.float32),
+            jax.ShapeDtypeStruct((b, 128), jnp.float32),
         ],
         scratch_shapes=[pltpu.VMEM((b, rows), jnp.float32), pltpu.VMEM((b, 1), jnp.float32)],
         cost_estimate=pl.CostEstimate(
@@ -121,9 +123,9 @@
             whole, transition, emitted_early[t], forward_probs[:, t, :]
         )
         vector_mat = lax.dynamic_update_slice(vector_mat, whole, (t * seq_count, 0))
-        scales.append(scale_sum)
+        scales.append(scale_sum[:, :1])
         backs.append(backward)
-        norms.append(norm_part)
+        norms.append(norm_part[:, :1])
     backs = backs[::-1]
     scales = jnp.concatenate(scales[::-1], axis=1)
     partial_norms = jnp.concatenate(norms[::-1], axis=1)

time: 410 us -> 410 us (level)
  no operation moved by 1% of the time
where the time goes in v9:
time: 410 us; the launch traced here: 409 us
  waiting for transfers between devices  233 us (57%)
  Pallas kernels  69.4 us (17%)
  local copies, waits for them, and re-layouts  37.9 us (9%)
  matrix products  31.4 us (8%)
  blocking collectives  19.5 us (5%)
  between operations  14.4 us (4%)
    all_gather x7, waiting for transfers between devices, on_device(): whole = lax.all_gather(weighted, 'state', axis=1, tiled=True)  233 us
    pallas_call x7, Pallas kernels, backward_step(): pl.pallas_call(_step_kernel, grid=(states // tk,), in_specs=[pl.BlockSpec...  47.5 us
    pallas_call x1, Pallas kernels, emitted_rows(): pl.pallas_call(_emit_kernel, grid=(vocab // tv,), in_specs=[pl.BlockSpec(...  21.8 us
    dynamic_update_slice x7, local copies, waits for them, and re-layouts, on_device(): vector_mat = lax.dynamic_update_slice(vector_mat, whole, (t * seq_count, 0))  20.1 us
    all_gather x1, blocking collectives, on_device(): norm_parts = lax.all_gather(partial_norms, 'state', axis=0, tiled=False)  19.5 us
    dot_general x1, matrix products, on_device(): lax.dot_general(share_mat, vector_mat, (((0,), (0,)), ((), ())), preferre...  19.3 us
    dot_general x1, matrix products, emitted_rows_xla(): lax.dot_general(onehot, emission, NT, preferred_element_type=jnp.float32)  12.2 us
    unnamed x70, local copies, waits for them, and re-layouts  9.75 us
  transfers between devices with their start and end apart: 7, of which 7 were waited for; matrix products, arithmetic and copies ran while one was open for 7% of the time, Pallas kernels for 5%

profile of v9, /device:TPU:0, one launch (start us, length us, event | category | flops | bytes accessed | tf_op | source)
XLA Modules:
  0.0 409.1 jit_solution(17514327020515813932)
XLA Ops:
  7.2 0.0 all-gather.9.cloned.1.call-start
  7.2 0.7 slice_bitcast_fusion.1
  7.9 12.2 %fusion.3 = bf16[128,512]{1,0:T(8,128)(2,1)} fusion(bf16[512,16384]{1,0:T(8,128)(2,1)} %em_ref.1, s32[128]{0:T(128)S(1)} %slice_bitcast_fusion.1), kind=kOutput, calls=%fused_computation.6 | convolution fusion | flops 2149646336 | bytes 16908800 | tf_op jit(solution)/shard_map/dot_general | solution.py:103
  20.1 0.0 all-gather.9.cloned.1.call-update
  20.1 0.0 all-gather.11.cloned.1.call-start
  20.2 1.0 copy.58
  21.2 1.9 fusion.4
  23.1 0.7 copy.78
  23.8 21.8 %shard_map.59 = f32[896,512]{1,0:T(8,128)} custom-call(s32[896,1]{1,0:T(8,128)} %bitcast.80, bf16[512,16384]{1,0:T(8,128)(2,1)} %em_ref.1), custom_call_target="tpu_custom_call" | custom-call | flops 15032385536 | bytes 18612224 | tf_op jit(solution)/shard_map/pallas_call | solution.py:29
  45.6 2.7 fusion.5
  48.3 15.9 %all-gather.9.cloned.1.call-done.whole_ref = bf16[128,8192]{1,0:T(8,128)(2,1)} async-done(((bf16[128,512]{1,0:T(8,128)(2,1)}), bf16[128,8192]{1,0:T(8,128)(2,1)}) %all-gather.9.cloned.1.call-update) | async-done | bytes 2097168 | tf_op jit(solution)/shard_map/all_gather | solution.py:121
  64.1 6.7 %shard_map.60 = (f32[128,512]{1,0:T(8,128)}, bf16[128,512]{1,0:T(8,128)(2,1)}, f32[128,128]{1,0:T(8,128)}, f32[128,128]{1,0:T(8,128)}) custom-call(bf16[128,8192]{1,0:T(8,128)(2,1)} %all-gather.9.cloned.1.call-done.whole_ref, bf16[512,8192]{1,0:T(8,128)(2,1)} %trans_ref.13, f32[128,512]{1,0:T(8,128)} %get-tuple-element.75.emit_ref, f32[128,512]{1,0:T(8,128)} %bitcast.74), custom_call_target="tpu_custom_call" | custom-call | flops 1073741824 | bytes 10485760 | tf_op jit(solution)/shard_map/pallas_call | solution.py:72
  70.9 0.0 all-gather.11.cloned.1.call-update
  70.9 0.0 all-gather.13.cloned.1.call-start
  71.0 0.7 copy.77
  71.7 39.5 %all-gather.11.cloned.1.call-done.whole_ref = bf16[128,8192]{1,0:T(8,128)(2,1)} async-done(((bf16[128,512]{1,0:T(8,128)(2,1)}), bf16[128,8192]{1,0:T(8,128)(2,1)}) %all-gather.11.cloned.1.call-update) | async-done | bytes 2097168 | tf_op jit(solution)/shard_map/all_gather | solution.py:121
  111.2 6.8 %shard_map.61 = (f32[128,512]{1,0:T(8,128)}, bf16[128,512]{1,0:T(8,128)(2,1)}, f32[128,128]{1,0:T(8,128)}, f32[128,128]{1,0:T(8,128)}) custom-call(bf16[128,8192]{1,0:T(8,128)(2,1)} %all-gather.11.cloned.1.call-done.whole_ref, bf16[512,8192]{1,0:T(8,128)(2,1)} %trans_ref.13, f32[128,512]{1,0:T(8,128)} %get-tuple-element.74.emit_ref, f32[128,512]{1,0:T(8,128)} %bitcast.76), custom_call_target="tpu_custom_call" | custom-call | flops 1073741824 | bytes 10485760 | tf_op jit(solution)/shard_map/pallas_call | solution.py:72
  117.9 0.0 all-gather.13.cloned.1.call-update
  118.0 0.0 all-gather.15.cloned.1.call-start
  118.0 0.7 copy.76
  118.7 39.5 %all-gather.13.cloned.1.call-done.whole_ref = bf16[128,8192]{1,0:T(8,128)(2,1)} async-done(((bf16[128,512]{1,0:T(8,128)(2,1)}), bf16[128,8192]{1,0:T(8,128)(2,1)}) %all-gather.13.cloned.1.call-update) | async-done | bytes 2097168 | tf_op jit(solution)/shard_map/all_gather | solution.py:121
  158.2 6.8 %shard_map.62 = (f32[128,512]{1,0:T(8,128)}, bf16[128,512]{1,0:T(8,128)(2,1)}, f32[128,128]{1,0:T(8,128)}, f32[128,128]{1,0:T(8,128)}) custom-call(bf16[128,8192]{1,0:T(8,128)(2,1)} %all-gather.13.cloned.1.call-done.whole_ref, bf16[512,8192]{1,0:T(8,128)(2,1)} %trans_ref.13, f32[128,512]{1,0:T(8,128)} %get-tuple-element.73.emit_ref, f32[128,512]{1,0:T(8,128)} %bitcast.77), custom_call_target="tpu_custom_call" | custom-call | flops 1073741824 | bytes 10485760 | tf_op jit(solution)/shard_map/pallas_call | solution.py:72
  165.0 0.0 all-gather.15.cloned.1.call-update
  165.0 0.0 all-gather.17.cloned.1.call-start
  165.1 0.7 copy.75
  165.8 39.5 %all-gather.15.cloned.1.call-done.whole_ref = bf16[128,8192]{1,0:T(8,128)(2,1)} async-done(((bf16[128,512]{1,0:T(8,128)(2,1)}), bf16[128,8192]{1,0:T(8,128)(2,1)}) %all-gather.15.cloned.1.call-update) | async-done | bytes 2097168 | tf_op jit(solution)/shard_map/all_gather | solution.py:121
  205.3 6.7 %shard_map.63 = (f32[128,512]{1,0:T(8,128)}, bf16[128,512]{1,0:T(8,128)(2,1)}, f32[128,128]{1,0:T(8,128)}, f32[128,128]{1,0:T(8,128)}) custom-call(bf16[128,8192]{1,0:T(8,128)(2,1)} %all-gather.15.cloned.1.call-done.whole_ref, bf16[512,8192]{1,0:T(8,128)(2,1)} %trans_ref.13, f32[128,512]{1,0:T(8,128)} %get-tuple-element.72.emit_ref, f32[128,512]{1,0:T(8,128)} %bitcast.78), custom_call_target="tpu_custom_call" | custom-call | flops 1073741824 | bytes 10485760 | tf_op jit(solution)/shard_map/pallas_call | solution.py:72
  212.0 0.2 all-gather.19.cloned.1.call-start
  212.3 0.7 copy.74
  213.0 39.3 %all-gather.17.cloned.1.call-done.whole_ref = bf16[128,8192]{1,0:T(8,128)(2,1)} async-done(((bf16[128,512]{1,0:T(8,128)(2,1)}), bf16[128,8192]{1,0:T(8,128)(2,1)}) %all-gather.17.cloned.1.call-update) | async-done | bytes 2097168 | tf_op jit(solution)/shard_map/all_gather | solution.py:121
  252.3 6.9 %shard_map.64 = (f32[128,512]{1,0:T(8,128)}, bf16[128,512]{1,0:T(8,128)(2,1)}, f32[128,128]{1,0:T(8,128)}, f32[128,128]{1,0:T(8,128)}) custom-call(bf16[128,8192]{1,0:T(8,128)(2,1)} %all-gather.17.cloned.1.call-done.whole_ref, bf16[512,8192]{1,0:T(8,128)(2,1)} %trans_ref.13, f32[128,512]{1,0:T(8,128)} %get-tuple-element.71.emit_ref, f32[128,512]{1,0:T(8,128)} %bitcast.79), custom_call_target="tpu_custom_call" | custom-call | flops 1073741824 | bytes 10485760 | tf_op jit(solution)/shard_map/pallas_call | solution.py:72
  259.2 0.0 all-gather.21.cloned.1.call-start
  259.3 0.7 copy.73
  260.0 0.7 copy.72
  260.7 0.1 copy.47
  260.8 0.1 copy.40
  260.8 7.4 %dynamic_update_slice.21 = bf16[896,8192]{1,0:T(8,128)(2,1)} pad(bf16[128,8192]{1,0:T(8,128)(2,1)S(1)} %copy-done, bf16[]{:T(256)} %constant.1.clone.1), padding=768_0x0_0 | pad | bytes 16777218 | tf_op jit(solution)/shard_map/dynamic_update_slice | solution.py:125
  268.3 31.2 %all-gather.19.cloned.1.call-done.whole_ref = bf16[128,8192]{1,0:T(8,128)(2,1)} async-done(((bf16[128,512]{1,0:T(8,128)(2,1)}), bf16[128,8192]{1,0:T(8,128)(2,1)}) %all-gather.19.cloned.1.call-update) | async-done | bytes 2097168 | tf_op jit(solution)/shard_map/all_gather | solution.py:121
  299.5 6.9 %shard_map.65 = (f32[128,512]{1,0:T(8,128)}, bf16[128,512]{1,0:T(8,128)(2,1)}, f32[128,128]{1,0:T(8,128)}, f32[128,128]{1,0:T(8,128)}) custom-call(bf16[128,8192]{1,0:T(8,128)(2,1)} %all-gather.19.cloned.1.call-done.whole_ref, bf16[512,8192]{1,0:T(8,128)(2,1)} %trans_ref.13, f32[128,512]{1,0:T(8,128)} %get-tuple-element.70.emit_ref, f32[128,512]{1,0:T(8,128)} %bitcast.75), custom_call_target="tpu_custom_call" | custom-call | flops 1073741824 | bytes 10485760 | tf_op jit(solution)/shard_map/pallas_call | solution.py:72
  306.4 1.6 constant_dynamic-update-slice_fusion.5
  308.0 0.1 copy.46
  308.1 0.1 copy.39
  308.1 0.1 copy.45
  308.2 0.1 copy.38
  308.3 3.3 constant_dynamic-update-slice_fusion.4
  311.6 0.1 copy.44
  311.6 0.1 copy.37
  311.7 1.5 constant_dynamic-update-slice_fusion.3
  313.3 0.1 copy.43
  313.4 0.1 copy.36
  313.4 3.3 constant_dynamic-update-slice_fusion.2
  316.7 0.1 copy.42
  316.8 0.1 copy.35
  316.9 1.5 constant_dynamic-update-slice_fusion.1
  318.4 28.2 %all-gather.21.cloned.1.call-done.whole_ref = bf16[128,8192]{1,0:T(8,128)(2,1)} async-done(((bf16[128,512]{1,0:T(8,128)(2,1)}), bf16[128,8192]{1,0:T(8,128)(2,1)}) %all-gather.21.cloned.1.call-update) | async-done | bytes 2097168 | tf_op jit(solution)/shard_map/all_gather | solution.py:121
  346.7 6.8 %shard_map.66 = (f32[128,512]{1,0:T(8,128)}, bf16[128,512]{1,0:T(8,128)(2,1)}, f32[128,128]{1,0:T(8,128)}, f32[128,128]{1,0:T(8,128)}) custom-call(bf16[128,8192]{1,0:T(8,128)(2,1)} %all-gather.21.cloned.1.call-done.whole_ref, bf16[512,8192]{1,0:T(8,128)(2,1)} %trans_ref.13, f32[128,512]{1,0:T(8,128)} %get-tuple-element.69.emit_ref, f32[128,512]{1,0:T(8,128)} %bitcast.73), custom_call_target="tpu_custom_call" | custom-call | flops 1073741824 | bytes 10485760 | tf_op jit(solution)/shard_map/pallas_call | solution.py:72
  353.5 1.0 copy.41
  354.5 19.5 %all-gather = f32[2048,7]{0,1:T(8,128)S(1)} all-gather(f32[128,7]{0,1:T(8,128)S(1)} %concatenate.11), channel_id=2, replica_groups=mesh['groups'=2,'state'=16] {'state'}, dimensions={0}, use_global_device_ids=true | all-gather | bytes 60928 | tf_op jit(solution)/shard_map/all_gather | solution.py:133
  374.0 0.9 copy.34
  374.9 1.0 bitcast_dynamic-update-slice_fusion.6
  376.2 2.5 copy.48
  378.8 2.8 fusion.2
  381.5 1.5 constant_dynamic-update-slice_fusion
  383.0 19.3 %multiply_multiply_fusion = f32[512,8192]{1,0:T(8,128)} fusion(bf16[512,8192]{1,0:T(8,128)(2,1)} %trans_ref.13, bf16[896,512]{1,0:T(8,128)(2,1)S(1)} %bitcast.71, bf16[896,8192]{1,0:T(8,128)(2,1)} %constant_dynamic-update-slice_fusion), kind=kOutput, calls=%fused_computation | convolution fusion | flops 7528775680 | bytes 40763392 | tf_op jit(solution)/shard_map/dot_general | solution.py:138
  (68 shorter events, 0.4 us)
Async XLA Ops:
  7.2 57.0 %all-gather.9.cloned.1.call-start = ((), (), s32[]{:S(2)}) async-start(), calls=%async_computation | async-start | bytes 2228224 | tf_op jit(solution)/shard_map/all_gather | solution.py:121
  7.9 12.2 %copy-start.25 = (s32[128,8]{0,1:T(8,128)S(1)}, s32[128,8]{0,1:T(8,128)}, u32[]{:S(2)}) copy-start(s32[128,8]{0,1:T(8,128)} %param.5) | copy-start | bytes 12292
  7.9 13.2 %copy-start.5 = (f32[128,8,512]{2,1,0:T(8,128)S(1)}, f32[128,8,512]{2,1,0:T(8,128)}, u32[]{:S(2)}) copy-start(f32[128,8,512]{2,1,0:T(8,128)} %param.4) | copy-start | bytes 6291460
  20.1 91.1 %all-gather.11.cloned.1.call-start = ((), (), s32[]{:S(2)}) async-start(), calls=%async_computation.1 | async-start | bytes 2228224 | tf_op jit(solution)/shard_map/all_gather | solution.py:121
  64.1 6.8 %copy-start.6 = (f32[128,1,512]{2,1,0:T(1,128)S(1)}, f32[128,1,512]{2,1,0:T(1,128)}, u32[]{:S(2)}) copy-start(f32[128,1,512]{2,1,0:T(1,128)} %get-tuple-element.67) | copy-start | bytes 786436
  70.9 87.3 %all-gather.13.cloned.1.call-start = ((), (), s32[]{:S(2)}) async-start(), calls=%async_computation.2 | async-start | bytes 2228224 | tf_op jit(solution)/shard_map/all_gather | solution.py:121
  118.0 87.3 %all-gather.15.cloned.1.call-start = ((), (), s32[]{:S(2)}) async-start(), calls=%async_computation.3 | async-start | bytes 2228224 | tf_op jit(solution)/shard_map/all_gather | solution.py:121
  165.0 87.3 %all-gather.17.cloned.1.call-start = ((), (), s32[]{:S(2)}) async-start(), calls=%async_computation.4 | async-start | bytes 2228224 | tf_op jit(solution)/shard_map/all_gather | solution.py:121
  212.0 87.5 %all-gather.19.cloned.1.call-start = ((), (), s32[]{:S(2)}) async-start(), calls=%async_computation.5 | async-start | bytes 2228224 | tf_op jit(solution)/shard_map/all_gather | solution.py:121
  252.3 8.4 %copy-start.16 = (f32[128,128]{1,0:T(8,128)S(1)}, f32[128,128]{1,0:T(8,128)}, u32[]{:S(2)}) copy-start(f32[128,128]{1,0:T(8,128)} %get-tuple-element.55) | copy-start | bytes 196612
  252.3 8.5 %copy-start.15 = (f32[128,128]{1,0:T(8,128)S(1)}, f32[128,128]{1,0:T(8,128)}, u32[]{:S(2)}) copy-start(f32[128,128]{1,0:T(8,128)} %get-tuple-element.48) | copy-start | bytes 196612
  252.3 8.5 %copy-start = (bf16[128,8192]{1,0:T(8,128)(2,1)S(1)}, bf16[128,8192]{1,0:T(8,128)(2,1)}, u32[]{:S(2)}) copy-start(bf16[128,8192]{1,0:T(8,128)(2,1)} %all-gather.9.cloned.1.call-done.whole_ref) | copy-start | bytes 6291460
  259.2 87.4 %all-gather.21.cloned.1.call-start = ((), (), s32[]{:S(2)}) async-start(), calls=%async_computation.6 | async-start | bytes 2228224 | tf_op jit(solution)/shard_map/all_gather | solution.py:121
  299.5 6.9 %copy-start.1 = (bf16[128,8192]{1,0:T(8,128)(2,1)S(1)}, bf16[128,8192]{1,0:T(8,128)(2,1)}, u32[]{:S(2)}) copy-start(bf16[128,8192]{1,0:T(8,128)(2,1)} %all-gather.11.cloned.1.call-done.whole_ref) | copy-start | bytes 6291460
  306.4 1.6 copy-start.14
  306.4 1.7 copy-start.13
  306.4 1.7 copy-start.18
  306.4 1.8 copy-start.17
  308.3 3.3 copy-start.20
  308.3 3.3 copy-start.19
  308.3 3.4 copy-start.3
  311.7 1.6 copy-start.22
  311.7 1.6 copy-start.21
  313.4 3.3 copy-start.24
  313.4 3.4 copy-start.23
  313.4 3.5 copy-start.4
  346.6 29.3 %copy-start.12 = (f32[128,512]{1,0:T(8,128)S(1)}, f32[128,512]{1,0:T(8,128)}, u32[]{:S(2)}) copy-start(f32[128,512]{1,0:T(8,128)} %get-tuple-element.36) | copy-start | bytes 786436
  346.6 29.3 %copy-start.11 = (f32[128,512]{1,0:T(8,128)S(1)}, f32[128,512]{1,0:T(8,128)}, u32[]{:S(2)}) copy-start(f32[128,512]{1,0:T(8,128)} %get-tuple-element.37) | copy-start | bytes 786436
  346.7 29.4 %copy-start.10 = (f32[128,512]{1,0:T(8,128)S(1)}, f32[128,512]{1,0:T(8,128)}, u32[]{:S(2)}) copy-start(f32[128,512]{1,0:T(8,128)} %get-tuple-element.38) | copy-start | bytes 786436
  353.5 22.6 %copy-start.9 = (f32[128,512]{1,0:T(8,128)S(1)}, f32[128,512]{1,0:T(8,128)}, u32[]{:S(2)}) copy-start(f32[128,512]{1,0:T(8,128)} %get-tuple-element.39) | copy-start | bytes 786436
  353.5 22.6 %copy-start.8 = (f32[128,512]{1,0:T(8,128)S(1)}, f32[128,512]{1,0:T(8,128)}, u32[]{:S(2)}) copy-start(f32[128,512]{1,0:T(8,128)} %get-tuple-element.40) | copy-start | bytes 786436
  353.5 22.6 %copy-start.7 = (f32[128,512]{1,0:T(8,128)S(1)}, f32[128,512]{1,0:T(8,128)}, u32[]{:S(2)}) copy-start(f32[128,512]{1,0:T(8,128)} %get-tuple-element.41) | copy-start | bytes 786436
  378.7 2.8 copy-start.2
Sparse Core Ops, SparseCore 0:
  20.2 43.8 all-gather.8
  71.0 40.1 all-gather.10
  118.1 40.1 all-gather.12
  165.1 40.1 all-gather.14
  212.2 40.1 all-gather.16
  259.3 40.1 all-gather.18
  306.5 40.1 all-gather.20

commit v10 on v5

--- a/solution.py
+++ b/solution.py
@@ -50,7 +50,7 @@
         ssum_ref[...] = jnp.zeros_like(ssum_ref)
 
     w = whole_ref[...]
-    acc_ref[...] += lax.dot_general(w, trans_ref[...], NT, preferred_element_type=jnp.float32)
+    acc_ref[...] += jnp.dot(w, trans_ref[...], preferred_element_type=jnp.float32)
     ssum_ref[...] += jnp.sum(w.astype(jnp.float32), axis=1, keepdims=True)
 
     @pl.when(k == pl.num_programs(0) - 1)
@@ -63,16 +63,16 @@
         norm_ref[...] = jnp.sum(fwd_ref[...] * back, axis=1, keepdims=True)
 
 
-def backward_step(whole, transition, emit_next, fwd, tk=2048):
+def backward_step(whole, transition_t, emit_next, fwd, tk=4096):
     b, states = whole.shape
-    rows = transition.shape[0]
+    rows = transition_t.shape[1]
     full = lambda k: (0, 0)
     return pl.pallas_call(
         _step_kernel,
         grid=(states // tk,),
         in_specs=[
             pl.BlockSpec((b, tk), lambda k: (0, k)),
-            pl.BlockSpec((rows, tk), lambda k: (0, k)),
+            pl.BlockSpec((tk, rows), lambda k: (k, 0)),
             pl.BlockSpec((b, rows), full),
             pl.BlockSpec((b, rows), full),
         ],
@@ -92,7 +92,7 @@
         cost_estimate=pl.CostEstimate(
             flops=2 * b * rows * states, bytes_accessed=rows * states * 2 + b * states * 2, transcendentals=0
         ),
-    )(whole, transition, emit_next, fwd)
+    )(whole, transition_t, emit_next, fwd)
 
 
 def _transpose_kernel(x_ref, o_ref):
@@ -108,15 +108,6 @@
         out_specs=pl.BlockSpec((tile, rows), lambda j: (j, 0)),
         out_shape=jax.ShapeDtypeStruct((cols, rows), x.dtype),
     )(x)
-
-
-def backward_step_xla(whole, transition_t, emit_next, fwd):
-    product = jnp.dot(whole, transition_t, preferred_element_type=jnp.float32)
-    scale_sum = jnp.sum(whole.astype(jnp.float32), axis=1, keepdims=True)
-    backward = product / scale_sum
-    weighted = (emit_next * backward).astype(jnp.bfloat16)
-    norm_part = jnp.sum(fwd * backward, axis=1, keepdims=True)
-    return backward, weighted, scale_sum, norm_part
 
 
 def emitted_rows_xla(ids, emission):
@@ -142,7 +133,7 @@
     norms = []
     for t in range(step_count - 2, -1, -1):
         whole = lax.all_gather(weighted, "state", axis=1, tiled=True)
-        backward, weighted, scale_sum, norm_part = backward_step_xla(
+        backward, weighted, scale_sum, norm_part = backward_step(
             whole, transition_t, emitted_early[t], forward_probs[:, t, :]
         )
         vector_mat = lax.dynamic_update_slice(vector_mat, whole, (t * seq_count, 0))

time: 414 us -> 406 us (0.981)
  Pallas kernels: 35.1 us -> 76.8 us
  matrix products: 68.9 us -> 31.4 us
  other arithmetic: 17.4 us -> 2.78 us
  local copies, waits for them, and re-layouts: 28 us -> 37.9 us
  waiting for transfers between devices: 229 us -> 221 us
    pallas_call x0 -> x7, Pallas kernels: none -> 42 us  [backward_step(): pl.pallas_call(_step_kernel, grid=(states // tk,), in_specs=[pl.BlockSpec...]
    dot_general x7 -> x0, matrix products: 37.6 us -> none  [backward_step_xla(): product = jnp.dot(whole, transition_t, preferred_element_type=jnp.float32)]
    reduce_sum x8 -> x0, other arithmetic: 14.7 us -> none  [the longest x7 14.6 us: backward_step_xla(): scale_sum = jnp.sum(whole.astype(jnp.float32), axis=1, keepdims=True)]
    all_gather x7, waiting for transfers between devices: 229 us -> 221 us  [on_device(): whole = lax.all_gather(weighted, 'state', axis=1, tiled=True)]
    unnamed x44 -> x70, local copies, waits for them, and re-layouts: 8.96 us -> 9.76 us
  transfers between devices with their start and end apart: 7 -> 7, of which waited for: 7 -> 7; matrix products, arithmetic and copies ran while one was open for 4% -> 7% of each run, Pallas kernels for 8% -> 9%
where the time goes in v10:
time: 406 us; the launch traced here: 405 us
  waiting for transfers between devices  221 us (54%)
  Pallas kernels  76.8 us (19%)
  local copies, waits for them, and re-layouts  37.9 us (9%)
  matrix products  31.4 us (8%)
  blocking collectives  19.5 us (5%)
  between operations  14.4 us (4%)
    all_gather x7, waiting for transfers between devices, on_device(): whole = lax.all_gather(weighted, 'state', axis=1, tiled=True)  221 us
    pallas_call x7, Pallas kernels, backward_step(): pl.pallas_call(_step_kernel, grid=(states // tk,), in_specs=[pl.BlockSpec...  42 us
    pallas_call x1, Pallas kernels, emitted_rows(): pl.pallas_call(_emit_kernel, grid=(vocab // tv,), in_specs=[pl.BlockSpec(...  21.8 us
    dynamic_update_slice x7, local copies, waits for them, and re-layouts, on_device(): vector_mat = lax.dynamic_update_slice(vector_mat, whole, (t * seq_count, 0))  20.1 us
    all_gather x1, blocking collectives, on_device(): norm_parts = lax.all_gather(partial_norms, 'state', axis=0, tiled=False)  19.5 us
    dot_general x1, matrix products, on_device(): lax.dot_general(share_mat, vector_mat, (((0,), (0,)), ((), ())), preferre...  19.3 us
    pallas_call x1, Pallas kernels, transposed(): pl.pallas_call(_transpose_kernel, grid=(cols // tile,), in_specs=[pl.Bloc...  13 us
    dot_general x1, matrix products, emitted_rows_xla(): lax.dot_general(onehot, emission, NT, preferred_element_type=jnp.float32)  12.2 us
  transfers between devices with their start and end apart: 7, of which 7 were waited for; matrix products, arithmetic and copies ran while one was open for 7% of the time, Pallas kernels for 9%

profile of v10, /device:TPU:0, one launch (start us, length us, event | category | flops | bytes accessed | tf_op | source)
XLA Modules:
  0.0 404.8 jit_solution(7963706550690602767)
XLA Ops:
  7.2 0.0 all-gather.9.cloned.1.call-start
  7.2 0.7 slice_bitcast_fusion.1
  7.9 12.2 %fusion.3 = bf16[128,512]{1,0:T(8,128)(2,1)} fusion(bf16[512,16384]{1,0:T(8,128)(2,1)} %em_ref.1, s32[128]{0:T(128)S(1)} %slice_bitcast_fusion.1), kind=kOutput, calls=%fused_computation.6 | convolution fusion | flops 2149646336 | bytes 16908800 | tf_op jit(solution)/shard_map/dot_general | solution.py:116
  20.1 0.0 all-gather.11.cloned.1.call-start
  20.2 1.0 copy.58
  21.2 1.9 fusion.4
  23.1 0.7 copy.78
  23.8 13.0 %shard_map.59.trans_ref = bf16[8192,512]{1,0:T(8,128)(2,1)} custom-call(bf16[512,8192]{1,0:T(8,128)(2,1)} %x_ref.1), custom_call_target="tpu_custom_call" | custom-call | tf_op jit(solution)/shard_map/pallas_call | solution.py:104
  36.8 21.8 %shard_map.60 = f32[896,512]{1,0:T(8,128)} custom-call(s32[896,1]{1,0:T(8,128)} %bitcast.66, bf16[512,16384]{1,0:T(8,128)(2,1)} %em_ref.1), custom_call_target="tpu_custom_call" | custom-call | flops 15032385536 | bytes 18612224 | tf_op jit(solution)/shard_map/pallas_call | solution.py:29
  58.7 2.7 fusion.5
  61.4 2.7 all-gather.9.cloned.1.call-done.whole_ref
  64.1 5.9 %shard_map.61 = (f32[128,512]{1,0:T(8,128)}, bf16[128,512]{1,0:T(8,128)(2,1)}, f32[128,1]{1,0:T(8,128)}, f32[128,1]{1,0:T(8,128)}) custom-call(bf16[128,8192]{1,0:T(8,128)(2,1)} %all-gather.9.cloned.1.call-done.whole_ref, bf16[8192,512]{1,0:T(8,128)(2,1)} %shard_map.59.trans_ref, f32[128,512]{1,0:T(8,128)} %get-tuple-element.75.emit_ref, f32[128,512]{1,0:T(8,128)} %bitcast.60), custom_call_target="tpu_custom_call" | custom-call | flops 1073741824 | bytes 10485760 | tf_op jit(solution)/shard_map/pallas_call | solution.py:70
  70.1 0.0 all-gather.11.cloned.1.call-update
  70.1 0.0 all-gather.13.cloned.1.call-start
  70.2 0.7 copy.77
  70.9 40.8 %all-gather.11.cloned.1.call-done.whole_ref = bf16[128,8192]{1,0:T(8,128)(2,1)} async-done(((bf16[128,512]{1,0:T(8,128)(2,1)}), bf16[128,8192]{1,0:T(8,128)(2,1)}) %all-gather.11.cloned.1.call-update) | async-done | bytes 2097168 | tf_op jit(solution)/shard_map/all_gather | solution.py:135
  111.6 5.9 %shard_map.62 = (f32[128,512]{1,0:T(8,128)}, bf16[128,512]{1,0:T(8,128)(2,1)}, f32[128,1]{1,0:T(8,128)}, f32[128,1]{1,0:T(8,128)}) custom-call(bf16[128,8192]{1,0:T(8,128)(2,1)} %all-gather.11.cloned.1.call-done.whole_ref, bf16[8192,512]{1,0:T(8,128)(2,1)} %shard_map.59.trans_ref, f32[128,512]{1,0:T(8,128)} %get-tuple-element.74.emit_ref, f32[128,512]{1,0:T(8,128)} %bitcast.62), custom_call_target="tpu_custom_call" | custom-call | flops 1073741824 | bytes 10485760 | tf_op jit(solution)/shard_map/pallas_call | solution.py:70
  117.6 0.0 all-gather.13.cloned.1.call-update
  117.6 0.0 all-gather.15.cloned.1.call-start
  117.6 0.7 copy.76
  118.4 39.5 %all-gather.13.cloned.1.call-done.whole_ref = bf16[128,8192]{1,0:T(8,128)(2,1)} async-done(((bf16[128,512]{1,0:T(8,128)(2,1)}), bf16[128,8192]{1,0:T(8,128)(2,1)}) %all-gather.13.cloned.1.call-update) | async-done | bytes 2097168 | tf_op jit(solution)/shard_map/all_gather | solution.py:135
  157.9 5.9 %shard_map.63 = (f32[128,512]{1,0:T(8,128)}, bf16[128,512]{1,0:T(8,128)(2,1)}, f32[128,1]{1,0:T(8,128)}, f32[128,1]{1,0:T(8,128)}) custom-call(bf16[128,8192]{1,0:T(8,128)(2,1)} %all-gather.13.cloned.1.call-done.whole_ref, bf16[8192,512]{1,0:T(8,128)(2,1)} %shard_map.59.trans_ref, f32[128,512]{1,0:T(8,128)} %get-tuple-element.73.emit_ref, f32[128,512]{1,0:T(8,128)} %bitcast.63), custom_call_target="tpu_custom_call" | custom-call | flops 1073741824 | bytes 10485760 | tf_op jit(solution)/shard_map/pallas_call | solution.py:70
  163.8 0.0 all-gather.17.cloned.1.call-start
  163.9 0.7 copy.75
  164.6 39.5 %all-gather.15.cloned.1.call-done.whole_ref = bf16[128,8192]{1,0:T(8,128)(2,1)} async-done(((bf16[128,512]{1,0:T(8,128)(2,1)}), bf16[128,8192]{1,0:T(8,128)(2,1)}) %all-gather.15.cloned.1.call-update) | async-done | bytes 2097168 | tf_op jit(solution)/shard_map/all_gather | solution.py:135
  204.1 5.9 %shard_map.64 = (f32[128,512]{1,0:T(8,128)}, bf16[128,512]{1,0:T(8,128)(2,1)}, f32[128,1]{1,0:T(8,128)}, f32[128,1]{1,0:T(8,128)}) custom-call(bf16[128,8192]{1,0:T(8,128)(2,1)} %all-gather.15.cloned.1.call-done.whole_ref, bf16[8192,512]{1,0:T(8,128)(2,1)} %shard_map.59.trans_ref, f32[128,512]{1,0:T(8,128)} %get-tuple-element.72.emit_ref, f32[128,512]{1,0:T(8,128)} %bitcast.64), custom_call_target="tpu_custom_call" | custom-call | flops 1073741824 | bytes 10485760 | tf_op jit(solution)/shard_map/pallas_call | solution.py:70
  210.1 0.0 all-gather.19.cloned.1.call-start
  210.1 0.7 copy.74
  210.8 39.5 %all-gather.17.cloned.1.call-done.whole_ref = bf16[128,8192]{1,0:T(8,128)(2,1)} async-done(((bf16[128,512]{1,0:T(8,128)(2,1)}), bf16[128,8192]{1,0:T(8,128)(2,1)}) %all-gather.17.cloned.1.call-update) | async-done | bytes 2097168 | tf_op jit(solution)/shard_map/all_gather | solution.py:135
  250.4 6.1 %shard_map.65 = (f32[128,512]{1,0:T(8,128)}, bf16[128,512]{1,0:T(8,128)(2,1)}, f32[128,1]{1,0:T(8,128)}, f32[128,1]{1,0:T(8,128)}) custom-call(bf16[128,8192]{1,0:T(8,128)(2,1)} %all-gather.17.cloned.1.call-done.whole_ref, bf16[8192,512]{1,0:T(8,128)(2,1)} %shard_map.59.trans_ref, f32[128,512]{1,0:T(8,128)} %get-tuple-element.71.emit_ref, f32[128,512]{1,0:T(8,128)} %bitcast.65), custom_call_target="tpu_custom_call" | custom-call | flops 1073741824 | bytes 10485760 | tf_op jit(solution)/shard_map/pallas_call | solution.py:70
  256.5 0.0 all-gather.19.cloned.1.call-update
  256.5 0.2 all-gather.21.cloned.1.call-start
  256.7 0.7 copy.72
  257.4 0.7 copy.73
  258.2 0.1 copy.40
  258.2 0.1 copy.47
  258.3 7.4 %dynamic_update_slice.21 = bf16[896,8192]{1,0:T(8,128)(2,1)} pad(bf16[128,8192]{1,0:T(8,128)(2,1)S(1)} %copy-done, bf16[]{:T(256)} %constant.1.clone.1), padding=768_0x0_0 | pad | bytes 16777218 | tf_op jit(solution)/shard_map/dynamic_update_slice | solution.py:139
  265.7 31.0 %all-gather.19.cloned.1.call-done.whole_ref = bf16[128,8192]{1,0:T(8,128)(2,1)} async-done(((bf16[128,512]{1,0:T(8,128)(2,1)}), bf16[128,8192]{1,0:T(8,128)(2,1)}) %all-gather.19.cloned.1.call-update) | async-done | bytes 2097168 | tf_op jit(solution)/shard_map/all_gather | solution.py:135
  296.8 6.1 %shard_map.66 = (f32[128,512]{1,0:T(8,128)}, bf16[128,512]{1,0:T(8,128)(2,1)}, f32[128,1]{1,0:T(8,128)}, f32[128,1]{1,0:T(8,128)}) custom-call(bf16[128,8192]{1,0:T(8,128)(2,1)} %all-gather.19.cloned.1.call-done.whole_ref, bf16[8192,512]{1,0:T(8,128)(2,1)} %shard_map.59.trans_ref, f32[128,512]{1,0:T(8,128)} %get-tuple-element.70.emit_ref, f32[128,512]{1,0:T(8,128)} %bitcast.61), custom_call_target="tpu_custom_call" | custom-call | flops 1073741824 | bytes 10485760 | tf_op jit(solution)/shard_map/pallas_call | solution.py:70
  302.9 1.6 constant_dynamic-update-slice_fusion.5
  304.5 0.1 copy.39
  304.5 0.1 copy.46
  304.6 0.1 copy.38
  304.7 0.1 copy.45
  304.8 3.3 constant_dynamic-update-slice_fusion.4
  308.1 0.1 copy.37
  308.1 0.1 copy.44
  308.2 1.5 constant_dynamic-update-slice_fusion.3
  309.8 0.1 copy.36
  309.8 0.1 copy.43
  309.9 3.3 constant_dynamic-update-slice_fusion.2
  313.2 0.1 copy.35
  313.3 0.1 copy.42
  313.4 1.5 constant_dynamic-update-slice_fusion.1
  314.9 28.2 %all-gather.21.cloned.1.call-done.whole_ref = bf16[128,8192]{1,0:T(8,128)(2,1)} async-done(((bf16[128,512]{1,0:T(8,128)(2,1)}), bf16[128,8192]{1,0:T(8,128)(2,1)}) %all-gather.21.cloned.1.call-update) | async-done | bytes 2097168 | tf_op jit(solution)/shard_map/all_gather | solution.py:135
  343.1 6.0 %shard_map.67 = (f32[128,512]{1,0:T(8,128)}, bf16[128,512]{1,0:T(8,128)(2,1)}, f32[128,1]{1,0:T(8,128)}, f32[128,1]{1,0:T(8,128)}) custom-call(bf16[128,8192]{1,0:T(8,128)(2,1)} %all-gather.21.cloned.1.call-done.whole_ref, bf16[8192,512]{1,0:T(8,128)(2,1)} %shard_map.59.trans_ref, f32[128,512]{1,0:T(8,128)} %get-tuple-element.69.emit_ref, f32[128,512]{1,0:T(8,128)} %bitcast.59), custom_call_target="tpu_custom_call" | custom-call | flops 1073741824 | bytes 10485760 | tf_op jit(solution)/shard_map/pallas_call | solution.py:70
  349.2 1.0 copy.34
  350.1 0.9 copy.41
  351.1 19.5 %all-gather = f32[2048,7]{0,1:T(8,128)S(1)} all-gather(f32[128,7]{0,1:T(8,128)S(1)} %concatenate.11), channel_id=2, replica_groups=mesh['groups'=2,'state'=16] {'state'}, dimensions={0}, use_global_device_ids=true | all-gather | bytes 60928 | tf_op jit(solution)/shard_map/all_gather | solution.py:147
  370.6 1.0 bitcast_dynamic-update-slice_fusion.6
  371.9 2.5 copy.48
  374.4 2.8 fusion.2
  377.2 1.5 constant_dynamic-update-slice_fusion
  378.7 19.3 %multiply_multiply_fusion = f32[512,8192]{1,0:T(8,128)} fusion(bf16[512,8192]{1,0:T(8,128)(2,1)} %x_ref.1, bf16[896,512]{1,0:T(8,128)(2,1)S(1)} %bitcast.57, bf16[896,8192]{1,0:T(8,128)(2,1)} %constant_dynamic-update-slice_fusion), kind=kOutput, calls=%fused_computation | convolution fusion | flops 7528775680 | bytes 40763392 | tf_op jit(solution)/shard_map/dot_general | solution.py:152
  (69 shorter events, 0.4 us)
Async XLA Ops:
  7.2 57.0 %all-gather.9.cloned.1.call-start = ((), (), s32[]{:S(2)}) async-start(), calls=%async_computation | async-start | bytes 2228224 | tf_op jit(solution)/shard_map/all_gather | solution.py:135
  7.9 12.2 %copy-start.25 = (s32[128,8]{0,1:T(8,128)S(1)}, s32[128,8]{0,1:T(8,128)}, u32[]{:S(2)}) copy-start(s32[128,8]{0,1:T(8,128)} %param.5) | copy-start | bytes 12292
  7.9 13.3 %copy-start.5 = (f32[128,8,512]{2,1,0:T(8,128)S(1)}, f32[128,8,512]{2,1,0:T(8,128)}, u32[]{:S(2)}) copy-start(f32[128,8,512]{2,1,0:T(8,128)} %param.4) | copy-start | bytes 6291460
  20.1 91.5 %all-gather.11.cloned.1.call-start = ((), (), s32[]{:S(2)}) async-start(), calls=%async_computation.1 | async-start | bytes 2228224 | tf_op jit(solution)/shard_map/all_gather | solution.py:135
  64.1 6.0 %copy-start.6 = (f32[128,1,512]{2,1,0:T(1,128)S(1)}, f32[128,1,512]{2,1,0:T(1,128)}, u32[]{:S(2)}) copy-start(f32[128,1,512]{2,1,0:T(1,128)} %get-tuple-element.67) | copy-start | bytes 786436
  70.1 87.8 %all-gather.13.cloned.1.call-start = ((), (), s32[]{:S(2)}) async-start(), calls=%async_computation.2 | async-start | bytes 2228224 | tf_op jit(solution)/shard_map/all_gather | solution.py:135
  117.6 86.5 %all-gather.15.cloned.1.call-start = ((), (), s32[]{:S(2)}) async-start(), calls=%async_computation.3 | async-start | bytes 2228224 | tf_op jit(solution)/shard_map/all_gather | solution.py:135
  163.8 86.5 %all-gather.17.cloned.1.call-start = ((), (), s32[]{:S(2)}) async-start(), calls=%async_computation.4 | async-start | bytes 2228224 | tf_op jit(solution)/shard_map/all_gather | solution.py:135
  210.1 86.7 %all-gather.19.cloned.1.call-start = ((), (), s32[]{:S(2)}) async-start(), calls=%async_computation.5 | async-start | bytes 2228224 | tf_op jit(solution)/shard_map/all_gather | solution.py:135
  250.4 7.8 %copy-start.16 = (f32[128,1]{1,0:T(8,128)S(1)}, f32[128,1]{1,0:T(8,128)}, u32[]{:S(2)}) copy-start(f32[128,1]{1,0:T(8,128)} %get-tuple-element.48) | copy-start | bytes 1540
  250.4 7.9 %copy-start.15 = (f32[128,1]{1,0:T(8,128)S(1)}, f32[128,1]{1,0:T(8,128)}, u32[]{:S(2)}) copy-start(f32[128,1]{1,0:T(8,128)} %get-tuple-element.55) | copy-start | bytes 1540
  250.4 7.9 %copy-start = (bf16[128,8192]{1,0:T(8,128)(2,1)S(1)}, bf16[128,8192]{1,0:T(8,128)(2,1)}, u32[]{:S(2)}) copy-start(bf16[128,8192]{1,0:T(8,128)(2,1)} %all-gather.9.cloned.1.call-done.whole_ref) | copy-start | bytes 6291460
  256.5 86.6 %all-gather.21.cloned.1.call-start = ((), (), s32[]{:S(2)}) async-start(), calls=%async_computation.6 | async-start | bytes 2228224 | tf_op jit(solution)/shard_map/all_gather | solution.py:135
  296.7 6.1 %copy-start.1 = (bf16[128,8192]{1,0:T(8,128)(2,1)S(1)}, bf16[128,8192]{1,0:T(8,128)(2,1)}, u32[]{:S(2)}) copy-start(bf16[128,8192]{1,0:T(8,128)(2,1)} %all-gather.11.cloned.1.call-done.whole_ref) | copy-start | bytes 6291460
  302.9 1.6 copy-start.14
  302.9 1.7 copy-start.13
  302.9 1.7 copy-start.18
  302.9 1.8 copy-start.17
  304.8 3.3 copy-start.20
  304.8 3.3 copy-start.19
  304.8 3.4 copy-start.3
  308.2 1.6 copy-start.22
  308.2 1.6 copy-start.21
  309.9 3.3 copy-start.24
  309.9 3.4 copy-start.23
  309.9 3.5 copy-start.4
  343.1 28.5 %copy-start.12 = (f32[128,512]{1,0:T(8,128)S(1)}, f32[128,512]{1,0:T(8,128)}, u32[]{:S(2)}) copy-start(f32[128,512]{1,0:T(8,128)} %get-tuple-element.36) | copy-start | bytes 786436
  343.1 28.5 %copy-start.11 = (f32[128,512]{1,0:T(8,128)S(1)}, f32[128,512]{1,0:T(8,128)}, u32[]{:S(2)}) copy-start(f32[128,512]{1,0:T(8,128)} %get-tuple-element.37) | copy-start | bytes 786436
  343.1 28.6 %copy-start.10 = (f32[128,512]{1,0:T(8,128)S(1)}, f32[128,512]{1,0:T(8,128)}, u32[]{:S(2)}) copy-start(f32[128,512]{1,0:T(8,128)} %get-tuple-element.38) | copy-start | bytes 786436
  349.2 22.6 %copy-start.9 = (f32[128,512]{1,0:T(8,128)S(1)}, f32[128,512]{1,0:T(8,128)}, u32[]{:S(2)}) copy-start(f32[128,512]{1,0:T(8,128)} %get-tuple-element.39) | copy-start | bytes 786436
  349.2 22.6 %copy-start.8 = (f32[128,512]{1,0:T(8,128)S(1)}, f32[128,512]{1,0:T(8,128)}, u32[]{:S(2)}) copy-start(f32[128,512]{1,0:T(8,128)} %get-tuple-element.40) | copy-start | bytes 786436
  349.2 22.6 %copy-start.7 = (f32[128,512]{1,0:T(8,128)S(1)}, f32[128,512]{1,0:T(8,128)}, u32[]{:S(2)}) copy-start(f32[128,512]{1,0:T(8,128)} %get-tuple-element.41) | copy-start | bytes 786436
  374.4 2.8 copy-start.2
Sparse Core Ops, SparseCore 0:
  20.2 43.8 all-gather.8
  70.2 41.3 all-gather.10
  117.7 40.1 all-gather.12
  163.9 40.1 all-gather.14
  210.2 40.1 all-gather.16
  256.6 40.0 all-gather.18
  303.0 40.1 all-gather.20

commit v11 on v10

--- a/solution.py
+++ b/solution.py
@@ -63,7 +63,7 @@
         norm_ref[...] = jnp.sum(fwd_ref[...] * back, axis=1, keepdims=True)
 
 
-def backward_step(whole, transition_t, emit_next, fwd, tk=4096):
+def backward_step(whole, transition_t, emit_next, fwd, tk=2048):
     b, states = whole.shape
     rows = transition_t.shape[1]
     full = lambda k: (0, 0)

time: 406 us -> 410 us (level)
  Pallas kernels: 76.8 us -> 81.4 us
    pallas_call x7, Pallas kernels: 42 us -> 46.5 us  [backward_step(): pl.pallas_call(_step_kernel, grid=(states // tk,), in_specs=[pl.BlockSpec...]
where the time goes in v11:
time: 410 us; the launch traced here: 409 us
  waiting for transfers between devices  221 us (54%)
  Pallas kernels  81.4 us (20%)
  local copies, waits for them, and re-layouts  37.9 us (9%)
  matrix products  31.4 us (8%)
  blocking collectives  19.5 us (5%)
  between operations  14.4 us (4%)
    all_gather x7, waiting for transfers between devices, on_device(): whole = lax.all_gather(weighted, 'state', axis=1, tiled=True)  221 us
    pallas_call x7, Pallas kernels, backward_step(): pl.pallas_call(_step_kernel, grid=(states // tk,), in_specs=[pl.BlockSpec...  46.5 us
    pallas_call x1, Pallas kernels, emitted_rows(): pl.pallas_call(_emit_kernel, grid=(vocab // tv,), in_specs=[pl.BlockSpec(...  21.8 us
    dynamic_update_slice x7, local copies, waits for them, and re-layouts, on_device(): vector_mat = lax.dynamic_update_slice(vector_mat, whole, (t * seq_count, 0))  20.1 us
    all_gather x1, blocking collectives, on_device(): norm_parts = lax.all_gather(partial_norms, 'state', axis=0, tiled=False)  19.5 us
    dot_general x1, matrix products, on_device(): lax.dot_general(share_mat, vector_mat, (((0,), (0,)), ((), ())), preferre...  19.3 us
    pallas_call x1, Pallas kernels, transposed(): pl.pallas_call(_transpose_kernel, grid=(cols // tile,), in_specs=[pl.Bloc...  13 us
    dot_general x1, matrix products, emitted_rows_xla(): lax.dot_general(onehot, emission, NT, preferred_element_type=jnp.float32)  12.2 us
  transfers between devices with their start and end apart: 7, of which 7 were waited for; matrix products, arithmetic and copies ran while one was open for 7% of the time, Pallas kernels for 9%

profile of v11, /device:TPU:0, one launch (start us, length us, event | category | flops | bytes accessed | tf_op | source)
XLA Modules:
  0.0 409.3 jit_solution(1979852630045453362)
XLA Ops:
  7.2 0.0 all-gather.9.cloned.1.call-start
  7.2 0.7 slice_bitcast_fusion.1
  7.9 12.2 %fusion.3 = bf16[128,512]{1,0:T(8,128)(2,1)} fusion(bf16[512,16384]{1,0:T(8,128)(2,1)} %em_ref.1, s32[128]{0:T(128)S(1)} %slice_bitcast_fusion.1), kind=kOutput, calls=%fused_computation.6 | convolution fusion | flops 2149646336 | bytes 16908800 | tf_op jit(solution)/shard_map/dot_general | solution.py:116
  20.1 0.0 all-gather.9.cloned.1.call-update
  20.1 0.0 all-gather.11.cloned.1.call-start
  20.2 1.0 copy.58
  21.2 1.9 fusion.4
  23.1 0.7 copy.78
  23.8 13.0 %shard_map.59.trans_ref = bf16[8192,512]{1,0:T(8,128)(2,1)} custom-call(bf16[512,8192]{1,0:T(8,128)(2,1)} %x_ref.1), custom_call_target="tpu_custom_call" | custom-call | tf_op jit(solution)/shard_map/pallas_call | solution.py:104
  36.8 21.8 %shard_map.60 = f32[896,512]{1,0:T(8,128)} custom-call(s32[896,1]{1,0:T(8,128)} %bitcast.66, bf16[512,16384]{1,0:T(8,128)(2,1)} %em_ref.1), custom_call_target="tpu_custom_call" | custom-call | flops 15032385536 | bytes 18612224 | tf_op jit(solution)/shard_map/pallas_call | solution.py:29
  58.7 2.7 fusion.5
  61.4 2.7 all-gather.9.cloned.1.call-done.whole_ref
  64.1 6.6 %shard_map.61 = (f32[128,512]{1,0:T(8,128)}, bf16[128,512]{1,0:T(8,128)(2,1)}, f32[128,1]{1,0:T(8,128)}, f32[128,1]{1,0:T(8,128)}) custom-call(bf16[128,8192]{1,0:T(8,128)(2,1)} %all-gather.9.cloned.1.call-done.whole_ref, bf16[8192,512]{1,0:T(8,128)(2,1)} %shard_map.59.trans_ref, f32[128,512]{1,0:T(8,128)} %get-tuple-element.75.emit_ref, f32[128,512]{1,0:T(8,128)} %bitcast.60), custom_call_target="tpu_custom_call" | custom-call | flops 1073741824 | bytes 10485760 | tf_op jit(solution)/shard_map/pallas_call | solution.py:70
  70.7 0.0 all-gather.11.cloned.1.call-update
  70.7 0.0 all-gather.13.cloned.1.call-start
  70.8 0.7 copy.77
  71.5 40.7 %all-gather.11.cloned.1.call-done.whole_ref = bf16[128,8192]{1,0:T(8,128)(2,1)} async-done(((bf16[128,512]{1,0:T(8,128)(2,1)}), bf16[128,8192]{1,0:T(8,128)(2,1)}) %all-gather.11.cloned.1.call-update) | async-done | bytes 2097168 | tf_op jit(solution)/shard_map/all_gather | solution.py:135
  112.3 6.6 %shard_map.62 = (f32[128,512]{1,0:T(8,128)}, bf16[128,512]{1,0:T(8,128)(2,1)}, f32[128,1]{1,0:T(8,128)}, f32[128,1]{1,0:T(8,128)}) custom-call(bf16[128,8192]{1,0:T(8,128)(2,1)} %all-gather.11.cloned.1.call-done.whole_ref, bf16[8192,512]{1,0:T(8,128)(2,1)} %shard_map.59.trans_ref, f32[128,512]{1,0:T(8,128)} %get-tuple-element.74.emit_ref, f32[128,512]{1,0:T(8,128)} %bitcast.62), custom_call_target="tpu_custom_call" | custom-call | flops 1073741824 | bytes 10485760 | tf_op jit(solution)/shard_map/pallas_call | solution.py:70
  118.9 0.0 all-gather.13.cloned.1.call-update
  118.9 0.0 all-gather.15.cloned.1.call-start
  118.9 0.7 copy.76
  119.7 39.5 %all-gather.13.cloned.1.call-done.whole_ref = bf16[128,8192]{1,0:T(8,128)(2,1)} async-done(((bf16[128,512]{1,0:T(8,128)(2,1)}), bf16[128,8192]{1,0:T(8,128)(2,1)}) %all-gather.13.cloned.1.call-update) | async-done | bytes 2097168 | tf_op jit(solution)/shard_map/all_gather | solution.py:135
  159.2 6.6 %shard_map.63 = (f32[128,512]{1,0:T(8,128)}, bf16[128,512]{1,0:T(8,128)(2,1)}, f32[128,1]{1,0:T(8,128)}, f32[128,1]{1,0:T(8,128)}) custom-call(bf16[128,8192]{1,0:T(8,128)(2,1)} %all-gather.13.cloned.1.call-done.whole_ref, bf16[8192,512]{1,0:T(8,128)(2,1)} %shard_map.59.trans_ref, f32[128,512]{1,0:T(8,128)} %get-tuple-element.73.emit_ref, f32[128,512]{1,0:T(8,128)} %bitcast.63), custom_call_target="tpu_custom_call" | custom-call | flops 1073741824 | bytes 10485760 | tf_op jit(solution)/shard_map/pallas_call | solution.py:70
  165.8 0.0 all-gather.17.cloned.1.call-start
  165.8 0.7 copy.75
  166.5 39.5 %all-gather.15.cloned.1.call-done.whole_ref = bf16[128,8192]{1,0:T(8,128)(2,1)} async-done(((bf16[128,512]{1,0:T(8,128)(2,1)}), bf16[128,8192]{1,0:T(8,128)(2,1)}) %all-gather.15.cloned.1.call-update) | async-done | bytes 2097168 | tf_op jit(solution)/shard_map/all_gather | solution.py:135
  206.0 6.6 %shard_map.64 = (f32[128,512]{1,0:T(8,128)}, bf16[128,512]{1,0:T(8,128)(2,1)}, f32[128,1]{1,0:T(8,128)}, f32[128,1]{1,0:T(8,128)}) custom-call(bf16[128,8192]{1,0:T(8,128)(2,1)} %all-gather.15.cloned.1.call-done.whole_ref, bf16[8192,512]{1,0:T(8,128)(2,1)} %shard_map.59.trans_ref, f32[128,512]{1,0:T(8,128)} %get-tuple-element.72.emit_ref, f32[128,512]{1,0:T(8,128)} %bitcast.64), custom_call_target="tpu_custom_call" | custom-call | flops 1073741824 | bytes 10485760 | tf_op jit(solution)/shard_map/pallas_call | solution.py:70
  212.7 0.0 all-gather.19.cloned.1.call-start
  212.7 0.7 copy.74
  213.4 39.5 %all-gather.17.cloned.1.call-done.whole_ref = bf16[128,8192]{1,0:T(8,128)(2,1)} async-done(((bf16[128,512]{1,0:T(8,128)(2,1)}), bf16[128,8192]{1,0:T(8,128)(2,1)}) %all-gather.17.cloned.1.call-update) | async-done | bytes 2097168 | tf_op jit(solution)/shard_map/all_gather | solution.py:135
  252.9 6.7 %shard_map.65 = (f32[128,512]{1,0:T(8,128)}, bf16[128,512]{1,0:T(8,128)(2,1)}, f32[128,1]{1,0:T(8,128)}, f32[128,1]{1,0:T(8,128)}) custom-call(bf16[128,8192]{1,0:T(8,128)(2,1)} %all-gather.17.cloned.1.call-done.whole_ref, bf16[8192,512]{1,0:T(8,128)(2,1)} %shard_map.59.trans_ref, f32[128,512]{1,0:T(8,128)} %get-tuple-element.71.emit_ref, f32[128,512]{1,0:T(8,128)} %bitcast.65), custom_call_target="tpu_custom_call" | custom-call | flops 1073741824 | bytes 10485760 | tf_op jit(solution)/shard_map/pallas_call | solution.py:70
  259.7 0.2 all-gather.21.cloned.1.call-start
  259.9 0.7 copy.72
  260.7 0.7 copy.73
  261.4 0.1 copy.40
  261.4 0.1 copy.47
  261.5 7.4 %dynamic_update_slice.21 = bf16[896,8192]{1,0:T(8,128)(2,1)} pad(bf16[128,8192]{1,0:T(8,128)(2,1)S(1)} %copy-done, bf16[]{:T(256)} %constant.1.clone.1), padding=768_0x0_0 | pad | bytes 16777218 | tf_op jit(solution)/shard_map/dynamic_update_slice | solution.py:139
  268.9 31.0 %all-gather.19.cloned.1.call-done.whole_ref = bf16[128,8192]{1,0:T(8,128)(2,1)} async-done(((bf16[128,512]{1,0:T(8,128)(2,1)}), bf16[128,8192]{1,0:T(8,128)(2,1)}) %all-gather.19.cloned.1.call-update) | async-done | bytes 2097168 | tf_op jit(solution)/shard_map/all_gather | solution.py:135
  300.0 6.7 %shard_map.66 = (f32[128,512]{1,0:T(8,128)}, bf16[128,512]{1,0:T(8,128)(2,1)}, f32[128,1]{1,0:T(8,128)}, f32[128,1]{1,0:T(8,128)}) custom-call(bf16[128,8192]{1,0:T(8,128)(2,1)} %all-gather.19.cloned.1.call-done.whole_ref, bf16[8192,512]{1,0:T(8,128)(2,1)} %shard_map.59.trans_ref, f32[128,512]{1,0:T(8,128)} %get-tuple-element.70.emit_ref, f32[128,512]{1,0:T(8,128)} %bitcast.61), custom_call_target="tpu_custom_call" | custom-call | flops 1073741824 | bytes 10485760 | tf_op jit(solution)/shard_map/pallas_call | solution.py:70
  306.8 1.6 constant_dynamic-update-slice_fusion.5
  308.3 0.1 copy.39
  308.4 0.1 copy.46
  308.5 0.1 copy.38
  308.6 0.1 copy.45
  308.7 3.3 constant_dynamic-update-slice_fusion.4
  311.9 0.1 copy.37
  312.0 0.1 copy.44
  312.1 1.5 constant_dynamic-update-slice_fusion.3
  313.6 0.1 copy.36
  313.7 0.1 copy.43
  313.8 3.3 constant_dynamic-update-slice_fusion.2
  317.1 0.1 copy.35
  317.2 0.1 copy.42
  317.2 1.5 constant_dynamic-update-slice_fusion.1
  318.8 28.2 %all-gather.21.cloned.1.call-done.whole_ref = bf16[128,8192]{1,0:T(8,128)(2,1)} async-done(((bf16[128,512]{1,0:T(8,128)(2,1)}), bf16[128,8192]{1,0:T(8,128)(2,1)}) %all-gather.21.cloned.1.call-update) | async-done | bytes 2097168 | tf_op jit(solution)/shard_map/all_gather | solution.py:135
  347.0 6.7 %shard_map.67 = (f32[128,512]{1,0:T(8,128)}, bf16[128,512]{1,0:T(8,128)(2,1)}, f32[128,1]{1,0:T(8,128)}, f32[128,1]{1,0:T(8,128)}) custom-call(bf16[128,8192]{1,0:T(8,128)(2,1)} %all-gather.21.cloned.1.call-done.whole_ref, bf16[8192,512]{1,0:T(8,128)(2,1)} %shard_map.59.trans_ref, f32[128,512]{1,0:T(8,128)} %get-tuple-element.69.emit_ref, f32[128,512]{1,0:T(8,128)} %bitcast.59), custom_call_target="tpu_custom_call" | custom-call | flops 1073741824 | bytes 10485760 | tf_op jit(solution)/shard_map/pallas_call | solution.py:70
  353.7 1.0 copy.34
  354.7 0.9 copy.41
  355.6 19.5 %all-gather = f32[2048,7]{0,1:T(8,128)S(1)} all-gather(f32[128,7]{0,1:T(8,128)S(1)} %concatenate.11), channel_id=2, replica_groups=mesh['groups'=2,'state'=16] {'state'}, dimensions={0}, use_global_device_ids=true | all-gather | bytes 60928 | tf_op jit(solution)/shard_map/all_gather | solution.py:147
  375.2 1.0 bitcast_dynamic-update-slice_fusion.6
  376.4 2.5 copy.48
  379.0 2.8 fusion.2
  381.7 1.5 constant_dynamic-update-slice_fusion
  383.2 19.3 %multiply_multiply_fusion = f32[512,8192]{1,0:T(8,128)} fusion(bf16[512,8192]{1,0:T(8,128)(2,1)} %x_ref.1, bf16[896,512]{1,0:T(8,128)(2,1)S(1)} %bitcast.57, bf16[896,8192]{1,0:T(8,128)(2,1)} %constant_dynamic-update-slice_fusion), kind=kOutput, calls=%fused_computation | convolution fusion | flops 7528775680 | bytes 40763392 | tf_op jit(solution)/shard_map/dot_general | solution.py:152
  (69 shorter events, 0.4 us)
Async XLA Ops:
  7.2 57.0 %all-gather.9.cloned.1.call-start = ((), (), s32[]{:S(2)}) async-start(), calls=%async_computation | async-start | bytes 2228224 | tf_op jit(solution)/shard_map/all_gather | solution.py:135
  7.9 12.2 %copy-start.25 = (s32[128,8]{0,1:T(8,128)S(1)}, s32[128,8]{0,1:T(8,128)}, u32[]{:S(2)}) copy-start(s32[128,8]{0,1:T(8,128)} %param.5) | copy-start | bytes 12292
  7.9 13.3 %copy-start.5 = (f32[128,8,512]{2,1,0:T(8,128)S(1)}, f32[128,8,512]{2,1,0:T(8,128)}, u32[]{:S(2)}) copy-start(f32[128,8,512]{2,1,0:T(8,128)} %param.4) | copy-start | bytes 6291460
  20.1 92.2 %all-gather.11.cloned.1.call-start = ((), (), s32[]{:S(2)}) async-start(), calls=%async_computation.1 | async-start | bytes 2228224 | tf_op jit(solution)/shard_map/all_gather | solution.py:135
  64.1 6.7 %copy-start.6 = (f32[128,1,512]{2,1,0:T(1,128)S(1)}, f32[128,1,512]{2,1,0:T(1,128)}, u32[]{:S(2)}) copy-start(f32[128,1,512]{2,1,0:T(1,128)} %get-tuple-element.67) | copy-start | bytes 786436
  70.7 88.4 %all-gather.13.cloned.1.call-start = ((), (), s32[]{:S(2)}) async-start(), calls=%async_computation.2 | async-start | bytes 2228224 | tf_op jit(solution)/shard_map/all_gather | solution.py:135
  118.9 87.2 %all-gather.15.cloned.1.call-start = ((), (), s32[]{:S(2)}) async-start(), calls=%async_computation.3 | async-start | bytes 2228224 | tf_op jit(solution)/shard_map/all_gather | solution.py:135
  165.8 87.2 %all-gather.17.cloned.1.call-start = ((), (), s32[]{:S(2)}) async-start(), calls=%async_computation.4 | async-start | bytes 2228224 | tf_op jit(solution)/shard_map/all_gather | solution.py:135
  212.7 87.3 %all-gather.19.cloned.1.call-start = ((), (), s32[]{:S(2)}) async-start(), calls=%async_computation.5 | async-start | bytes 2228224 | tf_op jit(solution)/shard_map/all_gather | solution.py:135
  252.9 8.4 %copy-start.16 = (f32[128,1]{1,0:T(8,128)S(1)}, f32[128,1]{1,0:T(8,128)}, u32[]{:S(2)}) copy-start(f32[128,1]{1,0:T(8,128)} %get-tuple-element.48) | copy-start | bytes 1540
  252.9 8.5 %copy-start.15 = (f32[128,1]{1,0:T(8,128)S(1)}, f32[128,1]{1,0:T(8,128)}, u32[]{:S(2)}) copy-start(f32[128,1]{1,0:T(8,128)} %get-tuple-element.55) | copy-start | bytes 1540
  252.9 8.6 %copy-start = (bf16[128,8192]{1,0:T(8,128)(2,1)S(1)}, bf16[128,8192]{1,0:T(8,128)(2,1)}, u32[]{:S(2)}) copy-start(bf16[128,8192]{1,0:T(8,128)(2,1)} %all-gather.9.cloned.1.call-done.whole_ref) | copy-start | bytes 6291460
  259.7 87.3 %all-gather.21.cloned.1.call-start = ((), (), s32[]{:S(2)}) async-start(), calls=%async_computation.6 | async-start | bytes 2228224 | tf_op jit(solution)/shard_map/all_gather | solution.py:135
  300.0 6.8 %copy-start.1 = (bf16[128,8192]{1,0:T(8,128)(2,1)S(1)}, bf16[128,8192]{1,0:T(8,128)(2,1)}, u32[]{:S(2)}) copy-start(bf16[128,8192]{1,0:T(8,128)(2,1)} %all-gather.11.cloned.1.call-done.whole_ref) | copy-start | bytes 6291460
  306.7 1.6 copy-start.14
  306.7 1.7 copy-start.13
  306.8 1.7 copy-start.18
  306.8 1.8 copy-start.17
  308.6 3.3 copy-start.20
  308.6 3.3 copy-start.19
  308.7 3.4 copy-start.3
  312.1 1.6 copy-start.22
  312.1 1.6 copy-start.21
  313.8 3.3 copy-start.24
  313.8 3.4 copy-start.23
  313.8 3.5 copy-start.4
  347.0 29.1 %copy-start.12 = (f32[128,512]{1,0:T(8,128)S(1)}, f32[128,512]{1,0:T(8,128)}, u32[]{:S(2)}) copy-start(f32[128,512]{1,0:T(8,128)} %get-tuple-element.36) | copy-start | bytes 786436
  347.0 29.2 %copy-start.11 = (f32[128,512]{1,0:T(8,128)S(1)}, f32[128,512]{1,0:T(8,128)}, u32[]{:S(2)}) copy-start(f32[128,512]{1,0:T(8,128)} %get-tuple-element.37) | copy-start | bytes 786436
  347.0 29.2 %copy-start.10 = (f32[128,512]{1,0:T(8,128)S(1)}, f32[128,512]{1,0:T(8,128)}, u32[]{:S(2)}) copy-start(f32[128,512]{1,0:T(8,128)} %get-tuple-element.38) | copy-start | bytes 786436
  353.7 22.6 %copy-start.9 = (f32[128,512]{1,0:T(8,128)S(1)}, f32[128,512]{1,0:T(8,128)}, u32[]{:S(2)}) copy-start(f32[128,512]{1,0:T(8,128)} %get-tuple-element.39) | copy-start | bytes 786436
  353.7 22.6 %copy-start.8 = (f32[128,512]{1,0:T(8,128)S(1)}, f32[128,512]{1,0:T(8,128)}, u32[]{:S(2)}) copy-start(f32[128,512]{1,0:T(8,128)} %get-tuple-element.40) | copy-start | bytes 786436
  353.7 22.6 %copy-start.7 = (f32[128,512]{1,0:T(8,128)S(1)}, f32[128,512]{1,0:T(8,128)}, u32[]{:S(2)}) copy-start(f32[128,512]{1,0:T(8,128)} %get-tuple-element.41) | copy-start | bytes 786436
  378.9 2.8 copy-start.2
Sparse Core Ops, SparseCore 0:
  20.2 43.8 all-gather.8
  70.9 41.3 all-gather.10
  119.0 40.1 all-gather.12
  165.9 40.1 all-gather.14
  212.8 40.1 all-gather.16
  259.8 40.1 all-gather.18
  306.8 40.1 all-gather.20

commit v12 on v11

--- a/solution.py
+++ b/solution.py
@@ -63,7 +63,7 @@
         norm_ref[...] = jnp.sum(fwd_ref[...] * back, axis=1, keepdims=True)
 
 
-def backward_step(whole, transition_t, emit_next, fwd, tk=2048):
+def backward_step(whole, transition_t, emit_next, fwd, tk=8192):
     b, states = whole.shape
     rows = transition_t.shape[1]
     full = lambda k: (0, 0)

time: 410 us -> 407 us (level)
  no operation moved by 1% of the time
where the time goes in v12:
time: 407 us; the launch traced here: 406 us
  waiting for transfers between devices  221 us (54%)
  Pallas kernels  78 us (19%)
  local copies, waits for them, and re-layouts  37.9 us (9%)
  matrix products  31.4 us (8%)
  blocking collectives  19.5 us (5%)
  between operations  14.4 us (4%)
    all_gather x7, waiting for transfers between devices, on_device(): whole = lax.all_gather(weighted, 'state', axis=1, tiled=True)  221 us
    pallas_call x7, Pallas kernels, backward_step(): pl.pallas_call(_step_kernel, grid=(states // tk,), in_specs=[pl.BlockSpec...  43.1 us
    pallas_call x1, Pallas kernels, emitted_rows(): pl.pallas_call(_emit_kernel, grid=(vocab // tv,), in_specs=[pl.BlockSpec(...  21.8 us
    dynamic_update_slice x7, local copies, waits for them, and re-layouts, on_device(): vector_mat = lax.dynamic_update_slice(vector_mat, whole, (t * seq_count, 0))  20.1 us
    all_gather x1, blocking collectives, on_device(): norm_parts = lax.all_gather(partial_norms, 'state', axis=0, tiled=False)  19.5 us
    dot_general x1, matrix products, on_device(): lax.dot_general(share_mat, vector_mat, (((0,), (0,)), ((), ())), preferre...  19.3 us
    pallas_call x1, Pallas kernels, transposed(): pl.pallas_call(_transpose_kernel, grid=(cols // tile,), in_specs=[pl.Bloc...  13 us
    dot_general x1, matrix products, emitted_rows_xla(): lax.dot_general(onehot, emission, NT, preferred_element_type=jnp.float32)  12.2 us
  transfers between devices with their start and end apart: 7, of which 7 were waited for; matrix products, arithmetic and copies ran while one was open for 7% of the time, Pallas kernels for 9%

profile of v12, /device:TPU:0, one launch (start us, length us, event | category | flops | bytes accessed | tf_op | source)
XLA Modules:
  0.0 406.0 jit_solution(8166594508150648377)
XLA Ops:
  7.2 0.0 all-gather.9.cloned.1.call-start
  7.2 0.7 slice_bitcast_fusion.1
  7.9 12.2 %fusion.3 = bf16[128,512]{1,0:T(8,128)(2,1)} fusion(bf16[512,16384]{1,0:T(8,128)(2,1)} %em_ref.1, s32[128]{0:T(128)S(1)} %slice_bitcast_fusion.1), kind=kOutput, calls=%fused_computation.6 | convolution fusion | flops 2149646336 | bytes 16908800 | tf_op jit(solution)/shard_map/dot_general | solution.py:116
  20.1 0.0 all-gather.9.cloned.1.call-update
  20.1 0.0 all-gather.11.cloned.1.call-start
  20.2 1.0 copy.58
  21.2 1.9 fusion.4
  23.1 0.7 copy.78
  23.8 13.0 %shard_map.59.trans_ref = bf16[8192,512]{1,0:T(8,128)(2,1)} custom-call(bf16[512,8192]{1,0:T(8,128)(2,1)} %x_ref.1), custom_call_target="tpu_custom_call" | custom-call | tf_op jit(solution)/shard_map/pallas_call | solution.py:104
  36.8 21.8 %shard_map.60 = f32[896,512]{1,0:T(8,128)} custom-call(s32[896,1]{1,0:T(8,128)} %bitcast.66, bf16[512,16384]{1,0:T(8,128)(2,1)} %em_ref.1), custom_call_target="tpu_custom_call" | custom-call | flops 15032385536 | bytes 18612224 | tf_op jit(solution)/shard_map/pallas_call | solution.py:29
  58.7 2.7 fusion.5
  61.4 2.7 all-gather.9.cloned.1.call-done.whole_ref
  64.1 6.1 %shard_map.61 = (f32[128,512]{1,0:T(8,128)}, bf16[128,512]{1,0:T(8,128)(2,1)}, f32[128,1]{1,0:T(8,128)}, f32[128,1]{1,0:T(8,128)}) custom-call(bf16[128,8192]{1,0:T(8,128)(2,1)} %all-gather.9.cloned.1.call-done.whole_ref, bf16[8192,512]{1,0:T(8,128)(2,1)} %shard_map.59.trans_ref, f32[128,512]{1,0:T(8,128)} %get-tuple-element.75.emit_ref, f32[128,512]{1,0:T(8,128)} %bitcast.60), custom_call_target="tpu_custom_call" | custom-call | flops 1073741824 | bytes 10485760 | tf_op jit(solution)/shard_map/pallas_call | solution.py:70
  70.2 0.0 all-gather.11.cloned.1.call-update
  70.3 0.0 all-gather.13.cloned.1.call-start
  70.3 0.7 copy.77
  71.0 40.7 %all-gather.11.cloned.1.call-done.whole_ref = bf16[128,8192]{1,0:T(8,128)(2,1)} async-done(((bf16[128,512]{1,0:T(8,128)(2,1)}), bf16[128,8192]{1,0:T(8,128)(2,1)}) %all-gather.11.cloned.1.call-update) | async-done | bytes 2097168 | tf_op jit(solution)/shard_map/all_gather | solution.py:135
  111.8 6.1 %shard_map.62 = (f32[128,512]{1,0:T(8,128)}, bf16[128,512]{1,0:T(8,128)(2,1)}, f32[128,1]{1,0:T(8,128)}, f32[128,1]{1,0:T(8,128)}) custom-call(bf16[128,8192]{1,0:T(8,128)(2,1)} %all-gather.11.cloned.1.call-done.whole_ref, bf16[8192,512]{1,0:T(8,128)(2,1)} %shard_map.59.trans_ref, f32[128,512]{1,0:T(8,128)} %get-tuple-element.74.emit_ref, f32[128,512]{1,0:T(8,128)} %bitcast.62), custom_call_target="tpu_custom_call" | custom-call | flops 1073741824 | bytes 10485760 | tf_op jit(solution)/shard_map/pallas_call | solution.py:70
  117.9 0.0 all-gather.13.cloned.1.call-update
  117.9 0.0 all-gather.15.cloned.1.call-start
  118.0 0.7 copy.76
  118.7 39.5 %all-gather.13.cloned.1.call-done.whole_ref = bf16[128,8192]{1,0:T(8,128)(2,1)} async-done(((bf16[128,512]{1,0:T(8,128)(2,1)}), bf16[128,8192]{1,0:T(8,128)(2,1)}) %all-gather.13.cloned.1.call-update) | async-done | bytes 2097168 | tf_op jit(solution)/shard_map/all_gather | solution.py:135
  158.2 6.1 %shard_map.63 = (f32[128,512]{1,0:T(8,128)}, bf16[128,512]{1,0:T(8,128)(2,1)}, f32[128,1]{1,0:T(8,128)}, f32[128,1]{1,0:T(8,128)}) custom-call(bf16[128,8192]{1,0:T(8,128)(2,1)} %all-gather.13.cloned.1.call-done.whole_ref, bf16[8192,512]{1,0:T(8,128)(2,1)} %shard_map.59.trans_ref, f32[128,512]{1,0:T(8,128)} %get-tuple-element.73.emit_ref, f32[128,512]{1,0:T(8,128)} %bitcast.63), custom_call_target="tpu_custom_call" | custom-call | flops 1073741824 | bytes 10485760 | tf_op jit(solution)/shard_map/pallas_call | solution.py:70
  164.3 0.0 all-gather.17.cloned.1.call-start
  164.4 0.7 copy.75
  165.1 39.5 %all-gather.15.cloned.1.call-done.whole_ref = bf16[128,8192]{1,0:T(8,128)(2,1)} async-done(((bf16[128,512]{1,0:T(8,128)(2,1)}), bf16[128,8192]{1,0:T(8,128)(2,1)}) %all-gather.15.cloned.1.call-update) | async-done | bytes 2097168 | tf_op jit(solution)/shard_map/all_gather | solution.py:135
  204.6 6.1 %shard_map.64 = (f32[128,512]{1,0:T(8,128)}, bf16[128,512]{1,0:T(8,128)(2,1)}, f32[128,1]{1,0:T(8,128)}, f32[128,1]{1,0:T(8,128)}) custom-call(bf16[128,8192]{1,0:T(8,128)(2,1)} %all-gather.15.cloned.1.call-done.whole_ref, bf16[8192,512]{1,0:T(8,128)(2,1)} %shard_map.59.trans_ref, f32[128,512]{1,0:T(8,128)} %get-tuple-element.72.emit_ref, f32[128,512]{1,0:T(8,128)} %bitcast.64), custom_call_target="tpu_custom_call" | custom-call | flops 1073741824 | bytes 10485760 | tf_op jit(solution)/shard_map/pallas_call | solution.py:70
  210.7 0.2 all-gather.19.cloned.1.call-start
  211.0 0.7 copy.74
  211.7 39.3 %all-gather.17.cloned.1.call-done.whole_ref = bf16[128,8192]{1,0:T(8,128)(2,1)} async-done(((bf16[128,512]{1,0:T(8,128)(2,1)}), bf16[128,8192]{1,0:T(8,128)(2,1)}) %all-gather.17.cloned.1.call-update) | async-done | bytes 2097168 | tf_op jit(solution)/shard_map/all_gather | solution.py:135
  251.0 6.3 %shard_map.65 = (f32[128,512]{1,0:T(8,128)}, bf16[128,512]{1,0:T(8,128)(2,1)}, f32[128,1]{1,0:T(8,128)}, f32[128,1]{1,0:T(8,128)}) custom-call(bf16[128,8192]{1,0:T(8,128)(2,1)} %all-gather.17.cloned.1.call-done.whole_ref, bf16[8192,512]{1,0:T(8,128)(2,1)} %shard_map.59.trans_ref, f32[128,512]{1,0:T(8,128)} %get-tuple-element.71.emit_ref, f32[128,512]{1,0:T(8,128)} %bitcast.65), custom_call_target="tpu_custom_call" | custom-call | flops 1073741824 | bytes 10485760 | tf_op jit(solution)/shard_map/pallas_call | solution.py:70
  257.3 0.0 all-gather.21.cloned.1.call-start
  257.4 0.7 copy.72
  258.1 0.7 copy.73
  258.8 0.1 copy.40
  258.9 0.1 copy.47
  258.9 7.4 %dynamic_update_slice.21 = bf16[896,8192]{1,0:T(8,128)(2,1)} pad(bf16[128,8192]{1,0:T(8,128)(2,1)S(1)} %copy-done, bf16[]{:T(256)} %constant.1.clone.1), padding=768_0x0_0 | pad | bytes 16777218 | tf_op jit(solution)/shard_map/dynamic_update_slice | solution.py:139
  266.4 31.2 %all-gather.19.cloned.1.call-done.whole_ref = bf16[128,8192]{1,0:T(8,128)(2,1)} async-done(((bf16[128,512]{1,0:T(8,128)(2,1)}), bf16[128,8192]{1,0:T(8,128)(2,1)}) %all-gather.19.cloned.1.call-update) | async-done | bytes 2097168 | tf_op jit(solution)/shard_map/all_gather | solution.py:135
  297.6 6.3 %shard_map.66 = (f32[128,512]{1,0:T(8,128)}, bf16[128,512]{1,0:T(8,128)(2,1)}, f32[128,1]{1,0:T(8,128)}, f32[128,1]{1,0:T(8,128)}) custom-call(bf16[128,8192]{1,0:T(8,128)(2,1)} %all-gather.19.cloned.1.call-done.whole_ref, bf16[8192,512]{1,0:T(8,128)(2,1)} %shard_map.59.trans_ref, f32[128,512]{1,0:T(8,128)} %get-tuple-element.70.emit_ref, f32[128,512]{1,0:T(8,128)} %bitcast.61), custom_call_target="tpu_custom_call" | custom-call | flops 1073741824 | bytes 10485760 | tf_op jit(solution)/shard_map/pallas_call | solution.py:70
  303.9 1.6 constant_dynamic-update-slice_fusion.5
  305.5 0.1 copy.39
  305.5 0.1 copy.46
  305.6 0.1 copy.38
  305.7 0.1 copy.45
  305.8 3.3 constant_dynamic-update-slice_fusion.4
  309.1 0.1 copy.37
  309.1 0.1 copy.44
  309.2 1.5 constant_dynamic-update-slice_fusion.3
  310.8 0.1 copy.36
  310.9 0.1 copy.43
  310.9 3.3 constant_dynamic-update-slice_fusion.2
  314.2 0.1 copy.35
  314.3 0.1 copy.42
  314.4 1.5 constant_dynamic-update-slice_fusion.1
  315.9 28.2 %all-gather.21.cloned.1.call-done.whole_ref = bf16[128,8192]{1,0:T(8,128)(2,1)} async-done(((bf16[128,512]{1,0:T(8,128)(2,1)}), bf16[128,8192]{1,0:T(8,128)(2,1)}) %all-gather.21.cloned.1.call-update) | async-done | bytes 2097168 | tf_op jit(solution)/shard_map/all_gather | solution.py:135
  344.2 6.2 %shard_map.67 = (f32[128,512]{1,0:T(8,128)}, bf16[128,512]{1,0:T(8,128)(2,1)}, f32[128,1]{1,0:T(8,128)}, f32[128,1]{1,0:T(8,128)}) custom-call(bf16[128,8192]{1,0:T(8,128)(2,1)} %all-gather.21.cloned.1.call-done.whole_ref, bf16[8192,512]{1,0:T(8,128)(2,1)} %shard_map.59.trans_ref, f32[128,512]{1,0:T(8,128)} %get-tuple-element.69.emit_ref, f32[128,512]{1,0:T(8,128)} %bitcast.59), custom_call_target="tpu_custom_call" | custom-call | flops 1073741824 | bytes 10485760 | tf_op jit(solution)/shard_map/pallas_call | solution.py:70
  350.3 1.0 copy.34
  351.3 0.9 copy.41
  352.3 19.5 %all-gather = f32[2048,7]{0,1:T(8,128)S(1)} all-gather(f32[128,7]{0,1:T(8,128)S(1)} %concatenate.11), channel_id=2, replica_groups=mesh['groups'=2,'state'=16] {'state'}, dimensions={0}, use_global_device_ids=true | all-gather | bytes 60928 | tf_op jit(solution)/shard_map/all_gather | solution.py:147
  371.8 1.0 bitcast_dynamic-update-slice_fusion.6
  373.0 2.5 copy.48
  375.6 2.8 fusion.2
  378.4 1.5 constant_dynamic-update-slice_fusion
  379.9 19.3 %multiply_multiply_fusion = f32[512,8192]{1,0:T(8,128)} fusion(bf16[512,8192]{1,0:T(8,128)(2,1)} %x_ref.1, bf16[896,512]{1,0:T(8,128)(2,1)S(1)} %bitcast.57, bf16[896,8192]{1,0:T(8,128)(2,1)} %constant_dynamic-update-slice_fusion), kind=kOutput, calls=%fused_computation | convolution fusion | flops 7528775680 | bytes 40763392 | tf_op jit(solution)/shard_map/dot_general | solution.py:152
  (69 shorter events, 0.4 us)
Async XLA Ops:
  7.2 57.0 %all-gather.9.cloned.1.call-start = ((), (), s32[]{:S(2)}) async-start(), calls=%async_computation | async-start | bytes 2228224 | tf_op jit(solution)/shard_map/all_gather | solution.py:135
  7.9 12.2 %copy-start.25 = (s32[128,8]{0,1:T(8,128)S(1)}, s32[128,8]{0,1:T(8,128)}, u32[]{:S(2)}) copy-start(s32[128,8]{0,1:T(8,128)} %param.5) | copy-start | bytes 12292
  7.9 13.3 %copy-start.5 = (f32[128,8,512]{2,1,0:T(8,128)S(1)}, f32[128,8,512]{2,1,0:T(8,128)}, u32[]{:S(2)}) copy-start(f32[128,8,512]{2,1,0:T(8,128)} %param.4) | copy-start | bytes 6291460
  20.1 91.7 %all-gather.11.cloned.1.call-start = ((), (), s32[]{:S(2)}) async-start(), calls=%async_computation.1 | async-start | bytes 2228224 | tf_op jit(solution)/shard_map/all_gather | solution.py:135
  64.1 6.2 %copy-start.6 = (f32[128,1,512]{2,1,0:T(1,128)S(1)}, f32[128,1,512]{2,1,0:T(1,128)}, u32[]{:S(2)}) copy-start(f32[128,1,512]{2,1,0:T(1,128)} %get-tuple-element.67) | copy-start | bytes 786436
  70.3 87.9 %all-gather.13.cloned.1.call-start = ((), (), s32[]{:S(2)}) async-start(), calls=%async_computation.2 | async-start | bytes 2228224 | tf_op jit(solution)/shard_map/all_gather | solution.py:135
  117.9 86.7 %all-gather.15.cloned.1.call-start = ((), (), s32[]{:S(2)}) async-start(), calls=%async_computation.3 | async-start | bytes 2228224 | tf_op jit(solution)/shard_map/all_gather | solution.py:135
  164.3 86.7 %all-gather.17.cloned.1.call-start = ((), (), s32[]{:S(2)}) async-start(), calls=%async_computation.4 | async-start | bytes 2228224 | tf_op jit(solution)/shard_map/all_gather | solution.py:135
  210.7 86.9 %all-gather.19.cloned.1.call-start = ((), (), s32[]{:S(2)}) async-start(), calls=%async_computation.5 | async-start | bytes 2228224 | tf_op jit(solution)/shard_map/all_gather | solution.py:135
  251.0 7.8 %copy-start.16 = (f32[128,1]{1,0:T(8,128)S(1)}, f32[128,1]{1,0:T(8,128)}, u32[]{:S(2)}) copy-start(f32[128,1]{1,0:T(8,128)} %get-tuple-element.48) | copy-start | bytes 1540
  251.0 7.9 %copy-start.15 = (f32[128,1]{1,0:T(8,128)S(1)}, f32[128,1]{1,0:T(8,128)}, u32[]{:S(2)}) copy-start(f32[128,1]{1,0:T(8,128)} %get-tuple-element.55) | copy-start | bytes 1540
  251.0 7.9 %copy-start = (bf16[128,8192]{1,0:T(8,128)(2,1)S(1)}, bf16[128,8192]{1,0:T(8,128)(2,1)}, u32[]{:S(2)}) copy-start(bf16[128,8192]{1,0:T(8,128)(2,1)} %all-gather.9.cloned.1.call-done.whole_ref) | copy-start | bytes 6291460
  257.3 86.8 %all-gather.21.cloned.1.call-start = ((), (), s32[]{:S(2)}) async-start(), calls=%async_computation.6 | async-start | bytes 2228224 | tf_op jit(solution)/shard_map/all_gather | solution.py:135
  297.6 6.3 %copy-start.1 = (bf16[128,8192]{1,0:T(8,128)(2,1)S(1)}, bf16[128,8192]{1,0:T(8,128)(2,1)}, u32[]{:S(2)}) copy-start(bf16[128,8192]{1,0:T(8,128)(2,1)} %all-gather.11.cloned.1.call-done.whole_ref) | copy-start | bytes 6291460
  303.9 1.6 copy-start.14
  303.9 1.7 copy-start.13
  303.9 1.7 copy-start.18
  303.9 1.8 copy-start.17
  305.8 3.3 copy-start.20
  305.8 3.3 copy-start.19
  305.8 3.4 copy-start.3
  309.2 1.6 copy-start.22
  309.2 1.6 copy-start.21
  310.9 3.3 copy-start.24
  310.9 3.4 copy-start.23
  310.9 3.5 copy-start.4
  344.1 28.6 %copy-start.12 = (f32[128,512]{1,0:T(8,128)S(1)}, f32[128,512]{1,0:T(8,128)}, u32[]{:S(2)}) copy-start(f32[128,512]{1,0:T(8,128)} %get-tuple-element.36) | copy-start | bytes 786436
  344.1 28.7 %copy-start.11 = (f32[128,512]{1,0:T(8,128)S(1)}, f32[128,512]{1,0:T(8,128)}, u32[]{:S(2)}) copy-start(f32[128,512]{1,0:T(8,128)} %get-tuple-element.37) | copy-start | bytes 786436
  344.1 28.7 %copy-start.10 = (f32[128,512]{1,0:T(8,128)S(1)}, f32[128,512]{1,0:T(8,128)}, u32[]{:S(2)}) copy-start(f32[128,512]{1,0:T(8,128)} %get-tuple-element.38) | copy-start | bytes 786436
  350.3 22.6 %copy-start.9 = (f32[128,512]{1,0:T(8,128)S(1)}, f32[128,512]{1,0:T(8,128)}, u32[]{:S(2)}) copy-start(f32[128,512]{1,0:T(8,128)} %get-tuple-element.39) | copy-start | bytes 786436
  350.3 22.6 %copy-start.8 = (f32[128,512]{1,0:T(8,128)S(1)}, f32[128,512]{1,0:T(8,128)}, u32[]{:S(2)}) copy-start(f32[128,512]{1,0:T(8,128)} %get-tuple-element.40) | copy-start | bytes 786436
  350.3 22.6 %copy-start.7 = (f32[128,512]{1,0:T(8,128)S(1)}, f32[128,512]{1,0:T(8,128)}, u32[]{:S(2)}) copy-start(f32[128,512]{1,0:T(8,128)} %get-tuple-element.41) | copy-start | bytes 786436
  375.6 2.8 copy-start.2
Sparse Core Ops, SparseCore 0:
  20.2 43.8 all-gather.8
  70.4 41.3 all-gather.10
  118.0 40.1 all-gather.12
  164.5 40.1 all-gather.14
  210.9 40.1 all-gather.16
  257.4 40.1 all-gather.18
  304.0 40.1 all-gather.20

commit v13 on v12

--- a/solution.py
+++ b/solution.py
@@ -41,7 +41,7 @@
     )(ids.reshape(n, 1), emission)
 
 
-def _step_kernel(whole_ref, trans_ref, emit_ref, fwd_ref, back_ref, wnext_ref, scale_ref, norm_ref, acc_ref, ssum_ref):
+def _step_kernel(whole_ref, trans_ref, emit_ref, back_ref, wnext_ref, scale_ref, acc_ref, ssum_ref):
     k = pl.program_id(0)
 
     @pl.when(k == 0)
@@ -60,10 +60,9 @@
         back_ref[...] = back
         wnext_ref[...] = (emit_ref[...] * back).astype(wnext_ref.dtype)
         scale_ref[...] = s
-        norm_ref[...] = jnp.sum(fwd_ref[...] * back, axis=1, keepdims=True)
 
 
-def backward_step(whole, transition_t, emit_next, fwd, tk=8192):
+def backward_step(whole, transition_t, emit_next, tk=4096):
     b, states = whole.shape
     rows = transition_t.shape[1]
     full = lambda k: (0, 0)
@@ -74,25 +73,22 @@
             pl.BlockSpec((b, tk), lambda k: (0, k)),
             pl.BlockSpec((tk, rows), lambda k: (k, 0)),
             pl.BlockSpec((b, rows), full),
-            pl.BlockSpec((b, rows), full),
         ],
         out_specs=[
             pl.BlockSpec((b, rows), full),
             pl.BlockSpec((b, rows), full),
-            pl.BlockSpec((b, 1), full),
             pl.BlockSpec((b, 1), full),
         ],
         out_shape=[
             jax.ShapeDtypeStruct((b, rows), jnp.float32),
             jax.ShapeDtypeStruct((b, rows), jnp.bfloat16),
             jax.ShapeDtypeStruct((b, 1), jnp.float32),
-            jax.ShapeDtypeStruct((b, 1), jnp.float32),
         ],
         scratch_shapes=[pltpu.VMEM((b, rows), jnp.float32), pltpu.VMEM((b, 1), jnp.float32)],
         cost_estimate=pl.CostEstimate(
             flops=2 * b * rows * states, bytes_accessed=rows * states * 2 + b * states * 2, transcendentals=0
         ),
-    )(whole, transition_t, emit_next, fwd)
+    )(whole, transition_t, emit_next)
 
 
 def _transpose_kernel(x_ref, o_ref):
@@ -133,9 +129,8 @@
     norms = []
     for t in range(step_count - 2, -1, -1):
         whole = lax.all_gather(weighted, "state", axis=1, tiled=True)
-        backward, weighted, scale_sum, norm_part = backward_step(
-            whole, transition_t, emitted_early[t], forward_probs[:, t, :]
-        )
+        backward, weighted, scale_sum = backward_step(whole, transition_t, emitted_early[t])
+        norm_part = jnp.sum(forward_probs[:, t, :] * backward, axis=1, keepdims=True)
         vector_mat = lax.dynamic_update_slice(vector_mat, whole, (t * seq_count, 0))
         scales.append(scale_sum)
         backs.append(backward)

time: 407 us -> 406 us (level)
  waiting for transfers between devices: 221 us -> 216 us
    slice x1, local copies, waits for them, and re-layouts: 1.91 us -> 8.8 us  [on_device(): forward_probs[:, t, :] * backward]
    all_gather x7, waiting for transfers between devices: 221 us -> 216 us  [on_device(): whole = lax.all_gather(weighted, 'state', axis=1, tiled=True)]
    unnamed x70 -> x51, local copies, waits for them, and re-layouts: 9.76 us -> 6.71 us
  transfers between devices with their start and end apart: 7 -> 7, of which waited for: 7 -> 7; matrix products, arithmetic and copies ran while one was open for 7% -> 9% of each run, Pallas kernels for 9% -> 9%
where the time goes in v13:
time: 406 us; the launch traced here: 404 us
  waiting for transfers between devices  216 us (53%)
  Pallas kernels  75.2 us (19%)
  local copies, waits for them, and re-layouts  41.9 us (10%)
  matrix products  31.3 us (8%)
  blocking collectives  19.7 us (5%)
  between operations  14.4 us (4%)
  other arithmetic  5.64 us (1%)
    all_gather x7, waiting for transfers between devices, on_device(): whole = lax.all_gather(weighted, 'state', axis=1, tiled=True)  216 us
    pallas_call x7, Pallas kernels, backward_step(): pl.pallas_call(_step_kernel, grid=(states // tk,), in_specs=[pl.BlockSpec...  40.3 us
    pallas_call x1, Pallas kernels, emitted_rows(): pl.pallas_call(_emit_kernel, grid=(vocab // tv,), in_specs=[pl.BlockSpec(...  21.8 us
    dynamic_update_slice x7, local copies, waits for them, and re-layouts, on_device(): vector_mat = lax.dynamic_update_slice(vector_mat, whole, (t * seq_count, 0))  21.6 us
    all_gather x1, blocking collectives, on_device(): norm_parts = lax.all_gather(partial_norms, 'state', axis=0, tiled=False)  19.7 us
    dot_general x1, matrix products, on_device(): lax.dot_general(share_mat, vector_mat, (((0,), (0,)), ((), ())), preferre...  19.3 us
    pallas_call x1, Pallas kernels, transposed(): pl.pallas_call(_transpose_kernel, grid=(cols // tile,), in_specs=[pl.Bloc...  13.1 us
    dot_general x1, matrix products, emitted_rows_xla(): lax.dot_general(onehot, emission, NT, preferred_element_type=jnp.float32)  12 us
  transfers between devices with their start and end apart: 7, of which 7 were waited for; matrix products, arithmetic and copies ran while one was open for 9% of the time, Pallas kernels for 9%

profile of v13, /device:TPU:0, one launch (start us, length us, event | category | flops | bytes accessed | tf_op | source)
XLA Modules:
  0.0 404.5 jit_solution(8450831710793927673)
XLA Ops:
  7.2 0.0 all-gather.9.cloned.1.call-start
  7.2 0.7 slice_bitcast_fusion.1
  7.9 12.0 %fusion.3 = bf16[128,512]{1,0:T(8,128)(2,1)} fusion(bf16[512,16384]{1,0:T(8,128)(2,1)} %em_ref.1, s32[128]{0:T(128)S(1)} %slice_bitcast_fusion.1), kind=kOutput, calls=%fused_computation.6 | convolution fusion | flops 2149646336 | bytes 16908800 | tf_op jit(solution)/shard_map/dot_general | solution.py:112
  19.9 0.0 all-gather.9.cloned.1.call-update
  20.0 0.0 all-gather.11.cloned.1.call-start
  20.0 13.1 %shard_map.59.trans_ref = bf16[8192,512]{1,0:T(8,128)(2,1)} custom-call(bf16[512,8192]{1,0:T(8,128)(2,1)} %x_ref.1), custom_call_target="tpu_custom_call" | custom-call | tf_op jit(solution)/shard_map/pallas_call | solution.py:100
  33.1 1.0 copy.51
  34.1 21.8 %shard_map.60 = f32[896,512]{1,0:T(8,128)} custom-call(s32[896,1]{1,0:T(8,128)} %bitcast.87, bf16[512,16384]{1,0:T(8,128)(2,1)} %em_ref.1), custom_call_target="tpu_custom_call" | custom-call | flops 15032385536 | bytes 18612224 | tf_op jit(solution)/shard_map/pallas_call | solution.py:29
  55.9 2.8 fusion.19
  58.7 5.3 %all-gather.9.cloned.1.call-done.whole_ref = bf16[128,8192]{1,0:T(8,128)(2,1)} async-done(((bf16[128,512]{1,0:T(8,128)(2,1)}), bf16[128,8192]{1,0:T(8,128)(2,1)}) %all-gather.9.cloned.1.call-update) | async-done | bytes 2097168 | tf_op jit(solution)/shard_map/all_gather | solution.py:131
  64.0 5.7 %shard_map.61 = (f32[128,512]{1,0:T(8,128)}, bf16[128,512]{1,0:T(8,128)(2,1)}, f32[128,1]{1,0:T(8,128)}) custom-call(bf16[128,8192]{1,0:T(8,128)(2,1)} %all-gather.9.cloned.1.call-done.whole_ref, bf16[8192,512]{1,0:T(8,128)(2,1)} %shard_map.59.trans_ref, f32[128,512]{1,0:T(8,128)} %get-tuple-element.61.emit_ref), custom_call_target="tpu_custom_call" | custom-call | flops 1073741824 | bytes 10485760 | tf_op jit(solution)/shard_map/pallas_call | solution.py:69
  69.7 0.0 all-gather.11.cloned.1.call-update
  69.8 0.0 all-gather.13.cloned.1.call-start
  69.8 40.7 %all-gather.11.cloned.1.call-done.whole_ref = bf16[128,8192]{1,0:T(8,128)(2,1)} async-done(((bf16[128,512]{1,0:T(8,128)(2,1)}), bf16[128,8192]{1,0:T(8,128)(2,1)}) %all-gather.11.cloned.1.call-update) | async-done | bytes 2097168 | tf_op jit(solution)/shard_map/all_gather | solution.py:131
  110.5 5.8 %shard_map.62 = (f32[128,512]{1,0:T(8,128)}, bf16[128,512]{1,0:T(8,128)(2,1)}, f32[128,1]{1,0:T(8,128)}) custom-call(bf16[128,8192]{1,0:T(8,128)(2,1)} %all-gather.11.cloned.1.call-done.whole_ref, bf16[8192,512]{1,0:T(8,128)(2,1)} %shard_map.59.trans_ref, f32[128,512]{1,0:T(8,128)} %get-tuple-element.60.emit_ref), custom_call_target="tpu_custom_call" | custom-call | flops 1073741824 | bytes 10485760 | tf_op jit(solution)/shard_map/pallas_call | solution.py:69
  116.2 0.0 all-gather.13.cloned.1.call-update
  116.2 0.0 all-gather.15.cloned.1.call-start
  116.3 40.2 %all-gather.13.cloned.1.call-done.whole_ref = bf16[128,8192]{1,0:T(8,128)(2,1)} async-done(((bf16[128,512]{1,0:T(8,128)(2,1)}), bf16[128,8192]{1,0:T(8,128)(2,1)}) %all-gather.13.cloned.1.call-update) | async-done | bytes 2097168 | tf_op jit(solution)/shard_map/all_gather | solution.py:131
  156.5 5.7 %shard_map.63 = (f32[128,512]{1,0:T(8,128)}, bf16[128,512]{1,0:T(8,128)(2,1)}, f32[128,1]{1,0:T(8,128)}) custom-call(bf16[128,8192]{1,0:T(8,128)(2,1)} %all-gather.13.cloned.1.call-done.whole_ref, bf16[8192,512]{1,0:T(8,128)(2,1)} %shard_map.59.trans_ref, f32[128,512]{1,0:T(8,128)} %get-tuple-element.59.emit_ref), custom_call_target="tpu_custom_call" | custom-call | flops 1073741824 | bytes 10485760 | tf_op jit(solution)/shard_map/pallas_call | solution.py:69
  162.3 0.0 all-gather.15.cloned.1.call-update
  162.3 0.0 all-gather.17.cloned.1.call-start
  162.3 40.2 %all-gather.15.cloned.1.call-done.whole_ref = bf16[128,8192]{1,0:T(8,128)(2,1)} async-done(((bf16[128,512]{1,0:T(8,128)(2,1)}), bf16[128,8192]{1,0:T(8,128)(2,1)}) %all-gather.15.cloned.1.call-update) | async-done | bytes 2097168 | tf_op jit(solution)/shard_map/all_gather | solution.py:131
  202.6 5.7 %shard_map.64 = (f32[128,512]{1,0:T(8,128)}, bf16[128,512]{1,0:T(8,128)(2,1)}, f32[128,1]{1,0:T(8,128)}) custom-call(bf16[128,8192]{1,0:T(8,128)(2,1)} %all-gather.15.cloned.1.call-done.whole_ref, bf16[8192,512]{1,0:T(8,128)(2,1)} %shard_map.59.trans_ref, f32[128,512]{1,0:T(8,128)} %get-tuple-element.58.emit_ref), custom_call_target="tpu_custom_call" | custom-call | flops 1073741824 | bytes 10485760 | tf_op jit(solution)/shard_map/pallas_call | solution.py:69
  208.3 0.0 all-gather.17.cloned.1.call-update
  208.3 0.0 all-gather.19.cloned.1.call-start
  208.4 40.2 %all-gather.17.cloned.1.call-done.whole_ref = bf16[128,8192]{1,0:T(8,128)(2,1)} async-done(((bf16[128,512]{1,0:T(8,128)(2,1)}), bf16[128,8192]{1,0:T(8,128)(2,1)}) %all-gather.17.cloned.1.call-update) | async-done | bytes 2097168 | tf_op jit(solution)/shard_map/all_gather | solution.py:131
  248.6 5.7 %shard_map.65 = (f32[128,512]{1,0:T(8,128)}, bf16[128,512]{1,0:T(8,128)(2,1)}, f32[128,1]{1,0:T(8,128)}) custom-call(bf16[128,8192]{1,0:T(8,128)(2,1)} %all-gather.17.cloned.1.call-done.whole_ref, bf16[8192,512]{1,0:T(8,128)(2,1)} %shard_map.59.trans_ref, f32[128,512]{1,0:T(8,128)} %get-tuple-element.57.emit_ref), custom_call_target="tpu_custom_call" | custom-call | flops 1073741824 | bytes 10485760 | tf_op jit(solution)/shard_map/pallas_call | solution.py:69
  254.4 0.0 all-gather.19.cloned.1.call-update
  254.4 0.2 all-gather.21.cloned.1.call-start
  254.6 8.8 %fusion.18 = (f32[128,1,512]{2,1,0:T(1,128)}, f32[128,1,512]{2,1,0:T(1,128)}, f32[128,1,512]{2,1,0:T(1,128)S(1)}, f32[128,1,512]{2,1,0:T(1,128)S(1)}, f32[128,1,...) fusion(f32[128,8,512]{2,1,0:T(8,128)} %param.4), kind=kLoop, calls=%fused_computation.46 | loop fusion | bytes 3670016 | tf_op jit(solution)/shard_map/slice | solution.py:133
  263.4 0.1 copy.33
  263.5 0.0 copy-start.5
  263.5 7.5 %dynamic_update_slice.21 = bf16[896,8192]{1,0:T(8,128)(2,1)} pad(bf16[128,8192]{1,0:T(8,128)(2,1)S(1)} %copy-done, bf16[]{:T(256)} %constant.1.clone.1), padding=768_0x0_0 | pad | bytes 16777218 | tf_op jit(solution)/shard_map/dynamic_update_slice | solution.py:134
  271.0 0.1 fusion.5
  271.1 0.1 copy.32
  271.2 1.2 fusion.7
  272.4 3.2 constant_dynamic-update-slice_fusion.5
  275.5 0.1 copy.31
  275.6 0.1 fusion.9
  275.7 18.9 %all-gather.19.cloned.1.call-done.whole_ref = bf16[128,8192]{1,0:T(8,128)(2,1)} async-done(((bf16[128,512]{1,0:T(8,128)(2,1)}), bf16[128,8192]{1,0:T(8,128)(2,1)}) %all-gather.19.cloned.1.call-update) | async-done | bytes 2097168 | tf_op jit(solution)/shard_map/all_gather | solution.py:131
  294.7 5.9 %shard_map.66 = (f32[128,512]{1,0:T(8,128)}, bf16[128,512]{1,0:T(8,128)(2,1)}, f32[128,1]{1,0:T(8,128)}) custom-call(bf16[128,8192]{1,0:T(8,128)(2,1)} %all-gather.19.cloned.1.call-done.whole_ref, bf16[8192,512]{1,0:T(8,128)(2,1)} %shard_map.59.trans_ref, f32[128,512]{1,0:T(8,128)} %get-tuple-element.56.emit_ref), custom_call_target="tpu_custom_call" | custom-call | flops 1073741824 | bytes 10485760 | tf_op jit(solution)/shard_map/pallas_call | solution.py:69
  300.6 0.0 all-gather.21.cloned.1.call-update
  300.6 1.5 constant_dynamic-update-slice_fusion.4
  302.2 0.1 copy.30
  302.2 0.1 fusion.11
  302.4 3.3 constant_dynamic-update-slice_fusion.3
  305.7 0.1 copy.29
  305.8 0.1 fusion.13
  305.9 1.5 constant_dynamic-update-slice_fusion.2
  307.5 0.1 copy.28
  307.5 0.1 fusion.15
  307.7 3.1 constant_dynamic-update-slice_fusion.1
  310.8 30.1 %all-gather.21.cloned.1.call-done.whole_ref = bf16[128,8192]{1,0:T(8,128)(2,1)} async-done(((bf16[128,512]{1,0:T(8,128)(2,1)}), bf16[128,8192]{1,0:T(8,128)(2,1)}) %all-gather.21.cloned.1.call-update) | async-done | bytes 2097168 | tf_op jit(solution)/shard_map/all_gather | solution.py:131
  340.9 5.7 %shard_map.67 = (f32[128,512]{1,0:T(8,128)}, bf16[128,512]{1,0:T(8,128)(2,1)}, f32[128,1]{1,0:T(8,128)}) custom-call(bf16[128,8192]{1,0:T(8,128)(2,1)} %all-gather.21.cloned.1.call-done.whole_ref, bf16[8192,512]{1,0:T(8,128)(2,1)} %shard_map.59.trans_ref, f32[128,512]{1,0:T(8,128)} %get-tuple-element.55.emit_ref), custom_call_target="tpu_custom_call" | custom-call | flops 1073741824 | bytes 10485760 | tf_op jit(solution)/shard_map/pallas_call | solution.py:69
  346.6 1.0 bitcast_dynamic-update-slice_fusion.6
  347.7 1.1 fusion.17
  348.8 19.7 %all-gather = f32[2048,7]{0,1:T(8,128)S(1)} all-gather(f32[128,7]{0,1:T(8,128)S(1)} %concatenate.11), channel_id=2, replica_groups=mesh['groups'=2,'state'=16] {'state'}, dimensions={0}, use_global_device_ids=true | all-gather | bytes 60928 | tf_op jit(solution)/shard_map/all_gather | solution.py:142
  368.5 0.9 copy.27
  369.4 1.0 bitcast_dynamic-update-slice_fusion.5
  370.4 1.0 bitcast_dynamic-update-slice_fusion.4
  371.5 2.5 copy.41
  374.1 2.8 fusion.2
  376.9 1.5 constant_dynamic-update-slice_fusion
  378.4 19.3 %multiply_multiply_fusion = f32[512,8192]{1,0:T(8,128)} fusion(bf16[512,8192]{1,0:T(8,128)(2,1)} %x_ref.1, bf16[896,512]{1,0:T(8,128)(2,1)S(1)} %bitcast.85, bf16[896,8192]{1,0:T(8,128)(2,1)} %constant_dynamic-update-slice_fusion), kind=kOutput, calls=%fused_computation | convolution fusion | flops 7528775680 | bytes 40763392 | tf_op jit(solution)/shard_map/dot_general | solution.py:147
  (50 shorter events, 0.3 us)
Async XLA Ops:
  7.2 56.8 %all-gather.9.cloned.1.call-start = ((), (), s32[]{:S(2)}) async-start(), calls=%async_computation | async-start | bytes 2228224 | tf_op jit(solution)/shard_map/all_gather | solution.py:131
  20.0 13.1 %copy-start.19 = (s32[128,8]{0,1:T(8,128)S(1)}, s32[128,8]{0,1:T(8,128)}, u32[]{:S(2)}) copy-start(s32[128,8]{0,1:T(8,128)} %param.5) | copy-start | bytes 12292
  20.0 90.5 %all-gather.11.cloned.1.call-start = ((), (), s32[]{:S(2)}) async-start(), calls=%async_computation.1 | async-start | bytes 2228224 | tf_op jit(solution)/shard_map/all_gather | solution.py:131
  69.8 86.8 %all-gather.13.cloned.1.call-start = ((), (), s32[]{:S(2)}) async-start(), calls=%async_computation.2 | async-start | bytes 2228224 | tf_op jit(solution)/shard_map/all_gather | solution.py:131
  116.2 86.3 %all-gather.15.cloned.1.call-start = ((), (), s32[]{:S(2)}) async-start(), calls=%async_computation.3 | async-start | bytes 2228224 | tf_op jit(solution)/shard_map/all_gather | solution.py:131
  162.3 86.3 %all-gather.17.cloned.1.call-start = ((), (), s32[]{:S(2)}) async-start(), calls=%async_computation.4 | async-start | bytes 2228224 | tf_op jit(solution)/shard_map/all_gather | solution.py:131
  208.3 86.3 %all-gather.19.cloned.1.call-start = ((), (), s32[]{:S(2)}) async-start(), calls=%async_computation.5 | async-start | bytes 2228224 | tf_op jit(solution)/shard_map/all_gather | solution.py:131
  254.3 9.1 %copy-start.13 = (f32[128,1]{1,0:T(8,128)S(1)}, f32[128,1]{1,0:T(8,128)}, u32[]{:S(2)}) copy-start(f32[128,1]{1,0:T(8,128)} %get-tuple-element.41) | copy-start | bytes 1540
  254.3 9.1 %copy-start = (bf16[128,8192]{1,0:T(8,128)(2,1)S(1)}, bf16[128,8192]{1,0:T(8,128)(2,1)}, u32[]{:S(2)}) copy-start(bf16[128,8192]{1,0:T(8,128)(2,1)} %all-gather.9.cloned.1.call-done.whole_ref) | copy-start | bytes 6291460
  254.4 86.5 %all-gather.21.cloned.1.call-start = ((), (), s32[]{:S(2)}) async-start(), calls=%async_computation.6 | async-start | bytes 2228224 | tf_op jit(solution)/shard_map/all_gather | solution.py:131
  263.5 7.5 %copy-start.4 = (f32[128,1,512]{2,1,0:T(1,128)S(1)}, f32[128,1,512]{2,1,0:T(1,128)}, u32[]{:S(2)}) copy-start(f32[128,1,512]{2,1,0:T(1,128)} %get-tuple-element.48) | copy-start | bytes 786436
  263.5 7.5 %copy-start.5 = (f32[128,512]{1,0:T(8,128)S(1)}, f32[128,512]{1,0:T(8,128)}, u32[]{:S(2)}) copy-start(f32[128,512]{1,0:T(8,128)} %get-tuple-element.34) | copy-start | bytes 786436
  263.5 7.6 %copy-start.14 = (f32[128,1]{1,0:T(8,128)S(1)}, f32[128,1]{1,0:T(8,128)}, u32[]{:S(2)}) copy-start(f32[128,1]{1,0:T(8,128)} %get-tuple-element.40) | copy-start | bytes 1540
  272.4 3.2 copy-start.16
  272.4 3.2 copy-start.8
  294.7 5.9 %copy-start.1 = (bf16[128,8192]{1,0:T(8,128)(2,1)S(1)}, bf16[128,8192]{1,0:T(8,128)(2,1)}, u32[]{:S(2)}) copy-start(bf16[128,8192]{1,0:T(8,128)(2,1)} %all-gather.13.cloned.1.call-done.whole_ref) | copy-start | bytes 6291460
  300.6 1.6 copy-start.15
  300.6 1.6 copy-start.10
  302.4 3.4 copy-start.17
  302.4 3.4 copy-start.11
  302.4 3.5 copy-start.3
  305.9 1.5 copy-start.18
  305.9 1.6 copy-start.12
  346.6 24.8 %copy-start.9 = (f32[128,512]{1,0:T(8,128)S(1)}, f32[128,512]{1,0:T(8,128)}, u32[]{:S(2)}) copy-start(f32[128,512]{1,0:T(8,128)} %get-tuple-element.32) | copy-start | bytes 786436
  346.6 24.8 %copy-start.7 = (f32[128,512]{1,0:T(8,128)S(1)}, f32[128,512]{1,0:T(8,128)}, u32[]{:S(2)}) copy-start(f32[128,512]{1,0:T(8,128)} %get-tuple-element.33) | copy-start | bytes 786436
  346.6 24.9 %copy-start.6 = (f32[128,512]{1,0:T(8,128)S(1)}, f32[128,512]{1,0:T(8,128)}, u32[]{:S(2)}) copy-start(f32[128,512]{1,0:T(8,128)} %get-tuple-element.34) | copy-start | bytes 786436
  374.1 2.8 copy-start.2
Sparse Core Ops, SparseCore 0:
  20.1 43.8 all-gather.8
  69.9 40.5 all-gather.10
  116.4 40.1 all-gather.12
  162.4 40.1 all-gather.14
  208.4 40.1 all-gather.16
  254.5 40.1 all-gather.18
  300.7 40.1 all-gather.20

commit v14 on v10

--- a/solution.py
+++ b/solution.py
@@ -112,8 +112,8 @@
 
 def emitted_rows_xla(ids, emission):
     vocab = emission.shape[1]
-    onehot = (ids[:, None] == lax.broadcasted_iota(jnp.int32, (1, vocab), 1)).astype(emission.dtype)
-    return lax.dot_general(onehot, emission, NT, preferred_element_type=jnp.float32)
+    onehot_t = (lax.broadcasted_iota(jnp.int32, (vocab, 1), 0) == ids[None, :]).astype(emission.dtype)
+    return jnp.dot(emission, onehot_t, preferred_element_type=jnp.float32).T
 
 
 def on_device(forward_probs, token_ids, transition, emission):

time: 406 us -> 406 us (level)
  no operation moved by 1% of the time
where the time goes in v14:
time: 406 us; the launch traced here: 405 us
  waiting for transfers between devices  221 us (54%)
  Pallas kernels  76.8 us (19%)
  local copies, waits for them, and re-layouts  37.9 us (9%)
  matrix products  31.5 us (8%)
  blocking collectives  19.5 us (5%)
  between operations  14.4 us (4%)
    all_gather x7, waiting for transfers between devices, on_device(): whole = lax.all_gather(weighted, 'state', axis=1, tiled=True)  221 us
    pallas_call x7, Pallas kernels, backward_step(): pl.pallas_call(_step_kernel, grid=(states // tk,), in_specs=[pl.BlockSpec...  41.9 us
    pallas_call x1, Pallas kernels, emitted_rows(): pl.pallas_call(_emit_kernel, grid=(vocab // tv,), in_specs=[pl.BlockSpec(...  21.8 us
    dynamic_update_slice x7, local copies, waits for them, and re-layouts, on_device(): vector_mat = lax.dynamic_update_slice(vector_mat, whole, (t * seq_count, 0))  20.1 us
    all_gather x1, blocking collectives, on_device(): norm_parts = lax.all_gather(partial_norms, 'state', axis=0, tiled=False)  19.5 us
    dot_general x1, matrix products, on_device(): lax.dot_general(share_mat, vector_mat, (((0,), (0,)), ((), ())), preferre...  19.3 us
    pallas_call x1, Pallas kernels, transposed(): pl.pallas_call(_transpose_kernel, grid=(cols // tile,), in_specs=[pl.Bloc...  13 us
    dot_general x1, matrix products, emitted_rows_xla(): return jnp.dot(emission, onehot_t, preferred_element_type=jnp.float32).T  12.3 us
  transfers between devices with their start and end apart: 7, of which 7 were waited for; matrix products, arithmetic and copies ran while one was open for 7% of the time, Pallas kernels for 9%

profile of v14, /device:TPU:0, one launch (start us, length us, event | category | flops | bytes accessed | tf_op | source)
XLA Modules:
  0.0 404.9 jit_solution(4853197347845204656)
XLA Ops:
  7.2 0.0 all-gather.9.cloned.1.call-start
  7.2 0.7 slice_bitcast_fusion.1
  7.9 12.3 %fusion.5 = bf16[128,512]{1,0:T(8,128)(2,1)} fusion(bf16[512,16384]{1,0:T(8,128)(2,1)} %em_ref.1, s32[128]{0:T(128)S(1)} %slice_bitcast_fusion.1), kind=kOutput, calls=%fused_computation.7 | convolution fusion | flops 2151743488 | bytes 16908800 | tf_op jit(solution)/shard_map/dot_general | solution.py:116
  20.2 0.0 all-gather.9.cloned.1.call-update
  20.2 0.0 all-gather.11.cloned.1.call-start
  20.3 1.0 copy.58
  21.3 1.9 fusion.8
  23.2 0.7 copy.78
  23.9 13.0 %shard_map.59.trans_ref = bf16[8192,512]{1,0:T(8,128)(2,1)} custom-call(bf16[512,8192]{1,0:T(8,128)(2,1)} %x_ref.1), custom_call_target="tpu_custom_call" | custom-call | tf_op jit(solution)/shard_map/pallas_call | solution.py:104
  36.9 21.8 %shard_map.60 = f32[896,512]{1,0:T(8,128)} custom-call(s32[896,1]{1,0:T(8,128)} %bitcast.66, bf16[512,16384]{1,0:T(8,128)(2,1)} %em_ref.1), custom_call_target="tpu_custom_call" | custom-call | flops 15032385536 | bytes 18612224 | tf_op jit(solution)/shard_map/pallas_call | solution.py:29
  58.8 2.7 fusion.9
  61.5 2.7 all-gather.9.cloned.1.call-done.whole_ref
  64.2 5.9 %shard_map.61 = (f32[128,512]{1,0:T(8,128)}, bf16[128,512]{1,0:T(8,128)(2,1)}, f32[128,1]{1,0:T(8,128)}, f32[128,1]{1,0:T(8,128)}) custom-call(bf16[128,8192]{1,0:T(8,128)(2,1)} %all-gather.9.cloned.1.call-done.whole_ref, bf16[8192,512]{1,0:T(8,128)(2,1)} %shard_map.59.trans_ref, f32[128,512]{1,0:T(8,128)} %get-tuple-element.75.emit_ref, f32[128,512]{1,0:T(8,128)} %bitcast.60), custom_call_target="tpu_custom_call" | custom-call | flops 1073741824 | bytes 10485760 | tf_op jit(solution)/shard_map/pallas_call | solution.py:70
  70.2 0.0 all-gather.11.cloned.1.call-update
  70.2 0.0 all-gather.13.cloned.1.call-start
  70.3 0.7 copy.77
  71.0 40.7 %all-gather.11.cloned.1.call-done.whole_ref = bf16[128,8192]{1,0:T(8,128)(2,1)} async-done(((bf16[128,512]{1,0:T(8,128)(2,1)}), bf16[128,8192]{1,0:T(8,128)(2,1)}) %all-gather.11.cloned.1.call-update) | async-done | bytes 2097168 | tf_op jit(solution)/shard_map/all_gather | solution.py:135
  111.7 6.0 %shard_map.62 = (f32[128,512]{1,0:T(8,128)}, bf16[128,512]{1,0:T(8,128)(2,1)}, f32[128,1]{1,0:T(8,128)}, f32[128,1]{1,0:T(8,128)}) custom-call(bf16[128,8192]{1,0:T(8,128)(2,1)} %all-gather.11.cloned.1.call-done.whole_ref, bf16[8192,512]{1,0:T(8,128)(2,1)} %shard_map.59.trans_ref, f32[128,512]{1,0:T(8,128)} %get-tuple-element.74.emit_ref, f32[128,512]{1,0:T(8,128)} %bitcast.62), custom_call_target="tpu_custom_call" | custom-call | flops 1073741824 | bytes 10485760 | tf_op jit(solution)/shard_map/pallas_call | solution.py:70
  117.7 0.0 all-gather.13.cloned.1.call-update
  117.7 0.0 all-gather.15.cloned.1.call-start
  117.8 0.7 copy.76
  118.5 39.5 %all-gather.13.cloned.1.call-done.whole_ref = bf16[128,8192]{1,0:T(8,128)(2,1)} async-done(((bf16[128,512]{1,0:T(8,128)(2,1)}), bf16[128,8192]{1,0:T(8,128)(2,1)}) %all-gather.13.cloned.1.call-update) | async-done | bytes 2097168 | tf_op jit(solution)/shard_map/all_gather | solution.py:135
  158.0 5.9 %shard_map.63 = (f32[128,512]{1,0:T(8,128)}, bf16[128,512]{1,0:T(8,128)(2,1)}, f32[128,1]{1,0:T(8,128)}, f32[128,1]{1,0:T(8,128)}) custom-call(bf16[128,8192]{1,0:T(8,128)(2,1)} %all-gather.13.cloned.1.call-done.whole_ref, bf16[8192,512]{1,0:T(8,128)(2,1)} %shard_map.59.trans_ref, f32[128,512]{1,0:T(8,128)} %get-tuple-element.73.emit_ref, f32[128,512]{1,0:T(8,128)} %bitcast.63), custom_call_target="tpu_custom_call" | custom-call | flops 1073741824 | bytes 10485760 | tf_op jit(solution)/shard_map/pallas_call | solution.py:70
  163.9 0.0 all-gather.17.cloned.1.call-start
  164.0 0.7 copy.75
  164.7 39.5 %all-gather.15.cloned.1.call-done.whole_ref = bf16[128,8192]{1,0:T(8,128)(2,1)} async-done(((bf16[128,512]{1,0:T(8,128)(2,1)}), bf16[128,8192]{1,0:T(8,128)(2,1)}) %all-gather.15.cloned.1.call-update) | async-done | bytes 2097168 | tf_op jit(solution)/shard_map/all_gather | solution.py:135
  204.2 5.9 %shard_map.64 = (f32[128,512]{1,0:T(8,128)}, bf16[128,512]{1,0:T(8,128)(2,1)}, f32[128,1]{1,0:T(8,128)}, f32[128,1]{1,0:T(8,128)}) custom-call(bf16[128,8192]{1,0:T(8,128)(2,1)} %all-gather.15.cloned.1.call-done.whole_ref, bf16[8192,512]{1,0:T(8,128)(2,1)} %shard_map.59.trans_ref, f32[128,512]{1,0:T(8,128)} %get-tuple-element.72.emit_ref, f32[128,512]{1,0:T(8,128)} %bitcast.64), custom_call_target="tpu_custom_call" | custom-call | flops 1073741824 | bytes 10485760 | tf_op jit(solution)/shard_map/pallas_call | solution.py:70
  210.2 0.0 all-gather.19.cloned.1.call-start
  210.2 0.7 copy.74
  210.9 39.5 %all-gather.17.cloned.1.call-done.whole_ref = bf16[128,8192]{1,0:T(8,128)(2,1)} async-done(((bf16[128,512]{1,0:T(8,128)(2,1)}), bf16[128,8192]{1,0:T(8,128)(2,1)}) %all-gather.17.cloned.1.call-update) | async-done | bytes 2097168 | tf_op jit(solution)/shard_map/all_gather | solution.py:135
  250.5 6.1 %shard_map.65 = (f32[128,512]{1,0:T(8,128)}, bf16[128,512]{1,0:T(8,128)(2,1)}, f32[128,1]{1,0:T(8,128)}, f32[128,1]{1,0:T(8,128)}) custom-call(bf16[128,8192]{1,0:T(8,128)(2,1)} %all-gather.17.cloned.1.call-done.whole_ref, bf16[8192,512]{1,0:T(8,128)(2,1)} %shard_map.59.trans_ref, f32[128,512]{1,0:T(8,128)} %get-tuple-element.71.emit_ref, f32[128,512]{1,0:T(8,128)} %bitcast.65), custom_call_target="tpu_custom_call" | custom-call | flops 1073741824 | bytes 10485760 | tf_op jit(solution)/shard_map/pallas_call | solution.py:70
  256.6 0.2 all-gather.21.cloned.1.call-start
  256.8 0.7 copy.72
  257.5 0.7 copy.73
  258.2 0.1 copy.40
  258.3 0.1 copy.47
  258.4 7.4 %dynamic_update_slice.21 = bf16[896,8192]{1,0:T(8,128)(2,1)} pad(bf16[128,8192]{1,0:T(8,128)(2,1)S(1)} %copy-done, bf16[]{:T(256)} %constant.1.clone.1), padding=768_0x0_0 | pad | bytes 16777218 | tf_op jit(solution)/shard_map/dynamic_update_slice | solution.py:139
  265.8 31.1 %all-gather.19.cloned.1.call-done.whole_ref = bf16[128,8192]{1,0:T(8,128)(2,1)} async-done(((bf16[128,512]{1,0:T(8,128)(2,1)}), bf16[128,8192]{1,0:T(8,128)(2,1)}) %all-gather.19.cloned.1.call-update) | async-done | bytes 2097168 | tf_op jit(solution)/shard_map/all_gather | solution.py:135
  296.9 6.1 %shard_map.66 = (f32[128,512]{1,0:T(8,128)}, bf16[128,512]{1,0:T(8,128)(2,1)}, f32[128,1]{1,0:T(8,128)}, f32[128,1]{1,0:T(8,128)}) custom-call(bf16[128,8192]{1,0:T(8,128)(2,1)} %all-gather.19.cloned.1.call-done.whole_ref, bf16[8192,512]{1,0:T(8,128)(2,1)} %shard_map.59.trans_ref, f32[128,512]{1,0:T(8,128)} %get-tuple-element.70.emit_ref, f32[128,512]{1,0:T(8,128)} %bitcast.61), custom_call_target="tpu_custom_call" | custom-call | flops 1073741824 | bytes 10485760 | tf_op jit(solution)/shard_map/pallas_call | solution.py:70
  303.0 1.6 constant_dynamic-update-slice_fusion.5
  304.6 0.1 copy.39
  304.6 0.1 copy.46
  304.7 0.1 copy.38
  304.8 0.1 copy.45
  304.9 3.3 constant_dynamic-update-slice_fusion.4
  308.2 0.1 copy.37
  308.2 0.1 copy.44
  308.3 1.5 constant_dynamic-update-slice_fusion.3
  309.9 0.1 copy.36
  309.9 0.1 copy.43
  310.0 3.3 constant_dynamic-update-slice_fusion.2
  313.3 0.1 copy.35
  313.4 0.1 copy.42
  313.5 1.5 constant_dynamic-update-slice_fusion.1
  315.0 28.2 %all-gather.21.cloned.1.call-done.whole_ref = bf16[128,8192]{1,0:T(8,128)(2,1)} async-done(((bf16[128,512]{1,0:T(8,128)(2,1)}), bf16[128,8192]{1,0:T(8,128)(2,1)}) %all-gather.21.cloned.1.call-update) | async-done | bytes 2097168 | tf_op jit(solution)/shard_map/all_gather | solution.py:135
  343.2 6.0 %shard_map.67 = (f32[128,512]{1,0:T(8,128)}, bf16[128,512]{1,0:T(8,128)(2,1)}, f32[128,1]{1,0:T(8,128)}, f32[128,1]{1,0:T(8,128)}) custom-call(bf16[128,8192]{1,0:T(8,128)(2,1)} %all-gather.21.cloned.1.call-done.whole_ref, bf16[8192,512]{1,0:T(8,128)(2,1)} %shard_map.59.trans_ref, f32[128,512]{1,0:T(8,128)} %get-tuple-element.69.emit_ref, f32[128,512]{1,0:T(8,128)} %bitcast.59), custom_call_target="tpu_custom_call" | custom-call | flops 1073741824 | bytes 10485760 | tf_op jit(solution)/shard_map/pallas_call | solution.py:70
  349.3 1.0 copy.34
  350.2 0.9 copy.41
  351.2 19.5 %all-gather = f32[2048,7]{0,1:T(8,128)S(1)} all-gather(f32[128,7]{0,1:T(8,128)S(1)} %concatenate.11), channel_id=2, replica_groups=mesh['groups'=2,'state'=16] {'state'}, dimensions={0}, use_global_device_ids=true | all-gather | bytes 60928 | tf_op jit(solution)/shard_map/all_gather | solution.py:147
  370.7 1.0 bitcast_dynamic-update-slice_fusion.6
  372.0 2.5 copy.48
  374.5 2.8 fusion.4
  377.3 1.5 constant_dynamic-update-slice_fusion
  378.8 19.3 %multiply_multiply_fusion = f32[512,8192]{1,0:T(8,128)} fusion(bf16[512,8192]{1,0:T(8,128)(2,1)} %x_ref.1, bf16[896,512]{1,0:T(8,128)(2,1)S(1)} %bitcast.57, bf16[896,8192]{1,0:T(8,128)(2,1)} %constant_dynamic-update-slice_fusion), kind=kOutput, calls=%fused_computation | convolution fusion | flops 7528775680 | bytes 40763392 | tf_op jit(solution)/shard_map/dot_general | solution.py:152
  (69 shorter events, 0.4 us)
Async XLA Ops:
  7.2 57.1 %all-gather.9.cloned.1.call-start = ((), (), s32[]{:S(2)}) async-start(), calls=%async_computation | async-start | bytes 2228224 | tf_op jit(solution)/shard_map/all_gather | solution.py:135
  7.9 12.3 %copy-start.25 = (s32[128,8]{0,1:T(8,128)S(1)}, s32[128,8]{0,1:T(8,128)}, u32[]{:S(2)}) copy-start(s32[128,8]{0,1:T(8,128)} %param.5) | copy-start | bytes 12292
  7.9 13.4 %copy-start.5 = (f32[128,8,512]{2,1,0:T(8,128)S(1)}, f32[128,8,512]{2,1,0:T(8,128)}, u32[]{:S(2)}) copy-start(f32[128,8,512]{2,1,0:T(8,128)} %param.4) | copy-start | bytes 6291460
  20.2 91.5 %all-gather.11.cloned.1.call-start = ((), (), s32[]{:S(2)}) async-start(), calls=%async_computation.1 | async-start | bytes 2228224 | tf_op jit(solution)/shard_map/all_gather | solution.py:135
  64.2 6.0 %copy-start.6 = (f32[128,1,512]{2,1,0:T(1,128)S(1)}, f32[128,1,512]{2,1,0:T(1,128)}, u32[]{:S(2)}) copy-start(f32[128,1,512]{2,1,0:T(1,128)} %get-tuple-element.67) | copy-start | bytes 786436
  70.2 87.8 %all-gather.13.cloned.1.call-start = ((), (), s32[]{:S(2)}) async-start(), calls=%async_computation.2 | async-start | bytes 2228224 | tf_op jit(solution)/shard_map/all_gather | solution.py:135
  117.7 86.5 %all-gather.15.cloned.1.call-start = ((), (), s32[]{:S(2)}) async-start(), calls=%async_computation.3 | async-start | bytes 2228224 | tf_op jit(solution)/shard_map/all_gather | solution.py:135
  163.9 86.5 %all-gather.17.cloned.1.call-start = ((), (), s32[]{:S(2)}) async-start(), calls=%async_computation.4 | async-start | bytes 2228224 | tf_op jit(solution)/shard_map/all_gather | solution.py:135
  210.2 86.7 %all-gather.19.cloned.1.call-start = ((), (), s32[]{:S(2)}) async-start(), calls=%async_computation.5 | async-start | bytes 2228224 | tf_op jit(solution)/shard_map/all_gather | solution.py:135
  250.4 7.8 %copy-start.16 = (f32[128,1]{1,0:T(8,128)S(1)}, f32[128,1]{1,0:T(8,128)}, u32[]{:S(2)}) copy-start(f32[128,1]{1,0:T(8,128)} %get-tuple-element.48) | copy-start | bytes 1540
  250.5 7.9 %copy-start.15 = (f32[128,1]{1,0:T(8,128)S(1)}, f32[128,1]{1,0:T(8,128)}, u32[]{:S(2)}) copy-start(f32[128,1]{1,0:T(8,128)} %get-tuple-element.55) | copy-start | bytes 1540
  250.5 7.9 %copy-start = (bf16[128,8192]{1,0:T(8,128)(2,1)S(1)}, bf16[128,8192]{1,0:T(8,128)(2,1)}, u32[]{:S(2)}) copy-start(bf16[128,8192]{1,0:T(8,128)(2,1)} %all-gather.9.cloned.1.call-done.whole_ref) | copy-start | bytes 6291460
  256.6 86.7 %all-gather.21.cloned.1.call-start = ((), (), s32[]{:S(2)}) async-start(), calls=%async_computation.6 | async-start | bytes 2228224 | tf_op jit(solution)/shard_map/all_gather | solution.py:135
  296.9 6.1 %copy-start.1 = (bf16[128,8192]{1,0:T(8,128)(2,1)S(1)}, bf16[128,8192]{1,0:T(8,128)(2,1)}, u32[]{:S(2)}) copy-start(bf16[128,8192]{1,0:T(8,128)(2,1)} %all-gather.11.cloned.1.call-done.whole_ref) | copy-start | bytes 6291460
  303.0 1.6 copy-start.14
  303.0 1.7 copy-start.13
  303.0 1.7 copy-start.18
  303.0 1.8 copy-start.17
  304.9 3.3 copy-start.20
  304.9 3.3 copy-start.19
  304.9 3.4 copy-start.3
  308.3 1.6 copy-start.22
  308.3 1.6 copy-start.21
  310.0 3.3 copy-start.24
  310.0 3.4 copy-start.23
  310.0 3.5 copy-start.4
  343.2 28.5 %copy-start.12 = (f32[128,512]{1,0:T(8,128)S(1)}, f32[128,512]{1,0:T(8,128)}, u32[]{:S(2)}) copy-start(f32[128,512]{1,0:T(8,128)} %get-tuple-element.36) | copy-start | bytes 786436
  343.2 28.5 %copy-start.11 = (f32[128,512]{1,0:T(8,128)S(1)}, f32[128,512]{1,0:T(8,128)}, u32[]{:S(2)}) copy-start(f32[128,512]{1,0:T(8,128)} %get-tuple-element.37) | copy-start | bytes 786436
  343.2 28.6 %copy-start.10 = (f32[128,512]{1,0:T(8,128)S(1)}, f32[128,512]{1,0:T(8,128)}, u32[]{:S(2)}) copy-start(f32[128,512]{1,0:T(8,128)} %get-tuple-element.38) | copy-start | bytes 786436
  349.3 22.6 %copy-start.9 = (f32[128,512]{1,0:T(8,128)S(1)}, f32[128,512]{1,0:T(8,128)}, u32[]{:S(2)}) copy-start(f32[128,512]{1,0:T(8,128)} %get-tuple-element.39) | copy-start | bytes 786436
  349.3 22.6 %copy-start.8 = (f32[128,512]{1,0:T(8,128)S(1)}, f32[128,512]{1,0:T(8,128)}, u32[]{:S(2)}) copy-start(f32[128,512]{1,0:T(8,128)} %get-tuple-element.40) | copy-start | bytes 786436
  349.3 22.6 %copy-start.7 = (f32[128,512]{1,0:T(8,128)S(1)}, f32[128,512]{1,0:T(8,128)}, u32[]{:S(2)}) copy-start(f32[128,512]{1,0:T(8,128)} %get-tuple-element.41) | copy-start | bytes 786436
  374.5 2.8 copy-start.2
Sparse Core Ops, SparseCore 0:
  20.3 43.8 all-gather.8
  70.3 41.3 all-gather.10
  117.8 40.1 all-gather.12
  164.1 40.0 all-gather.14
  210.3 40.1 all-gather.16
  256.7 40.1 all-gather.18
  303.1 40.1 all-gather.20
